TPU v7x, 32 devices: a whole 2x2x4 slice. The times are simulated.
32 devices in a mesh: section: 2 (over core), dp: 4 (over z), mp: 4 (over y, x).
Axes of the slice: x: 2, y: 2, z: 4, core: 2. Of those that a mesh axis runs over, the one named last changes fastest.
Arguments:
- tokens: bfloat16 [1024, 2048], P('dp', 'mp'), may hold values from -40 to 40
- norm_gain: float32 [2, 2048], P('section'), may hold values from 0.25 to 1.75
- in_proj: bfloat16 [2, 2048, 4672], P('section', None, 'mp'), may hold values from -0.125 to 0.125
- conv_weight: float32 [2, 4, 2560], P('section', None, 'mp'), may hold values from -3 to 3
- conv_bias: float32 [2, 2560], P('section', 'mp'), may hold values from -3 to 3
- step_bias: float32 [2, 64], P('section', 'mp'), may hold values from -6 to -2
- decay_rate: float32 [2, 64], P('section', 'mp'), may hold values from 1 to 16
- skip_gain: float32 [2, 64], P('section', 'mp'), may hold values from 0.5 to 1.5
- gate_gain: float32 [2, 2048], P('section', 'mp'), may hold values from 0.25 to 1.75
- out_proj: bfloat16 [2, 2048, 2048], P('section', 'mp'), may hold values from -0.1875 to 0.1875
- kept_state: bfloat16 [2, 64, 64, 2048], P('section', 'dp', 'mp'), may hold values from -2 to 2
- kept_conv: bfloat16 [2, 64, 3, 2560], P('section', 'dp', None, 'mp'), may hold values from -6 to 6
- doc_owner: int32 [64], replicated, may hold values from 0 to 3, as said below
- doc_slot: int32 [64], replicated, may hold values from 0 to 15, as said below
- window_start: int32 [64], P('dp'), may hold values from 0 to 1136, as said below
Outputs:
- layer_out: bfloat16 [2, 1024, 2048], P('section', 'dp', 'mp')
- new_state: bfloat16 [2, 64, 64, 2048], P('section', 'dp', 'mp')
- new_conv: bfloat16 [2, 64, 3, 2560], P('section', 'dp', None, 'mp')
Inputs may be any that keep to these rules, and one draw needn't show every extreme that they name: `doc_owner`: receiver q's documents are q * 16 to q * 16 + 15; each owner serves a receiver none or exactly 4 of its documents, and each owner keeps exactly 16 documents' states. `doc_slot`: the documents of one owner have distinct slots. `window_start`: A multiple of 16; 0 marks a book's first window.
All inputs are finite; a program needn't handle non-finite values.
Results may differ from a plain program's by a relative error of at most 0.012.
Values may be sent and summed in bfloat16 or wider, within the bound.
No kernel may reach another device: no remote copies, remote signals or barrier semaphores. Data moves between devices by JAX's collectives and lax.ppermute only.
A program may use at most 64 MiB of HBM per device.

v0:
```python
import jax
import jax.numpy as jnp
from jax import lax
from jax.sharding import PartitionSpec as P

epsilon = 1e-05
highest = lax.Precision.HIGHEST
three_pass = lax.Precision.HIGH


def from_behind(value, axis, steps):
    count = lax.axis_size(axis)
    first, last = (max(0, -steps), min(count, count - steps))
    return lax.ppermute(value, axis, [(source, source + steps) for source in range(first, last)])


def row_norm(values, norm_scale):
    inv_rms = lax.rsqrt(jnp.mean(values * values, axis=-1, keepdims=True) + epsilon)
    return values * inv_rms * norm_scale


def mix_channels(
    projected,
    conv_prev,
    state_prev,
    conv_kernel,
    conv_shift,
    step_shift,
    decay_speed,
    skip_weight,
    norm_scale,
    out_weight,
):
    doc_count = projected.shape[0]
    length = projected.shape[1]
    inner = norm_scale.shape[0]
    head_count = decay_speed.shape[0]
    head_dim = inner // head_count
    state_width = (projected.shape[2] - 2 * inner - head_count) // 2
    kernel_len = conv_kernel.shape[0]
    gate_cols = projected[:, :, :inner]
    mixed_in = projected[:, :, inner : 2 * inner + 2 * state_width]
    step_raw = projected[:, :, 2 * inner + 2 * state_width :]
    padded = jnp.concatenate([conv_prev, mixed_in], axis=1)
    conv_out = jnp.zeros_like(mixed_in) + conv_shift
    for offset in range(kernel_len):
        conv_out = conv_out + conv_kernel[offset] * padded[:, offset : offset + length]
    activated = jax.nn.silu(conv_out)
    chan_vals = activated[:, :, :inner]
    expander = (
        jnp.arange(inner)[None, :] // head_dim == jnp.arange(head_count)[:, None]
    ).astype(jnp.float32)

    def expand(per_head):
        return jnp.einsum("...h,hm->...m", per_head, expander, precision=highest)

    key_proj = activated[:, :, inner : inner + state_width]
    query_proj = activated[:, :, inner + state_width :]
    step_size = jax.nn.softplus(step_raw + step_shift)
    cum_decay = jnp.cumsum(-step_size * decay_speed, axis=1)
    pair_decay = cum_decay[:, :, None, :] - cum_decay[:, None, :, :]
    positions = jnp.arange(length)
    causal = positions[:, None] >= positions[None, :]
    decay = jnp.exp(jnp.where(causal[None, :, :, None], pair_decay, -1e30))
    scores = jnp.einsum("dtn,dsn->dts", query_proj, key_proj, precision=three_pass)
    weights = decay * scores[:, :, :, None] * step_size[:, None, :, :]
    spread = chan_vals[:, :, None, :] * expander[None, None, :, :]
    mixed_out = jnp.einsum("dtsh,dshm->dtm", weights, spread, precision=three_pass)
    start_state = state_prev.reshape(doc_count, inner, state_width).astype(jnp.float32)
    carried = jnp.einsum("dtn,dmn->dtm", query_proj, start_state, precision=three_pass)
    mixed_out = mixed_out + expand(jnp.exp(cum_decay)) * carried
    mixed_out = mixed_out + jnp.repeat(skip_weight, head_dim)[None, None, :] * chan_vals
    tail_weight = jnp.exp(cum_decay[:, -1:, :] - cum_decay) * step_size
    scaled_vals = expand(tail_weight) * chan_vals
    end_state = expand(jnp.exp(cum_decay[:, -1, :]))[:, :, None] * start_state
    end_state = end_state + jnp.einsum("dsm,dsn->dmn", scaled_vals, key_proj, precision=three_pass)
    new_conv = mixed_in[:, length - (kernel_len - 1) :].astype(jnp.bfloat16)
    gated = mixed_out * jax.nn.silu(gate_cols)
    gnormed = row_norm(gated, norm_scale).astype(jnp.bfloat16)
    partial_value = jnp.dot(
        gnormed.reshape(doc_count * length, inner), out_weight, preferred_element_type=jnp.float32
    )
    end_rounded = end_state.reshape(doc_count, head_count, head_dim * state_width).astype(
        jnp.bfloat16
    )
    return (partial_value, end_rounded, new_conv)


def shifted(value, axis, steps):
    count = lax.axis_size(axis)
    return lax.ppermute(value, axis, [(source, (source + steps) % count) for source in range(count)])


def gather_columns(value):
    count = lax.axis_size("mp")
    parts = [value] + [shifted(value, "mp", steps) for steps in range(1, count)]
    return jnp.concatenate(parts[::-1], axis=1)


def rotate_rows(value, block):
    count = lax.axis_size("mp")
    position = lax.axis_index("mp")
    doubled = jnp.concatenate([value, value], axis=0)
    return lax.dynamic_slice_in_dim(doubled, ((position + 1) % count) * block, count * block, 0)


def gather_from_behind(value):
    count = lax.axis_size("mp")
    sections = lax.axis_size("section")
    width = value.shape[1]
    position = lax.axis_index("mp")
    parts = []
    for steps in range(count):
        pairs = [
            (section * count + source, (section + 1) * count + (source + steps) % count)
            for section in range(sections - 1)
            for source in range(count)
        ]
        parts.append(lax.ppermute(value, ("section", "mp"), pairs))
    whole = jnp.concatenate(parts[::-1], axis=1)
    return whole, parts[0]


def scatter_sum(partial_value, base):
    count = lax.axis_size("mp")
    position = lax.axis_index("mp")
    rows = partial_value.shape[0]
    blocks = partial_value.astype(jnp.bfloat16).reshape(rows, count, -1)
    total = base + lax.dynamic_index_in_dim(blocks, position, 1, False).astype(jnp.float32)
    for steps in range(1, count):
        block = lax.dynamic_index_in_dim(blocks, (position + steps) % count, 1, False)
        total = total + shifted(block, "mp", steps).astype(jnp.float32)
    return total


def per_device(
    tokens,
    norm_gain,
    in_proj,
    conv_weight,
    conv_bias,
    step_bias,
    decay_rate,
    skip_gain,
    gate_gain,
    out_proj,
    kept_state,
    kept_conv,
    doc_owner,
    doc_slot,
    window_start,
):
    dp_count = lax.axis_size("dp")
    section_count = lax.axis_size("section")
    dp_idx = lax.axis_index("dp")
    section_idx = lax.axis_index("section")
    doc_count = window_start.shape[0]
    length = tokens.shape[0] // doc_count
    shard_width = tokens.shape[1]
    capacity = (doc_count + dp_count - 1) // dp_count
    owners = doc_owner.reshape(dp_count, doc_count)
    slots = doc_slot.reshape(dp_count, doc_count)
    positions = jnp.arange(doc_count)
    earlier = positions[:, None] > positions[None, :]
    same_owner = owners[:, :, None] == owners[:, None, :]
    owner_rank = jnp.sum(jnp.logical_and(same_owner, earlier[None]), axis=2)
    chosen = jnp.logical_and(
        (owners == dp_idx)[:, :, None],
        owner_rank[:, :, None] == jnp.arange(capacity)[None, None, :],
    )
    send_index = jnp.sum(jnp.where(chosen, slots[:, :, None], 0), axis=1).reshape(-1)
    heads_dev = kept_state.shape[2]
    state_cols = kept_state.shape[3]
    chans = conv_weight.shape[2]
    kernel_len = conv_weight.shape[1]
    send_state = kept_state[0][send_index]
    send_conv = kept_conv[0][send_index]
    got_conv = lax.all_to_all(send_conv, "dp", split_axis=0, concat_axis=0, tiled=True)
    got_state = lax.all_to_all(send_state, "dp", split_axis=0, concat_axis=0, tiled=True)
    my_owners = lax.dynamic_index_in_dim(owners, dp_idx, 0, keepdims=False)
    my_rank = lax.dynamic_index_in_dim(owner_rank, dp_idx, 0, keepdims=False)
    recv_row = my_owners * capacity + my_rank
    keep_flag = (window_start > 0).astype(jnp.float32)
    state_start = got_state[recv_row] * keep_flag.astype(jnp.bfloat16)[:, None, None]
    conv_start = got_conv[recv_row].astype(jnp.float32) * keep_flag[:, None, None]
    gain_rotated = rotate_rows(norm_gain[0], shard_width)
    proj_rotated = rotate_rows(in_proj[0], shard_width)
    results = None
    incoming = None
    first_rows = None
    for phase in range(section_count):
        if incoming is None:
            current = tokens
            whole_rows = gather_columns(current)
            first_rows = whole_rows
        else:
            gathered, incoming = gather_from_behind(result)
            current = jnp.where(section_idx == 0, tokens, incoming)
            whole_rows = jnp.where(section_idx == 0, first_rows, gathered)
        normed = row_norm(whole_rows.astype(jnp.float32), gain_rotated).astype(jnp.bfloat16)
        projected = jnp.dot(normed, proj_rotated, preferred_element_type=jnp.float32)
        partial_value, state_new, conv_new = mix_channels(
            projected.reshape(doc_count, length, -1),
            conv_start,
            state_start,
            conv_weight[0],
            conv_bias[0],
            step_bias[0],
            decay_rate[0],
            skip_gain[0],
            gate_gain[0],
            out_proj[0],
        )
        result = scatter_sum(partial_value, current.astype(jnp.float32)).astype(jnp.bfloat16)
        results = (result, state_new, conv_new)
        incoming = result
    out_rows, new_states, new_convs = results
    return (out_rows[None], new_states[None], new_convs[None])


def solution(mesh):
    in_specs = (
        P("dp", "mp"),
        P("section", None),
        P("section", None, "mp"),
        P("section", None, "mp"),
        P("section", "mp"),
        P("section", "mp"),
        P("section", "mp"),
        P("section", "mp"),
        P("section", "mp"),
        P("section", "mp", None),
        P("section", "dp", "mp", None),
        P("section", "dp", None, "mp"),
        P(),
        P(),
        P("dp"),
    )
    out_specs = (
        P("section", "dp", "mp"),
        P("section", "dp", "mp", None),
        P("section", "dp", None, "mp"),
    )
    return jax.shard_map(
        per_device, mesh=mesh, in_specs=in_specs, out_specs=out_specs, check_vma=False
    )
```

profile of v0, /device:TPU:0, one launch (start us, length us, event | category | flops | bytes accessed | tf_op | source)
XLA Modules:
  0.0 146.1 jit_solution(15450918688632733094)
XLA Ops:
  0.7 3.0 %collective-permute-start.2 = (bf16[256,512]{1,0:T(8,128)(2,1)}, bf16[256,512]{1,0:T(8,128)(2,1)S(1)}, u32[]{:S(2)}, u32[]{:S(2)}) collective-permute-start(bf16[256,512]{1,0:T(8,128)(2,1)} %param.15), channel_id=1, source_target_pairs={{0,1},{1,2},{2,3},{3,0},{4,5},{5,6},{6,7},{7,4},{8,9},{9,10},{10,1... | collective-permute-start | bytes 786440 | tf_op jit(solution)/shard_map/ppermute | solution.py:91
  3.6 1.5 %collective-permute-start.1 = (bf16[256,512]{1,0:T(8,128)(2,1)}, bf16[256,512]{1,0:T(8,128)(2,1)S(1)}, u32[]{:S(2)}, u32[]{:S(2)}) collective-permute-start(bf16[256,512]{1,0:T(8,128)(2,1)} %param.15), channel_id=1, source_target_pairs={{0,2},{1,3},{2,0},{3,1},{4,6},{5,7},{6,4},{7,5},{8,10},{9,11},{10,... | collective-permute-start | bytes 786440 | tf_op jit(solution)/shard_map/ppermute | solution.py:91
  5.2 1.4 collective-permute-start
  7.3 0.7 broadcast_in_dim.40
  8.6 0.9 copy.135
  9.4 1.3 gather_fusion
  10.7 4.9 %all-to-all-start = ((bf16[16,3,640]{2,1,0:T(4,128)(2,1)}), bf16[16,3,640]{2,1,0:T(4,128)(2,1)S(1)}, u32[]{:S(2)}, u32[]{:S(2)}) async-start(bf16[16,3,640]{2,1,0:T(4,128)(2,1)} %gather_fusion), calls=%async_computation | async-start | bytes 163840 | tf_op jit(solution)/shard_map/all_to_all | solution.py:178
  15.6 1.2 fusion.138
  16.8 0.9 slice_reduce_fusion.3
  17.7 0.8 fusion.126
  20.0 2.8 %gather_fusion.2 = bf16[16,16,2048]{2,1,0:T(8,128)(2,1)} fusion(bf16[16,16,2048]{2,1,0:T(8,128)(2,1)} %bitcast.76, s32[1024]{0:T(1024)S(1)} %pad_clamp_fusion.1), kind=kCustom, calls=%fused_computation.2 | custom fusion | bytes 2097216 | tf_op jit(solution)/shard_map/gather | solution.py:176
  22.8 5.2 %all-to-all-start.1 = ((bf16[16,16,2048]{2,1,0:T(8,128)(2,1)}), bf16[16,16,2048]{2,1,0:T(8,128)(2,1)}, u32[]{:S(2)}, u32[]{:S(2)}) async-start(bf16[16,16,2048]{2,1,0:T(8,128)(2,1)} %gather_fusion.2), calls=%async_computation.1 | async-start | bytes 2097152 | tf_op jit(solution)/shard_map/all_to_all | solution.py:179
  28.8 1.0 constant_dynamic-update-slice_fusion.3
  30.3 4.8 %fusion.45 = f32[256,1168]{1,0:T(8,128)S(1)} fusion(bf16[256,2048]{1,0:T(8,128)(2,1)S(1)} %constant_dynamic-update-slice_fusion, f32[2048]{0:T(1024)S(1)} %fusion.126, f32[256]{0:T(256)S(1)} %add_rsqrt_fusion.3, s32[]{:T(128)S(6)} %select_n.130, bf16[2048,1168]{0,1:T(8,128)(2,1)} %bitcast.98), kind=kOutput, calls=%fused_computation.58 | convolution fusion | flops 1236402176 | bytes 7037956 | tf_op jit(solution)/shard_map/dot_general | solution.py:201
  35.2 1.0 copy-done.14
  36.3 0.8 copy.66
  37.8 1.7 %copy.63 = f32[16,16,16]{1,2,0:T(8,128)} copy(f32[16,16,16]{2,0,1:T(8,128)} %get-tuple-element.31) | data formatting | bytes 32768 | tf_op jit(solution)/shard_map/jit(cumsum)/reduce_window_sum | solution.py:60
  40.1 0.8 copy-done.7
  41.2 1.2 fusion.103
  42.3 5.8 %fusion.33 = f32[16,16,512]{2,1,0:T(8,128)} fusion(f32[16,512]{1,0:T(8,128)S(1)} %fusion.118, f32[16,16,512]{2,1,0:T(8,128)S(1)} %slice.123, f32[16,16,16]{1,2,0:T(8,128)S(1)} %copy-done.16, f32[16,16,16]{2,1,0:T(8,128)S(1)} %fusion.94, f32[16,16,16]{1,2,0:T(8,128)S(1)} %copy-done.17, pred[16,16]{1,0:T(8,128)(4,1)S(1)} %iota_compare_fusion.4), kind=kOutput, calls=%fused_computation.51 | convolution fusion | flops 203685888 | bytes 1130752 | tf_op jit(solution)/shard_map/dtsh,dshm->dtm/dot_general | solution.py:68
  48.1 4.4 %all-to-all-done.1 = bf16[16,16,2048]{2,1,0:T(8,128)(2,1)} async-done(((bf16[16,16,2048]{2,1,0:T(8,128)(2,1)}), bf16[16,16,2048]{2,1,0:T(8,128)(2,1)}, u32[]{:S(2)}, u32[]{:S(2)}) %all-to-all-start.1) | async-done | bytes 1048608 | tf_op jit(solution)/shard_map/all_to_all | solution.py:179
  52.5 2.0 %gather_fusion.3 = bf16[16,16,2048]{2,1,0:T(8,128)(2,1)S(1)} fusion(bf16[16,16,2048]{2,1,0:T(8,128)(2,1)} %all-to-all-done.1, s32[1024]{0:T(1024)} %copy-done.28), kind=kCustom, calls=%fused_computation.3 | custom fusion | bytes 2097216 | tf_op jit(solution)/shard_map/gather | solution.py:184
  54.5 3.1 %gather.18 = bf16[16,512,64]{2,1,0:T(8,128)(2,1)} reshape(bf16[16,16,2048]{2,1,0:T(8,128)(2,1)S(1)} %gather_fusion.3) | data formatting | bytes 2097152 | tf_op jit(solution)/shard_map/gather | solution.py:184
  57.6 1.9 %copy.68 = bf16[16,512,64]{1,2,0:T(8,128)(2,1)S(1)} copy(bf16[16,512,64]{2,1,0:T(8,128)(2,1)} %gather.18) | data formatting | bytes 2097152 | tf_op jit(solution)/shard_map/gather | solution.py:184
  59.6 2.5 %multiply_reduce_fusion.1 = (f32[16,16]{1,0:T(8,128)S(1)}, f32[16,16,512]{2,1,0:T(8,128)S(1)}) fusion(f32[16,16,1168]{2,1,0:T(8,128)} %bitcast.85, f32[16,16,640]{2,1,0:T(8,128)} %copy-done.7, f32[512]{0:T(512)S(1)} %copy-done.34, f32[16,16,512]{2,1,0:T(8,128)} %fusion.33, f32[16,16,512]{2,1,0:T(8,128)} %fusion.103, bf16[16,512,64]{1,2,0:T(8,128)(2,1)S(1)} %copy.68, ...), kind=kOutput, calls=%fused_computation.113 | convolution fusion | flops 52297472 | bytes 3804192 | tf_op jit(solution)/shard_map/dtn,dmn->dtm/dot_general | solution.py:70
  62.3 1.7 %convolution_convert_fusion.1 = bf16[256,2048]{1,0:T(8,128)(2,1)} fusion(bf16[256,512]{1,0:T(8,128)(2,1)S(1)} %bitcast.77, bf16[1,512,2048]{2,1,0:T(8,128)(2,1)S(1)} %copy-done), kind=kOutput, calls=%fused_computation.20 | convolution fusion | flops 537395200 | bytes 3407872 | tf_op jit(solution)/shard_map/dot_general | solution.py:80
  64.0 2.0 %reshape.264 = bf16[256,4,512]{2,1,0:T(4,128)(2,1)S(1)} reshape(bf16[256,2048]{1,0:T(8,128)(2,1)} %convolution_convert_fusion.1) | data formatting | bytes 2097152 | tf_op jit(solution)/shard_map/reshape | solution.py:128
  66.0 2.2 %constant_dynamic-slice_fusion.6 = (bf16[256,1,512]{2,1,0:T(2,128)(2,1)S(1)}, bf16[256,1,512]{2,1,0:T(2,128)(2,1)S(1)}, bf16[256,1,512]{2,1,0:T(2,128)(2,1)S(1)}, bf16[256,1,512]{2,1,0:T(2,128)(2,1)S(1)}) fusion(bf16[256,4,512]{2,1,0:T(4,128)(2,1)S(1)} %reshape.264, s32[]{:T(128)S(6)} %select_n.138, s32[]{:T(128)S(6)} %select_n.141, s32[]{:T(128)S(6)} %select_n.139, ...), kind=kLoop, calls=%fused_computation.193 | loop fusion | bytes 2097168 | tf_op jit(solution)/shard_map/jit(dynamic_index_in_dim)/dynamic_slice | solution.py:129
  68.9 1.5 %collective-permute-start.3 = (bf16[256,512]{1,0:T(8,128)(2,1)S(1)}, bf16[256,512]{1,0:T(8,128)(2,1)S(1)}, u32[]{:S(2)}, u32[]{:S(2)}) collective-permute-start(bf16[256,512]{1,0:T(8,128)(2,1)S(1)} %bitcast.88), channel_id=1, source_target_pairs={{0,1},{1,2},{2,3},{3,0},{4,5},{5,6},{6,7},{7,4},{8,9},{9,10},{10,1... | collective-permute-start | bytes 786440 | tf_op jit(solution)/shard_map/ppermute | solution.py:91
  71.0 6.7 %collective-permute-done.5 = bf16[256,512]{1,0:T(8,128)(2,1)S(1)} collective-permute-done((bf16[256,512]{1,0:T(8,128)(2,1)S(1)}, bf16[256,512]{1,0:T(8,128)(2,1)S(1)}, u32[]{:S(2)}, u32[]{:S(2)}) %collective-permute-start.5) | collective-permute-done | bytes 262176 | tf_op jit(solution)/shard_map/ppermute | solution.py:91
  77.6 3.7 %collective-permute-done.3 = bf16[256,512]{1,0:T(8,128)(2,1)S(1)} collective-permute-done((bf16[256,512]{1,0:T(8,128)(2,1)S(1)}, bf16[256,512]{1,0:T(8,128)(2,1)S(1)}, u32[]{:S(2)}, u32[]{:S(2)}) %collective-permute-start.3) | collective-permute-done | bytes 262176 | tf_op jit(solution)/shard_map/ppermute | solution.py:91
  81.3 1.4 collective-permute-done.4
  82.8 0.9 fusion.90
  83.6 2.2 %collective-permute-start.9 = (bf16[256,512]{1,0:T(8,128)(2,1)}, bf16[256,512]{1,0:T(8,128)(2,1)}, u32[]{:S(2)}, u32[]{:S(2)}) collective-permute-start(bf16[256,512]{1,0:T(8,128)(2,1)} %fusion.90), channel_id=1, source_target_pairs={{0,17},{1,18},{2,19},{3,16},{4,21},{5,22},{6,23},{7,20},{8,25},{9,... | collective-permute-start | bytes 786440 | tf_op jit(solution)/shard_map/ppermute | solution.py:119
  85.8 2.0 %collective-permute-start.8 = (bf16[256,512]{1,0:T(8,128)(2,1)}, bf16[256,512]{1,0:T(8,128)(2,1)}, u32[]{:S(2)}, u32[]{:S(2)}) collective-permute-start(bf16[256,512]{1,0:T(8,128)(2,1)} %fusion.90), channel_id=1, source_target_pairs={{0,18},{1,19},{2,16},{3,17},{4,22},{5,23},{6,20},{7,21},{8,26},{9,... | collective-permute-start | bytes 786440 | tf_op jit(solution)/shard_map/ppermute | solution.py:119
  87.8 2.0 %collective-permute-start.7 = (bf16[256,512]{1,0:T(8,128)(2,1)}, bf16[256,512]{1,0:T(8,128)(2,1)}, u32[]{:S(2)}, u32[]{:S(2)}) collective-permute-start(bf16[256,512]{1,0:T(8,128)(2,1)} %fusion.90), channel_id=1, source_target_pairs={{0,19},{1,16},{2,17},{3,18},{4,23},{5,20},{6,21},{7,22},{8,27},{9,... | collective-permute-start | bytes 786440 | tf_op jit(solution)/shard_map/ppermute | solution.py:119
  89.8 2.0 %collective-permute-start.6 = (bf16[256,512]{1,0:T(8,128)(2,1)}, bf16[256,512]{1,0:T(8,128)(2,1)}, u32[]{:S(2)}, u32[]{:S(2)}) collective-permute-start(bf16[256,512]{1,0:T(8,128)(2,1)} %fusion.90), channel_id=1, source_target_pairs={{0,16},{1,17},{2,18},{3,19},{4,20},{5,21},{6,22},{7,23},{8,24},{9,... | collective-permute-start | bytes 786440 | tf_op jit(solution)/shard_map/ppermute | solution.py:119
  91.8 1.5 %collective-permute-done.7 = bf16[256,512]{1,0:T(8,128)(2,1)} collective-permute-done((bf16[256,512]{1,0:T(8,128)(2,1)}, bf16[256,512]{1,0:T(8,128)(2,1)}, u32[]{:S(2)}, u32[]{:S(2)}) %collective-permute-start.7) | collective-permute-done | bytes 262176 | tf_op jit(solution)/shard_map/ppermute | solution.py:119
  93.3 1.6 %fusion.12 = f32[256]{0:T(256)S(1)} fusion(bf16[256,2048]{1,0:T(8,128)(2,1)S(1)} %copy-done.3, bf16[256,512]{1,0:T(8,128)(2,1)} %collective-permute-done.6, bf16[256,512]{1,0:T(8,128)(2,1)} %collective-permute-done.9, bf16[256,512]{1,0:T(8,128)(2,1)} %collective-permute-done.8, bf16[256,512]{1,0:T(8,128)(2,1)} %collective-permute-done.7, pred[]{:T(512)S(6)} %eq.103), kind=kLoop, calls=%fused_computation.24 | loop fusion | flops 6291200 | bytes 2098177 | tf_op jit(solution)/shard_map/reduce_sum | solution.py:18
  95.0 5.2 %fusion.43 = f32[256,1168]{1,0:T(8,128)S(1)} fusion(f32[256]{0:T(256)S(1)} %add_rsqrt_fusion.2, f32[2048]{0:T(1024)S(1)} %copy-done.27, bf16[256,2048]{1,0:T(8,128)(2,1)S(1)} %copy-done.3, bf16[256,512]{1,0:T(8,128)(2,1)} %collective-permute-done.6, bf16[256,512]{1,0:T(8,128)(2,1)} %collective-permute-done.9, bf16[256,512]{1,0:T(8,128)(2,1)} %collective-permute-done.8, ...), kind=kOutput, calls=%fused_computation.57 | convolution fusion | flops 1241120768 | bytes 8086533 | tf_op jit(solution)/shard_map/dot_general | solution.py:201
  100.3 0.9 copy-done.13
  101.9 0.8 fusion.116
  102.7 0.8 copy.75
  103.4 1.1 slice.126
  105.4 0.9 slice.133
  106.9 0.8 copy.77
  107.7 1.3 fusion.99
  109.0 1.2 convolution_multiply_fusion.2
  110.2 6.3 %fusion.38 = f32[16,16,512]{2,1,0:T(8,128)S(1)} fusion(f32[16,16,512]{2,1,0:T(8,128)} %slice.133, f32[16,512]{1,0:T(8,128)S(1)} %copy-done.23, f32[16,16,16]{1,2,0:T(8,128)} %copy.77, f32[16,16,16]{2,1,0:T(8,128)S(1)} %fusion.108, f32[16,16,16]{1,2,0:T(8,128)} %copy.75, pred[16,16]{1,0:T(8,128)(4,1)S(1)} %copy-done.37), kind=kOutput, calls=%fused_computation.52 | convolution fusion | flops 203685888 | bytes 1130752 | tf_op jit(solution)/shard_map/dtsh,dshm->dtm/dot_general | solution.py:68
  116.5 1.6 %multiply_reduce_fusion = (f32[16,16]{1,0:T(8,128)S(1)}, f32[16,16,512]{2,1,0:T(8,128)S(1)}) fusion(f32[16,16,1168]{2,1,0:T(8,128)} %bitcast.82, f32[16,16,640]{2,1,0:T(8,128)S(1)} %divide_multiply_fusion, f32[512]{0:T(512)S(1)} %copy-done.35, f32[16,16,512]{2,1,0:T(8,128)S(1)} %fusion.38, f32[16,16,512]{2,1,0:T(8,128)S(1)} %fusion.99, ...), kind=kOutput, calls=%fused_computation.111 | convolution fusion | flops 52297472 | bytes 3804192 | tf_op jit(solution)/shard_map/dtn,dmn->dtm/dot_general | solution.py:70
  118.2 1.7 %convolution_convert_fusion = bf16[256,2048]{1,0:T(8,128)(2,1)} fusion(bf16[256,512]{1,0:T(8,128)(2,1)S(1)} %bitcast.78, bf16[1,512,2048]{2,1,0:T(8,128)(2,1)S(1)} %copy-done), kind=kOutput, calls=%fused_computation.19 | convolution fusion | flops 537395200 | bytes 3407872 | tf_op jit(solution)/shard_map/dot_general | solution.py:80
  119.9 1.8 %reshape.267 = bf16[256,4,512]{2,1,0:T(4,128)(2,1)S(1)} reshape(bf16[256,2048]{1,0:T(8,128)(2,1)} %convolution_convert_fusion) | data formatting | bytes 2097152 | tf_op jit(solution)/shard_map/reshape | solution.py:128
  121.8 3.0 %constant_dynamic-slice_fusion.2 = (bf16[256,1,512]{2,1,0:T(2,128)(2,1)}, bf16[256,1,512]{2,1,0:T(2,128)(2,1)S(1)}, bf16[256,1,512]{2,1,0:T(2,128)(2,1)S(1)}, bf16[256,1,512]{2,1,0:T(2,128)(2,1)S(1)}) fusion(bf16[256,4,512]{2,1,0:T(4,128)(2,1)S(1)} %reshape.267, s32[]{:T(128)S(6)} %select_n.138, s32[]{:T(128)S(6)} %select_n.141, s32[]{:T(128)S(6)} %select_n.139, ...), kind=kLoop, calls=%fused_computation.189 | loop fusion | bytes 2097168 | tf_op jit(solution)/shard_map/jit(dynamic_index_in_dim)/dynamic_slice | solution.py:129
  124.8 0.8 copy.130
  125.5 0.7 copy.131
  126.3 0.7 copy.129
  127.0 0.8 collective-permute-start.12
  127.8 1.3 collective-permute-start.10
  129.6 2.1 %add_convert_fusion = bf16[16,512,64]{1,2,0:T(8,128)(2,1)S(1)} fusion(f32[16,16,512]{2,1,0:T(8,128)S(1)} %copy-done.9, f32[16,512]{1,0:T(8,128)S(1)} %copy-done.15, bf16[16,512,64]{1,2,0:T(8,128)(2,1)S(1)} %copy-done.6, bf16[16]{0:T(256)(128)(2,1)S(1)} %copy-done.39, f32[16,16,640]{2,1,0:T(8,128)} %copy-done.1), kind=kOutput, calls=%fused_computation.29 | convolution fusion | flops 52953088 | bytes 2785312 | tf_op jit(solution)/shard_map/dsm,dsn->dmn/dot_general | solution.py:76
  131.8 1.8 %copy.84 = bf16[16,512,64]{2,1,0:T(8,128)(2,1)} copy(bf16[16,512,64]{1,2,0:T(8,128)(2,1)S(1)} %add_convert_fusion) | data formatting | bytes 2097152 | tf_op jit(solution)/shard_map/convert_element_type | solution.py:83
  133.6 4.3 %convert_element_type.135 = bf16[1,16,16,2048]{3,2,1,0:T(8,128)(2,1)} reshape(bf16[16,512,64]{2,1,0:T(8,128)(2,1)} %copy.84) | data formatting | bytes 2097152 | tf_op jit(solution)/shard_map/convert_element_type | solution.py:83
  137.8 4.0 %collective-permute-done.10 = bf16[256,512]{1,0:T(8,128)(2,1)} collective-permute-done((bf16[256,512]{1,0:T(8,128)(2,1)}, bf16[256,512]{1,0:T(8,128)(2,1)}, u32[]{:S(2)}, u32[]{:S(2)}) %collective-permute-start.10) | collective-permute-done | bytes 262176 | tf_op jit(solution)/shard_map/ppermute | solution.py:91
  141.8 2.3 %collective-permute-done.11 = bf16[256,512]{1,0:T(8,128)(2,1)} collective-permute-done((bf16[256,512]{1,0:T(8,128)(2,1)}, bf16[256,512]{1,0:T(8,128)(2,1)}, u32[]{:S(2)}, u32[]{:S(2)}) %collective-permute-start.11) | collective-permute-done | bytes 262176 | tf_op jit(solution)/shard_map/ppermute | solution.py:91
  144.1 2.0 %fusion.93 = bf16[1,256,512]{2,1,0:T(8,128)(2,1)} fusion(bf16[256,512]{1,0:T(8,128)(2,1)} %collective-permute-done.12, bf16[256,512]{1,0:T(8,128)(2,1)} %collective-permute-done.11, bf16[256,512]{1,0:T(8,128)(2,1)} %collective-permute-done.10, bf16[256,1,512]{2,1,0:T(2,128)(2,1)S(1)} %copy-done.10, bf16[256,512]{1,0:T(8,128)(2,1)S(1)} %copy-done.8, ...), kind=kLoop, calls=%fused_computation.118 | loop fusion | flops 1441792 | bytes 1835009 | tf_op jit(solution)/shard_map/broadcast_in_dim | solution.py:218
  (132 shorter events, 10.0 us)
Async XLA Ops:
  0.6 61.6 %copy-start = (bf16[1,512,2048]{2,1,0:T(8,128)(2,1)S(1)}, bf16[1,512,2048]{2,1,0:T(8,128)(2,1)}, u32[]{:S(2)}) copy-start(bf16[1,512,2048]{2,1,0:T(8,128)(2,1)} %param.24) | copy-start | bytes 6291460
  0.6 22.2 %copy-start.29 = (f32[1,640]{1,0:T(1,128)S(1)}, f32[1,640]{1,0:T(1,128)}, u32[]{:S(2)}) copy-start(f32[1,640]{1,0:T(1,128)} %param.19) | copy-start | bytes 7684
  0.7 29.3 %collective-permute-start.2 = (bf16[256,512]{1,0:T(8,128)(2,1)}, bf16[256,512]{1,0:T(8,128)(2,1)S(1)}, u32[]{:S(2)}, u32[]{:S(2)}) collective-permute-start(bf16[256,512]{1,0:T(8,128)(2,1)} %param.15), channel_id=1, source_target_pairs={{0,1},{1,2},{2,3},{3,0},{4,5},{5,6},{6,7},{7,4},{8,9},{9,10},{10,1... | collective-permute-start | bytes 786440 | tf_op jit(solution)/shard_map/ppermute | solution.py:91
  3.6 26.2 %collective-permute-start.1 = (bf16[256,512]{1,0:T(8,128)(2,1)}, bf16[256,512]{1,0:T(8,128)(2,1)S(1)}, u32[]{:S(2)}, u32[]{:S(2)}) collective-permute-start(bf16[256,512]{1,0:T(8,128)(2,1)} %param.15), channel_id=1, source_target_pairs={{0,2},{1,3},{2,0},{3,1},{4,6},{5,7},{6,4},{7,5},{8,10},{9,11},{10,... | collective-permute-start | bytes 786440 | tf_op jit(solution)/shard_map/ppermute | solution.py:91
  5.2 23.6 %collective-permute-start = (bf16[256,512]{1,0:T(8,128)(2,1)}, bf16[256,512]{1,0:T(8,128)(2,1)}, u32[]{:S(2)}, u32[]{:S(2)}) collective-permute-start(bf16[256,512]{1,0:T(8,128)(2,1)} %param.15), channel_id=1, source_target_pairs={{0,3},{1,0},{2,1},{3,2},{4,7},{5,4},{6,5},{7,6},{8,11},{9,8},{10,9... | collective-permute-start | bytes 786440 | tf_op jit(solution)/shard_map/ppermute | solution.py:91
  10.7 12.1 %all-to-all-start = ((bf16[16,3,640]{2,1,0:T(4,128)(2,1)}), bf16[16,3,640]{2,1,0:T(4,128)(2,1)S(1)}, u32[]{:S(2)}, u32[]{:S(2)}) async-start(bf16[16,3,640]{2,1,0:T(4,128)(2,1)} %gather_fusion), calls=%async_computation | async-start | bytes 163840 | tf_op jit(solution)/shard_map/all_to_all | solution.py:178
  16.8 11.3 %copy-start.28 = (s32[1024]{0:T(1024)}, s32[1024]{0:T(1024)S(1)}, u32[]{:S(2)}) copy-start(s32[1024]{0:T(1024)S(1)} %pad_clamp_fusion) | copy-start | bytes 12292
  17.7 21.8 %copy-start.18 = (f32[640]{0:T(1024)}, f32[640]{0:T(1024)S(1)}, u32[]{:S(2)}) copy-start(f32[640]{0:T(1024)S(1)} %get-tuple-element.14) | copy-start | bytes 7684
  17.7 21.8 %copy-start.20 = (f32[640]{0:T(1024)}, f32[640]{0:T(1024)S(1)}, u32[]{:S(2)}) copy-start(f32[640]{0:T(1024)S(1)} %get-tuple-element.15) | copy-start | bytes 7684
  17.7 24.6 %copy-start.22 = (f32[16,512]{1,0:T(8,128)}, f32[16,512]{1,0:T(8,128)S(1)}, u32[]{:S(2)}) copy-start(f32[16,512]{1,0:T(8,128)S(1)} %fusion.118) | copy-start | bytes 98308
  18.6 11.7 %copy-start.26 = (f32[2048]{0:T(1024)}, f32[2048]{0:T(1024)S(1)}, u32[]{:S(2)}) copy-start(f32[2048]{0:T(1024)S(1)} %fusion.126) | copy-start | bytes 24580
  18.6 23.8 %copy-start.36 = (pred[16,16]{1,0:T(8,128)(4,1)}, pred[16,16]{1,0:T(8,128)(4,1)S(1)}, u32[]{:S(2)}) copy-start(pred[16,16]{1,0:T(8,128)(4,1)S(1)} %iota_compare_fusion.4) | copy-start | bytes 772
  22.8 7.1 %copy-start.8 = (bf16[256,512]{1,0:T(8,128)(2,1)S(1)}, bf16[256,512]{1,0:T(8,128)(2,1)}, u32[]{:S(2)}) copy-start(bf16[256,512]{1,0:T(8,128)(2,1)} %param.15) | copy-start | bytes 786436
  22.8 29.7 %all-to-all-start.1 = ((bf16[16,16,2048]{2,1,0:T(8,128)(2,1)}), bf16[16,16,2048]{2,1,0:T(8,128)(2,1)}, u32[]{:S(2)}, u32[]{:S(2)}) async-start(bf16[16,16,2048]{2,1,0:T(8,128)(2,1)} %gather_fusion.2), calls=%async_computation.1 | async-start | bytes 2097152 | tf_op jit(solution)/shard_map/all_to_all | solution.py:179
  28.8 10.7 %copy-start.11 = (f32[16,3,640]{2,1,0:T(4,128)}, f32[16,3,640]{2,1,0:T(4,128)S(1)}, u32[]{:S(2)}) copy-start(f32[16,3,640]{2,1,0:T(4,128)S(1)} %convert_multiply_fusion.4) | copy-start | bytes 368644
  30.0 5.1 %copy-start.2 = (bf16[256,2048]{1,0:T(8,128)(2,1)}, bf16[256,2048]{1,0:T(8,128)(2,1)S(1)}, u32[]{:S(2)}) copy-start(bf16[256,2048]{1,0:T(8,128)(2,1)S(1)} %constant_dynamic-update-slice_fusion) | copy-start | bytes 3145732
  30.3 5.9 %copy-start.30 = (f32[1,16]{1,0:T(1,128)S(1)}, f32[1,16]{1,0:T(1,128)}, u32[]{:S(2)}) copy-start(f32[1,16]{1,0:T(1,128)} %param.21) | copy-start | bytes 196
  30.3 5.9 %copy-start.32 = (f32[1,16]{1,0:T(1,128)S(1)}, f32[1,16]{1,0:T(1,128)}, u32[]{:S(2)}) copy-start(f32[1,16]{1,0:T(1,128)} %param.20) | copy-start | bytes 196
  35.1 1.1 copy-start.14
  37.8 4.6 %copy-start.16 = (f32[16,16,16]{1,2,0:T(8,128)S(1)}, f32[16,16,16]{1,2,0:T(8,128)}, u32[]{:S(2)}) copy-start(f32[16,16,16]{1,2,0:T(8,128)} %copy.66) | copy-start | bytes 49156
  39.5 2.8 %copy-start.17 = (f32[16,16,16]{1,2,0:T(8,128)S(1)}, f32[16,16,16]{1,2,0:T(8,128)}, u32[]{:S(2)}) copy-start(f32[16,16,16]{1,2,0:T(8,128)} %copy.63) | copy-start | bytes 49156
  40.0 0.8 copy-start.7
  57.6 1.9 %copy-start.34 = (f32[512]{0:T(512)S(1)}, f32[512]{0:T(512)}, u32[]{:S(2)}) copy-start(f32[512]{0:T(512)} %mul.335) | copy-start | bytes 6148
  57.6 1.9 %copy-start.38 = (bf16[16]{0:T(256)(128)(2,1)S(1)}, bf16[16]{0:T(256)(128)(2,1)}, u32[]{:S(2)}) copy-start(bf16[16]{0:T(256)(128)(2,1)} %get-tuple-element.28) | copy-start | bytes 100
  59.5 2.6 %copy-start.4 = (bf16[16,512,64]{1,2,0:T(8,128)(2,1)}, bf16[16,512,64]{1,2,0:T(8,128)(2,1)S(1)}, u32[]{:S(2)}) copy-start(bf16[16,512,64]{1,2,0:T(8,128)(2,1)S(1)} %copy.68) | copy-start | bytes 3145732
  59.6 2.6 %copy-start.24 = (f32[1,512]{1,0:T(1,128)S(1)}, f32[1,512]{1,0:T(1,128)}, u32[]{:S(2)}) copy-start(f32[1,512]{1,0:T(1,128)} %param.23) | copy-start | bytes 6148
  68.2 25.1 %copy-start.3 = (bf16[256,2048]{1,0:T(8,128)(2,1)S(1)}, bf16[256,2048]{1,0:T(8,128)(2,1)}, u32[]{:S(2)}) copy-start(bf16[256,2048]{1,0:T(8,128)(2,1)} %copy-done.2) | copy-start | bytes 3145732
  68.3 26.6 %copy-start.27 = (f32[2048]{0:T(1024)S(1)}, f32[2048]{0:T(1024)}, u32[]{:S(2)}) copy-start(f32[2048]{0:T(1024)} %copy-done.26) | copy-start | bytes 24580
  68.4 9.3 %collective-permute-start.5 = (bf16[256,512]{1,0:T(8,128)(2,1)S(1)}, bf16[256,512]{1,0:T(8,128)(2,1)S(1)}, u32[]{:S(2)}, u32[]{:S(2)}) collective-permute-start(bf16[256,512]{1,0:T(8,128)(2,1)S(1)} %bitcast.89), channel_id=1, source_target_pairs={{0,3},{1,0},{2,1},{3,2},{4,7},{5,4},{6,5},{7,6},{8,11},{9,8},{10,9... | collective-permute-start | bytes 786440 | tf_op jit(solution)/shard_map/ppermute | solution.py:91
  68.9 12.4 %collective-permute-start.3 = (bf16[256,512]{1,0:T(8,128)(2,1)S(1)}, bf16[256,512]{1,0:T(8,128)(2,1)S(1)}, u32[]{:S(2)}, u32[]{:S(2)}) collective-permute-start(bf16[256,512]{1,0:T(8,128)(2,1)S(1)} %bitcast.88), channel_id=1, source_target_pairs={{0,1},{1,2},{2,3},{3,0},{4,5},{5,6},{6,7},{7,4},{8,9},{9,10},{10,1... | collective-permute-start | bytes 786440 | tf_op jit(solution)/shard_map/ppermute | solution.py:91
  70.4 12.3 %collective-permute-start.4 = (bf16[256,512]{1,0:T(8,128)(2,1)S(1)}, bf16[256,512]{1,0:T(8,128)(2,1)S(1)}, u32[]{:S(2)}, u32[]{:S(2)}) collective-permute-start(bf16[256,512]{1,0:T(8,128)(2,1)S(1)} %bitcast.87), channel_id=1, source_target_pairs={{0,2},{1,3},{2,0},{3,1},{4,6},{5,7},{6,4},{7,5},{8,10},{9,11},{10,... | collective-permute-start | bytes 786440 | tf_op jit(solution)/shard_map/ppermute | solution.py:91
  83.6 8.2 %collective-permute-start.9 = (bf16[256,512]{1,0:T(8,128)(2,1)}, bf16[256,512]{1,0:T(8,128)(2,1)}, u32[]{:S(2)}, u32[]{:S(2)}) collective-permute-start(bf16[256,512]{1,0:T(8,128)(2,1)} %fusion.90), channel_id=1, source_target_pairs={{0,17},{1,18},{2,19},{3,16},{4,21},{5,22},{6,23},{7,20},{8,25},{9,... | collective-permute-start | bytes 786440 | tf_op jit(solution)/shard_map/ppermute | solution.py:119
  85.8 6.0 %collective-permute-start.8 = (bf16[256,512]{1,0:T(8,128)(2,1)}, bf16[256,512]{1,0:T(8,128)(2,1)}, u32[]{:S(2)}, u32[]{:S(2)}) collective-permute-start(bf16[256,512]{1,0:T(8,128)(2,1)} %fusion.90), channel_id=1, source_target_pairs={{0,18},{1,19},{2,16},{3,17},{4,22},{5,23},{6,20},{7,21},{8,26},{9,... | collective-permute-start | bytes 786440 | tf_op jit(solution)/shard_map/ppermute | solution.py:119
  87.8 5.5 %collective-permute-start.7 = (bf16[256,512]{1,0:T(8,128)(2,1)}, bf16[256,512]{1,0:T(8,128)(2,1)}, u32[]{:S(2)}, u32[]{:S(2)}) collective-permute-start(bf16[256,512]{1,0:T(8,128)(2,1)} %fusion.90), channel_id=1, source_target_pairs={{0,19},{1,16},{2,17},{3,18},{4,23},{5,20},{6,21},{7,22},{8,27},{9,... | collective-permute-start | bytes 786440 | tf_op jit(solution)/shard_map/ppermute | solution.py:119
  89.8 3.5 %collective-permute-start.6 = (bf16[256,512]{1,0:T(8,128)(2,1)}, bf16[256,512]{1,0:T(8,128)(2,1)}, u32[]{:S(2)}, u32[]{:S(2)}) collective-permute-start(bf16[256,512]{1,0:T(8,128)(2,1)} %fusion.90), channel_id=1, source_target_pairs={{0,16},{1,17},{2,18},{3,19},{4,20},{5,21},{6,22},{7,23},{8,24},{9,... | collective-permute-start | bytes 786440 | tf_op jit(solution)/shard_map/ppermute | solution.py:119
  94.9 5.3 %copy-start.31 = (f32[1,16]{1,0:T(1,128)S(1)}, f32[1,16]{1,0:T(1,128)}, u32[]{:S(2)}) copy-start(f32[1,16]{1,0:T(1,128)} %param.21) | copy-start | bytes 196
  94.9 5.3 %copy-start.33 = (f32[1,16]{1,0:T(1,128)S(1)}, f32[1,16]{1,0:T(1,128)}, u32[]{:S(2)}) copy-start(f32[1,16]{1,0:T(1,128)} %param.20) | copy-start | bytes 196
  100.1 1.1 copy-start.13
  100.1 4.4 %copy-start.12 = (f32[16,3,640]{2,1,0:T(4,128)S(1)}, f32[16,3,640]{2,1,0:T(4,128)}, u32[]{:S(2)}) copy-start(f32[16,3,640]{2,1,0:T(4,128)} %copy-done.11) | copy-start | bytes 368644
  100.2 4.4 %copy-start.19 = (f32[640]{0:T(1024)S(1)}, f32[640]{0:T(1024)}, u32[]{:S(2)}) copy-start(f32[640]{0:T(1024)} %copy-done.18) | copy-start | bytes 7684
  100.2 4.4 %copy-start.21 = (f32[640]{0:T(1024)S(1)}, f32[640]{0:T(1024)}, u32[]{:S(2)}) copy-start(f32[640]{0:T(1024)} %copy-done.20) | copy-start | bytes 7684
  105.1 11.3 %copy-start.1 = (f32[16,16,640]{2,1,0:T(8,128)}, f32[16,16,640]{2,1,0:T(8,128)S(1)}, u32[]{:S(2)}) copy-start(f32[16,16,640]{2,1,0:T(8,128)S(1)} %divide_multiply_fusion) | copy-start | bytes 1966084
  105.1 5.0 %copy-start.23 = (f32[16,512]{1,0:T(8,128)S(1)}, f32[16,512]{1,0:T(8,128)}, u32[]{:S(2)}) copy-start(f32[16,512]{1,0:T(8,128)} %copy-done.22) | copy-start | bytes 98308
  105.1 5.0 %copy-start.37 = (pred[16,16]{1,0:T(8,128)(4,1)S(1)}, pred[16,16]{1,0:T(8,128)(4,1)}, u32[]{:S(2)}) copy-start(pred[16,16]{1,0:T(8,128)(4,1)} %copy-done.36) | copy-start | bytes 772
  110.1 6.3 %copy-start.5 = (bf16[16,512,64]{1,2,0:T(8,128)(2,1)S(1)}, bf16[16,512,64]{1,2,0:T(8,128)(2,1)}, u32[]{:S(2)}) copy-start(bf16[16,512,64]{1,2,0:T(8,128)(2,1)} %copy-done.4) | copy-start | bytes 3145732
  110.1 6.3 %copy-start.35 = (f32[512]{0:T(512)S(1)}, f32[512]{0:T(512)}, u32[]{:S(2)}) copy-start(f32[512]{0:T(512)} %mul.335) | copy-start | bytes 6148
  110.1 6.3 %copy-start.39 = (bf16[16]{0:T(256)(128)(2,1)S(1)}, bf16[16]{0:T(256)(128)(2,1)}, u32[]{:S(2)}) copy-start(bf16[16]{0:T(256)(128)(2,1)} %get-tuple-element.28) | copy-start | bytes 100
  116.4 1.7 %copy-start.25 = (f32[1,512]{1,0:T(1,128)S(1)}, f32[1,512]{1,0:T(1,128)}, u32[]{:S(2)}) copy-start(f32[1,512]{1,0:T(1,128)} %param.23) | copy-start | bytes 6148
  124.8 4.9 %copy-start.6 = (bf16[16,512,64]{1,2,0:T(8,128)(2,1)S(1)}, bf16[16,512,64]{1,2,0:T(8,128)(2,1)}, u32[]{:S(2)}) copy-start(bf16[16,512,64]{1,2,0:T(8,128)(2,1)} %copy-done.4) | copy-start | bytes 3145732
  124.8 4.9 %copy-start.9 = (f32[16,16,512]{2,1,0:T(8,128)S(1)}, f32[16,16,512]{2,1,0:T(8,128)}, u32[]{:S(2)}) copy-start(f32[16,16,512]{2,1,0:T(8,128)} %convolution_multiply_fusion.2) | copy-start | bytes 1572868
  124.8 4.9 %copy-start.15 = (f32[16,512]{1,0:T(8,128)S(1)}, f32[16,512]{1,0:T(8,128)}, u32[]{:S(2)}) copy-start(f32[16,512]{1,0:T(8,128)} %fusion.116) | copy-start | bytes 98308
  127.0 10.8 %collective-permute-start.12 = (bf16[256,512]{1,0:T(8,128)(2,1)}, bf16[256,512]{1,0:T(8,128)(2,1)}, u32[]{:S(2)}, u32[]{:S(2)}) collective-permute-start(bf16[256,512]{1,0:T(8,128)(2,1)} %bitcast.69), channel_id=1, source_target_pairs={{0,3},{1,0},{2,1},{3,2},{4,7},{5,4},{6,5},{7,6},{8,11},{9,8},{10,9... | collective-permute-start | bytes 786440 | tf_op jit(solution)/shard_map/ppermute | solution.py:91
  127.8 14.1 %collective-permute-start.10 = (bf16[256,512]{1,0:T(8,128)(2,1)}, bf16[256,512]{1,0:T(8,128)(2,1)}, u32[]{:S(2)}, u32[]{:S(2)}) collective-permute-start(bf16[256,512]{1,0:T(8,128)(2,1)} %bitcast.71), channel_id=1, source_target_pairs={{0,1},{1,2},{2,3},{3,0},{4,5},{5,6},{6,7},{7,4},{8,9},{9,10},{10,1... | collective-permute-start | bytes 786440 | tf_op jit(solution)/shard_map/ppermute | solution.py:91
  129.0 15.1 %collective-permute-start.11 = (bf16[256,512]{1,0:T(8,128)(2,1)}, bf16[256,512]{1,0:T(8,128)(2,1)}, u32[]{:S(2)}, u32[]{:S(2)}) collective-permute-start(bf16[256,512]{1,0:T(8,128)(2,1)} %bitcast.70), channel_id=1, source_target_pairs={{0,2},{1,3},{2,0},{3,1},{4,6},{5,7},{6,4},{7,5},{8,10},{9,11},{10,... | collective-permute-start | bytes 786440 | tf_op jit(solution)/shard_map/ppermute | solution.py:91
  133.5 10.6 %copy-start.10 = (bf16[256,1,512]{2,1,0:T(2,128)(2,1)S(1)}, bf16[256,1,512]{2,1,0:T(2,128)(2,1)}, u32[]{:S(2)}) copy-start(bf16[256,1,512]{2,1,0:T(2,128)(2,1)} %get-tuple-element.20) | copy-start | bytes 786436
where the time goes:
time: 147 us; the launch traced here: 146 us
  local copies, waits for them, and re-layouts  44.5 us (30%)
  matrix products  36.6 us (25%)
  starting transfers between devices  29.4 us (20%)
  waiting for transfers between devices  23.9 us (16%)
  other arithmetic  10.3 us (7%)
    ppermute x9, waiting for transfers between devices, shifted(): lax.ppermute(value, axis, [(source, (source + steps) % count) for source...  18.1 us
    dot_general x2, matrix products, mix_channels(): jnp.einsum('dtsh,dshm->dtm', weights, spread, precision=three_pass)  12 us
    ppermute x9, starting transfers between devices, shifted(): lax.ppermute(value, axis, [(source, (source + steps) % count) for source...  11.1 us
    dot_general x2, matrix products, per_device(): jnp.dot(normed, proj_rotated, preferred_element_type=jnp.float32)  9.95 us
    ppermute x4, starting transfers between devices, gather_from_behind(): parts.append(lax.ppermute(value, ('section', 'mp'), pairs))  8.16 us
    unnamed x91, local copies, waits for them, and re-layouts  7.79 us
    gather x3, local copies, waits for them, and re-layouts, per_device(): got_state[recv_row] * keep_flag.astype(jnp.bfloat16)[:, None, None]  7 us
    convert_element_type x2, local copies, waits for them, and re-layouts, mix_channels(): end_state.reshape(doc_count, head_count, head_dim * state_width)  6.07 us
  transfers between devices with their start and end apart: 15, of which 7 were waited for; matrix products, arithmetic and copies ran while one was open for 26% of the time, Pallas kernels for 0%

commit v1 on v0

--- a/solution.py
+++ b/solution.py
@@ -77,9 +77,7 @@
     new_conv = mixed_in[:, length - (kernel_len - 1) :].astype(jnp.bfloat16)
     gated = mixed_out * jax.nn.silu(gate_cols)
     gnormed = row_norm(gated, norm_scale).astype(jnp.bfloat16)
-    partial_value = jnp.dot(
-        gnormed.reshape(doc_count * length, inner), out_weight, preferred_element_type=jnp.float32
-    )
+    partial_value = gnormed.reshape(doc_count * length, inner)
     end_rounded = end_state.reshape(doc_count, head_count, head_dim * state_width).astype(
         jnp.bfloat16
     )
@@ -121,15 +119,23 @@
     return whole, parts[0]
 
 
-def scatter_sum(partial_value, base):
+def column_blocks(out_weight):
     count = lax.axis_size("mp")
     position = lax.axis_index("mp")
-    rows = partial_value.shape[0]
-    blocks = partial_value.astype(jnp.bfloat16).reshape(rows, count, -1)
-    total = base + lax.dynamic_index_in_dim(blocks, position, 1, False).astype(jnp.float32)
-    for steps in range(1, count):
-        block = lax.dynamic_index_in_dim(blocks, (position + steps) % count, 1, False)
-        total = total + shifted(block, "mp", steps).astype(jnp.float32)
+    width = out_weight.shape[1] // count
+    return [
+        lax.dynamic_slice_in_dim(out_weight, ((position + steps) % count) * width, width, 1)
+        for steps in range(count)
+    ]
+
+
+def scatter_sum(gnormed, weight_blocks, base):
+    total = base
+    for steps, weight_block in enumerate(weight_blocks):
+        block = jnp.dot(gnormed, weight_block, preferred_element_type=jnp.float32).astype(jnp.bfloat16)
+        if steps > 0:
+            block = shifted(block, "mp", steps)
+        total = total + block.astype(jnp.float32)
     return total
 
 
@@ -185,6 +191,7 @@
     conv_start = got_conv[recv_row].astype(jnp.float32) * keep_flag[:, None, None]
     gain_rotated = rotate_rows(norm_gain[0], shard_width)
     proj_rotated = rotate_rows(in_proj[0], shard_width)
+    weight_blocks = column_blocks(out_proj[0])
     results = None
     incoming = None
     first_rows = None
@@ -211,7 +218,7 @@
             gate_gain[0],
             out_proj[0],
         )
-        result = scatter_sum(partial_value, current.astype(jnp.float32)).astype(jnp.bfloat16)
+        result = scatter_sum(partial_value, weight_blocks, current.astype(jnp.float32)).astype(jnp.bfloat16)
         results = (result, state_new, conv_new)
         incoming = result
     out_rows, new_states, new_convs = results

time: 147 us -> 140 us (0.952)
  waiting for transfers between devices: 23.9 us -> 14.3 us
  matrix products: 36.6 us -> 42.5 us
  local copies, waits for them, and re-layouts: 44.5 us -> 39 us
  starting transfers between devices: 29.4 us -> 31.1 us
    dot_general x2 -> x8, matrix products: 3.41 us -> 10.5 us  [scatter_sum(): jnp.dot(gnormed, weight_block, preferred_element_type=jnp.float32)]
    ppermute x9, waiting for transfers between devices: 18.1 us -> 12.1 us  [shifted(): lax.ppermute(value, axis, [(source, (source + steps) % count) for source...]
    dynamic_slice x2 -> x0, local copies, waits for them, and re-layouts: 5.14 us -> none  [scatter_sum(): lax.dynamic_index_in_dim(blocks, position, 1, False).astype(jnp.float32)]
    all_to_all x1, waiting for transfers between devices: 4.4 us -> 0.01 us  [per_device(): lax.all_to_all(send_state, 'dp', split_axis=0, concat_axis=0, tiled=True)]
    reshape x2 -> x0, local copies, waits for them, and re-layouts: 3.87 us -> none  [scatter_sum(): blocks = partial_value.astype(jnp.bfloat16).reshape(rows, count, -1)]
    gather x3, local copies, waits for them, and re-layouts: 7 us -> 9.91 us  [per_device(): got_state[recv_row] * keep_flag.astype(jnp.bfloat16)[:, None, None]]
    ppermute x9, starting transfers between devices: 11.1 us -> 13.8 us  [shifted(): lax.ppermute(value, axis, [(source, (source + steps) % count) for source...]
    mul x2, other arithmetic: 1.01 us -> 3.09 us  [mix_channels(): activated = jax.nn.silu(conv_out)]
  transfers between devices with their start and end apart: 15 -> 15, of which waited for: 7 -> 5; matrix products, arithmetic and copies ran while one was open for 26% -> 32% of each run, Pallas kernels for 0% -> 0%
where the time goes in v1:
time: 140 us; the launch traced here: 139 us
  matrix products  42.5 us (30%)
  local copies, waits for them, and re-layouts  39 us (28%)
  starting transfers between devices  31.1 us (22%)
  waiting for transfers between devices  14.3 us (10%)
  other arithmetic  11.1 us (8%)
    ppermute x9, starting transfers between devices, shifted(): lax.ppermute(value, axis, [(source, (source + steps) % count) for source...  13.8 us
    ppermute x9, waiting for transfers between devices, shifted(): lax.ppermute(value, axis, [(source, (source + steps) % count) for source...  12.1 us
    dot_general x2, matrix products, mix_channels(): jnp.einsum('dtsh,dshm->dtm', weights, spread, precision=three_pass)  11.8 us
    dot_general x8, matrix products, scatter_sum(): jnp.dot(gnormed, weight_block, preferred_element_type=jnp.float32)  10.5 us
    gather x3, local copies, waits for them, and re-layouts, per_device(): got_state[recv_row] * keep_flag.astype(jnp.bfloat16)[:, None, None]  9.91 us
    dot_general x2, matrix products, per_device(): jnp.dot(normed, proj_rotated, preferred_element_type=jnp.float32)  9.81 us
    ppermute x4, starting transfers between devices, gather_from_behind(): parts.append(lax.ppermute(value, ('section', 'mp'), pairs))  7.25 us
    convert_element_type x2, local copies, waits for them, and re-layouts, mix_channels(): end_state.reshape(doc_count, head_count, head_dim * state_width)  7 us
  transfers between devices with their start and end apart: 15, of which 5 were waited for; matrix products, arithmetic and copies ran while one was open for 32% of the time, Pallas kernels for 0%

profile of v1, /device:TPU:0, one launch (start us, length us, event | category | flops | bytes accessed | tf_op | source)
XLA Modules:
  0.0 139.3 jit_solution(15910951529435903784)
XLA Ops:
  0.7 3.0 %collective-permute-start.2 = (bf16[256,512]{1,0:T(8,128)(2,1)}, bf16[256,512]{1,0:T(8,128)(2,1)}, u32[]{:S(2)}, u32[]{:S(2)}) collective-permute-start(bf16[256,512]{1,0:T(8,128)(2,1)} %param.15), channel_id=1, source_target_pairs={{0,1},{1,2},{2,3},{3,0},{4,5},{5,6},{6,7},{7,4},{8,9},{9,10},{10,1... | collective-permute-start | bytes 786440 | tf_op jit(solution)/shard_map/ppermute | solution.py:89
  3.6 1.5 %collective-permute-start.1 = (bf16[256,512]{1,0:T(8,128)(2,1)}, bf16[256,512]{1,0:T(8,128)(2,1)}, u32[]{:S(2)}, u32[]{:S(2)}) collective-permute-start(bf16[256,512]{1,0:T(8,128)(2,1)} %param.15), channel_id=1, source_target_pairs={{0,2},{1,3},{2,0},{3,1},{4,6},{5,7},{6,4},{7,5},{8,10},{9,11},{10,... | collective-permute-start | bytes 786440 | tf_op jit(solution)/shard_map/ppermute | solution.py:89
  5.2 1.4 %collective-permute-start = (bf16[256,512]{1,0:T(8,128)(2,1)}, bf16[256,512]{1,0:T(8,128)(2,1)}, u32[]{:S(2)}, u32[]{:S(2)}) collective-permute-start(bf16[256,512]{1,0:T(8,128)(2,1)} %param.15), channel_id=1, source_target_pairs={{0,3},{1,0},{2,1},{3,2},{4,7},{5,4},{6,5},{7,6},{8,11},{9,8},{10,9... | collective-permute-start | bytes 786440 | tf_op jit(solution)/shard_map/ppermute | solution.py:89
  6.6 0.7 reshape.255
  7.3 0.7 broadcast_in_dim.40
  8.6 0.9 copy.91
  9.4 1.3 gather_fusion
  10.7 4.9 %all-to-all-start = ((bf16[16,3,640]{2,1,0:T(4,128)(2,1)}), bf16[16,3,640]{2,1,0:T(4,128)(2,1)S(1)}, u32[]{:S(2)}, u32[]{:S(2)}) async-start(bf16[16,3,640]{2,1,0:T(4,128)(2,1)} %gather_fusion), calls=%async_computation | async-start | bytes 163840 | tf_op jit(solution)/shard_map/all_to_all | solution.py:184
  16.2 0.9 slice_reduce_fusion.3
  17.2 0.8 fusion.137
  18.1 0.7 broadcast_in_dim.43
  18.9 2.8 %gather_fusion.2 = bf16[16,16,2048]{2,1,0:T(8,128)(2,1)} fusion(bf16[16,16,2048]{2,1,0:T(8,128)(2,1)} %bitcast.81, s32[1024]{0:T(1024)S(1)} %pad_clamp_fusion.1), kind=kCustom, calls=%fused_computation.2 | custom fusion | bytes 2097216 | tf_op jit(solution)/shard_map/gather | solution.py:182
  21.7 5.2 %all-to-all-start.1 = ((bf16[16,16,2048]{2,1,0:T(8,128)(2,1)}), bf16[16,16,2048]{2,1,0:T(8,128)(2,1)}, u32[]{:S(2)}, u32[]{:S(2)}) async-start(bf16[16,16,2048]{2,1,0:T(8,128)(2,1)} %gather_fusion.2), calls=%async_computation.1 | async-start | bytes 2097152 | tf_op jit(solution)/shard_map/all_to_all | solution.py:185
  27.6 0.8 convert_multiply_fusion.4
  28.4 1.0 constant_dynamic-update-slice_fusion.3
  29.4 1.0 constant_dynamic-update-slice_fusion.2
  30.4 1.0 constant_dynamic-update-slice_fusion.1
  31.7 4.7 %fusion.46 = f32[256,1168]{1,0:T(8,128)S(1)} fusion(bf16[256,2048]{1,0:T(8,128)(2,1)S(1)} %constant_dynamic-update-slice_fusion, f32[2048]{0:T(1024)S(1)} %fusion.137, f32[256]{0:T(256)S(1)} %add_rsqrt_fusion.3, s32[]{:T(128)S(6)} %select_n.123, bf16[2048,1168]{0,1:T(8,128)(2,1)} %bitcast.98), kind=kOutput, calls=%fused_computation.65 | convolution fusion | flops 1236402176 | bytes 7037956 | tf_op jit(solution)/shard_map/dot_general | solution.py:208
  36.5 0.9 slice.116
  37.7 0.7 negate_multiply_fusion.1
  38.5 0.8 copy.56
  39.2 1.6 %fusion.162 = (f32[16,16,16]{2,0,1:T(8,128)S(1)}, f32[16,16,16]{2,0,1:T(8,128)}) fusion(f32[16,16,16]{2,1,0:T(8,128)} %get-tuple-element.18), kind=kOutput, calls=%fused_computation.224 | output fusion | flops 61440 | bytes 49152 | tf_op jit(solution)/shard_map/jit(cumsum)/reduce_window_sum | solution.py:60
  40.9 1.7 %copy.53 = f32[16,16,16]{1,2,0:T(8,128)} copy(f32[16,16,16]{2,0,1:T(8,128)} %get-tuple-element.23) | data formatting | bytes 32768 | tf_op jit(solution)/shard_map/jit(cumsum)/reduce_window_sum | solution.py:60
  42.6 2.6 %divide_multiply_fusion.1 = f32[16,16,640]{2,1,0:T(8,128)S(1)} fusion(f32[16,16,640]{2,1,0:T(8,128)} %slice.116, f32[16,3,640]{2,1,0:T(4,128)S(1)} %copy-done.5, f32[640]{0:T(1024)S(1)} %get-tuple-element.14, f32[640]{0:T(1024)S(1)} %get-tuple-element.15, f32[640]{0:T(1024)S(1)} %get-tuple-element.13, f32[640]{0:T(1024)S(1)} %get-tuple-element.12, ...), kind=kLoop, calls=%fused_computation.106 | loop fusion | flops 2457600 | bytes 1446400 | tf_op jit(solution)/shard_map/jit(silu)/mul | solution.py:48
  45.2 0.8 copy-done.2
  46.3 1.2 fusion.114
  47.5 5.7 %fusion.31 = f32[16,16,512]{2,1,0:T(8,128)} fusion(f32[16,512]{1,0:T(8,128)S(1)} %fusion.129, f32[16,16,512]{2,1,0:T(8,128)S(1)} %slice.123, f32[16,16,16]{1,2,0:T(8,128)S(1)} %copy-done.12, f32[16,16,16]{2,1,0:T(8,128)S(1)} %fusion.105, f32[16,16,16]{1,2,0:T(8,128)S(1)} %copy-done.13, pred[16,16]{1,0:T(8,128)(4,1)S(1)} %iota_compare_fusion.4), kind=kOutput, calls=%fused_computation.47 | convolution fusion | flops 203685888 | bytes 1130752 | tf_op jit(solution)/shard_map/dtsh,dshm->dtm/dot_general | solution.py:68
  53.2 2.8 %gather_fusion.3 = bf16[16,16,2048]{2,1,0:T(8,128)(2,1)} fusion(bf16[16,16,2048]{2,1,0:T(8,128)(2,1)} %all-to-all-done.1, s32[1024]{0:T(1024)S(1)} %pad_clamp_fusion), kind=kCustom, calls=%fused_computation.3 | custom fusion | bytes 2097216 | tf_op jit(solution)/shard_map/gather | solution.py:190
  56.0 4.4 %gather.18 = bf16[16,512,64]{2,1,0:T(8,128)(2,1)} reshape(bf16[16,16,2048]{2,1,0:T(8,128)(2,1)} %gather_fusion.3) | data formatting | bytes 2097152 | tf_op jit(solution)/shard_map/gather | solution.py:190
  60.4 2.7 %copy.58 = bf16[16,512,64]{1,2,0:T(8,128)(2,1)} copy(bf16[16,512,64]{2,1,0:T(8,128)(2,1)} %gather.18) | data formatting | bytes 2097152 | tf_op jit(solution)/shard_map/gather | solution.py:190
  63.1 2.5 %multiply_reduce_fusion.1 = (f32[16,16]{1,0:T(8,128)S(1)}, f32[16,16,512]{2,1,0:T(8,128)S(1)}) fusion(f32[16,16,1168]{2,1,0:T(8,128)} %bitcast.88, f32[16,16,640]{2,1,0:T(8,128)} %copy-done.2, f32[512]{0:T(512)S(1)} %mul.345, f32[16,16,512]{2,1,0:T(8,128)} %fusion.31, f32[16,16,512]{2,1,0:T(8,128)} %fusion.114, bf16[16,512,64]{1,2,0:T(8,128)(2,1)} %copy.58, ...), kind=kOutput, calls=%fused_computation.120 | convolution fusion | flops 52297472 | bytes 3804192 | tf_op jit(solution)/shard_map/dtn,dmn->dtm/dot_general | solution.py:70
  65.8 1.0 convolution_convert_fusion.4
  66.8 1.0 convolution_convert_fusion.5
  67.8 1.0 convolution_convert_fusion.6
  69.9 2.4 %collective-permute-start.5 = (bf16[256,512]{1,0:T(8,128)(2,1)}, bf16[256,512]{1,0:T(8,128)(2,1)}, u32[]{:S(2)}, u32[]{:S(2)}) collective-permute-start(bf16[256,512]{1,0:T(8,128)(2,1)} %convolution_convert_fusion.4), channel_id=1, source_target_pairs={{0,3},{1,0},{2,1},{3,2},{4,7},{5,4},{6,5},{7,6},{8,11},{9,8},{10,9... | collective-permute-start | bytes 786440 | tf_op jit(solution)/shard_map/ppermute | solution.py:89
  72.3 7.0 %collective-permute-done.3 = bf16[256,512]{1,0:T(8,128)(2,1)} collective-permute-done((bf16[256,512]{1,0:T(8,128)(2,1)}, bf16[256,512]{1,0:T(8,128)(2,1)}, u32[]{:S(2)}, u32[]{:S(2)}) %collective-permute-start.3) | collective-permute-done | bytes 262176 | tf_op jit(solution)/shard_map/ppermute | solution.py:89
  79.3 2.2 %collective-permute-done.4 = bf16[256,512]{1,0:T(8,128)(2,1)} collective-permute-done((bf16[256,512]{1,0:T(8,128)(2,1)}, bf16[256,512]{1,0:T(8,128)(2,1)}, u32[]{:S(2)}, u32[]{:S(2)}) %collective-permute-start.4) | collective-permute-done | bytes 262176 | tf_op jit(solution)/shard_map/ppermute | solution.py:89
  81.5 2.3 %add_convert_fusion.2 = bf16[256,512]{1,0:T(8,128)(2,1)} fusion(bf16[256,512]{1,0:T(8,128)(2,1)} %collective-permute-done.5, bf16[256,512]{1,0:T(8,128)(2,1)} %collective-permute-done.4, bf16[256,512]{1,0:T(8,128)(2,1)} %collective-permute-done.3, bf16[256,512]{1,0:T(8,128)(2,1)S(1)} %bitcast.76, bf16[256,512]{1,0:T(8,128)(2,1)} %param.15, ...), kind=kOutput, calls=%fused_computation.118 | convolution fusion | flops 135659520 | bytes 2097156 | tf_op jit(solution)/shard_map/dot_general | solution.py:135
  83.8 2.0 %collective-permute-start.9 = (bf16[256,512]{1,0:T(8,128)(2,1)}, bf16[256,512]{1,0:T(8,128)(2,1)}, u32[]{:S(2)}, u32[]{:S(2)}) collective-permute-start(bf16[256,512]{1,0:T(8,128)(2,1)} %add_convert_fusion.2), channel_id=1, source_target_pairs={{0,17},{1,18},{2,19},{3,16},{4,21},{5,22},{6,23},{7,20},{8,25},{9,... | collective-permute-start | bytes 786440 | tf_op jit(solution)/shard_map/ppermute | solution.py:117
  85.8 2.0 %collective-permute-start.8 = (bf16[256,512]{1,0:T(8,128)(2,1)}, bf16[256,512]{1,0:T(8,128)(2,1)}, u32[]{:S(2)}, u32[]{:S(2)}) collective-permute-start(bf16[256,512]{1,0:T(8,128)(2,1)} %add_convert_fusion.2), channel_id=1, source_target_pairs={{0,18},{1,19},{2,16},{3,17},{4,22},{5,23},{6,20},{7,21},{8,26},{9,... | collective-permute-start | bytes 786440 | tf_op jit(solution)/shard_map/ppermute | solution.py:117
  87.7 2.0 %collective-permute-start.7 = (bf16[256,512]{1,0:T(8,128)(2,1)}, bf16[256,512]{1,0:T(8,128)(2,1)}, u32[]{:S(2)}, u32[]{:S(2)}) collective-permute-start(bf16[256,512]{1,0:T(8,128)(2,1)} %add_convert_fusion.2), channel_id=1, source_target_pairs={{0,19},{1,16},{2,17},{3,18},{4,23},{5,20},{6,21},{7,22},{8,27},{9,... | collective-permute-start | bytes 786440 | tf_op jit(solution)/shard_map/ppermute | solution.py:117
  89.7 1.3 collective-permute-start.6
  91.0 1.9 %collective-permute-done.8 = bf16[256,512]{1,0:T(8,128)(2,1)} collective-permute-done((bf16[256,512]{1,0:T(8,128)(2,1)}, bf16[256,512]{1,0:T(8,128)(2,1)}, u32[]{:S(2)}, u32[]{:S(2)}) %collective-permute-start.8) | collective-permute-done | bytes 262176 | tf_op jit(solution)/shard_map/ppermute | solution.py:117
  93.3 1.5 %fusion.12 = f32[256]{0:T(256)S(1)} fusion(bf16[256,2048]{1,0:T(8,128)(2,1)S(1)} %constant_dynamic-update-slice_fusion, bf16[256,512]{1,0:T(8,128)(2,1)S(1)} %collective-permute-done.6, bf16[256,512]{1,0:T(8,128)(2,1)} %collective-permute-done.9, bf16[256,512]{1,0:T(8,128)(2,1)} %collective-permute-done.8, bf16[256,512]{1,0:T(8,128)(2,1)} %collective-permute-done.7, ...), kind=kLoop, calls=%fused_computation.22 | loop fusion | flops 6291200 | bytes 2098177 | tf_op jit(solution)/shard_map/reduce_sum | solution.py:18
  94.8 5.1 %fusion.44 = f32[256,1168]{1,0:T(8,128)S(1)} fusion(f32[256]{0:T(256)S(1)} %add_rsqrt_fusion.2, f32[2048]{0:T(1024)} %copy-done.22, bf16[256,2048]{1,0:T(8,128)(2,1)S(1)} %constant_dynamic-update-slice_fusion, bf16[256,512]{1,0:T(8,128)(2,1)S(1)} %collective-permute-done.6, bf16[256,512]{1,0:T(8,128)(2,1)} %collective-permute-done.9, ...), kind=kOutput, calls=%fused_computation.64 | convolution fusion | flops 1241120768 | bytes 8086533 | tf_op jit(solution)/shard_map/dot_general | solution.py:208
  101.1 0.7 fusion.163
  102.4 0.8 fusion.127
  103.1 0.8 copy.61
  103.9 1.1 slice.126
  105.9 0.8 slice.133
  106.7 0.8 copy.63
  107.5 1.3 fusion.110
  108.8 6.1 %fusion.36 = f32[16,16,512]{2,1,0:T(8,128)S(1)} fusion(f32[16,16,512]{2,1,0:T(8,128)} %slice.133, f32[16,512]{1,0:T(8,128)} %copy-done.19, f32[16,16,16]{1,2,0:T(8,128)} %copy.63, f32[16,16,16]{2,1,0:T(8,128)S(1)} %fusion.119, f32[16,16,16]{1,2,0:T(8,128)S(1)} %copy-done.11, pred[16,16]{1,0:T(8,128)(4,1)S(1)} %copy-done.31), kind=kOutput, calls=%fused_computation.48 | convolution fusion | flops 203685888 | bytes 1130752 | tf_op jit(solution)/shard_map/dtsh,dshm->dtm/dot_general | solution.py:68
  114.9 1.6 %multiply_reduce_fusion = (f32[16,16]{1,0:T(8,128)S(1)}, f32[16,16,512]{2,1,0:T(8,128)S(1)}) fusion(f32[16,16,1168]{2,1,0:T(8,128)} %bitcast.85, f32[16,16,640]{2,1,0:T(8,128)S(1)} %divide_multiply_fusion, f32[512]{0:T(512)S(1)} %copy-done.29, f32[16,16,512]{2,1,0:T(8,128)S(1)} %fusion.36, f32[16,16,512]{2,1,0:T(8,128)S(1)} %fusion.110, ...), kind=kOutput, calls=%fused_computation.117 | convolution fusion | flops 52297472 | bytes 3804192 | tf_op jit(solution)/shard_map/dtn,dmn->dtm/dot_general | solution.py:70
  116.7 1.0 convolution_convert_fusion
  117.7 1.0 convolution_convert_fusion.1
  118.7 1.0 convolution_convert_fusion.2
  120.7 2.4 %collective-permute-start.10 = (bf16[256,512]{1,0:T(8,128)(2,1)}, bf16[256,512]{1,0:T(8,128)(2,1)S(1)}, u32[]{:S(2)}, u32[]{:S(2)}) collective-permute-start(bf16[256,512]{1,0:T(8,128)(2,1)} %convolution_convert_fusion.2), channel_id=1, source_target_pairs={{0,1},{1,2},{2,3},{3,0},{4,5},{5,6},{6,7},{7,4},{8,9},{9,10},{10,1... | collective-permute-start | bytes 786440 | tf_op jit(solution)/shard_map/ppermute | solution.py:89
  123.1 1.6 %collective-permute-start.11 = (bf16[256,512]{1,0:T(8,128)(2,1)}, bf16[256,512]{1,0:T(8,128)(2,1)}, u32[]{:S(2)}, u32[]{:S(2)}) collective-permute-start(bf16[256,512]{1,0:T(8,128)(2,1)} %convolution_convert_fusion.1), channel_id=1, source_target_pairs={{0,2},{1,3},{2,0},{3,1},{4,6},{5,7},{6,4},{7,5},{8,10},{9,11},{10,... | collective-permute-start | bytes 786440 | tf_op jit(solution)/shard_map/ppermute | solution.py:89
  125.1 2.2 %add_convert_fusion = bf16[16,512,64]{1,2,0:T(8,128)(2,1)} fusion(f32[16,16,512]{2,1,0:T(8,128)S(1)} %convolution_multiply_fusion.2, f32[16,512]{1,0:T(8,128)S(1)} %copy-done.10, bf16[16,512,64]{1,2,0:T(8,128)(2,1)S(1)} %copy-done.1, bf16[16]{0:T(256)(128)(2,1)S(1)} %copy-done.33, f32[16,16,640]{2,1,0:T(8,128)S(1)} %divide_multiply_fusion), kind=kOutput, calls=%fused_computation.25 | convolution fusion | flops 52953088 | bytes 2785792 | tf_op jit(solution)/shard_map/dsm,dsn->dmn/dot_general | solution.py:76
  127.3 2.7 %copy.66 = bf16[16,512,64]{2,1,0:T(8,128)(2,1)} copy(bf16[16,512,64]{1,2,0:T(8,128)(2,1)} %add_convert_fusion) | data formatting | bytes 2097152 | tf_op jit(solution)/shard_map/convert_element_type | solution.py:81
  130.0 4.3 %convert_element_type.151 = bf16[1,16,16,2048]{3,2,1,0:T(8,128)(2,1)} reshape(bf16[16,512,64]{2,1,0:T(8,128)(2,1)} %copy.66) | data formatting | bytes 2097152 | tf_op jit(solution)/shard_map/convert_element_type | solution.py:81
  134.3 2.9 %collective-permute-done.11 = bf16[256,512]{1,0:T(8,128)(2,1)} collective-permute-done((bf16[256,512]{1,0:T(8,128)(2,1)}, bf16[256,512]{1,0:T(8,128)(2,1)}, u32[]{:S(2)}, u32[]{:S(2)}) %collective-permute-start.11) | collective-permute-done | bytes 262176 | tf_op jit(solution)/shard_map/ppermute | solution.py:89
  137.2 2.1 %fusion.104 = bf16[1,256,512]{2,1,0:T(8,128)(2,1)} fusion(bf16[256,512]{1,0:T(8,128)(2,1)} %collective-permute-done.12, bf16[256,512]{1,0:T(8,128)(2,1)} %collective-permute-done.11, bf16[256,512]{1,0:T(8,128)(2,1)S(1)} %collective-permute-done.10, bf16[256,512]{1,0:T(8,128)(2,1)S(1)} %copy-done.4, bf16[256,512]{1,0:T(8,128)(2,1)S(1)} %collective-permute-done.6, ...), kind=kOutput, calls=%fused_computation.133 | convolution fusion | flops 135790592 | bytes 2359301 | tf_op jit(solution)/shard_map/dot_general | solution.py:135
  (114 shorter events, 8.6 us)
Async XLA Ops:
  0.6 65.1 %copy-start = (bf16[1,512,2048]{2,1,0:T(8,128)(2,1)S(1)}, bf16[1,512,2048]{2,1,0:T(8,128)(2,1)}, u32[]{:S(2)}) copy-start(bf16[1,512,2048]{2,1,0:T(8,128)(2,1)} %param.24) | copy-start | bytes 6291460
  0.6 21.1 %copy-start.23 = (f32[1,640]{1,0:T(1,128)S(1)}, f32[1,640]{1,0:T(1,128)}, u32[]{:S(2)}) copy-start(f32[1,640]{1,0:T(1,128)} %param.19) | copy-start | bytes 7684
  0.7 29.7 %collective-permute-start.2 = (bf16[256,512]{1,0:T(8,128)(2,1)}, bf16[256,512]{1,0:T(8,128)(2,1)}, u32[]{:S(2)}, u32[]{:S(2)}) collective-permute-start(bf16[256,512]{1,0:T(8,128)(2,1)} %param.15), channel_id=1, source_target_pairs={{0,1},{1,2},{2,3},{3,0},{4,5},{5,6},{6,7},{7,4},{8,9},{9,10},{10,1... | collective-permute-start | bytes 786440 | tf_op jit(solution)/shard_map/ppermute | solution.py:89
  3.6 25.7 %collective-permute-start.1 = (bf16[256,512]{1,0:T(8,128)(2,1)}, bf16[256,512]{1,0:T(8,128)(2,1)}, u32[]{:S(2)}, u32[]{:S(2)}) collective-permute-start(bf16[256,512]{1,0:T(8,128)(2,1)} %param.15), channel_id=1, source_target_pairs={{0,2},{1,3},{2,0},{3,1},{4,6},{5,7},{6,4},{7,5},{8,10},{9,11},{10,... | collective-permute-start | bytes 786440 | tf_op jit(solution)/shard_map/ppermute | solution.py:89
  5.2 23.2 %collective-permute-start = (bf16[256,512]{1,0:T(8,128)(2,1)}, bf16[256,512]{1,0:T(8,128)(2,1)}, u32[]{:S(2)}, u32[]{:S(2)}) collective-permute-start(bf16[256,512]{1,0:T(8,128)(2,1)} %param.15), channel_id=1, source_target_pairs={{0,3},{1,0},{2,1},{3,2},{4,7},{5,4},{6,5},{7,6},{8,11},{9,8},{10,9... | collective-permute-start | bytes 786440 | tf_op jit(solution)/shard_map/ppermute | solution.py:89
  10.7 11.1 %all-to-all-start = ((bf16[16,3,640]{2,1,0:T(4,128)(2,1)}), bf16[16,3,640]{2,1,0:T(4,128)(2,1)S(1)}, u32[]{:S(2)}, u32[]{:S(2)}) async-start(bf16[16,3,640]{2,1,0:T(4,128)(2,1)} %gather_fusion), calls=%async_computation | async-start | bytes 163840 | tf_op jit(solution)/shard_map/all_to_all | solution.py:184
  16.2 46.9 %copy-start.32 = (bf16[16]{0:T(256)(128)(2,1)}, bf16[16]{0:T(256)(128)(2,1)S(1)}, u32[]{:S(2)}) copy-start(bf16[16]{0:T(256)(128)(2,1)S(1)} %get-tuple-element.20) | copy-start | bytes 100
  17.1 25.4 %copy-start.14 = (f32[640]{0:T(1024)}, f32[640]{0:T(1024)S(1)}, u32[]{:S(2)}) copy-start(f32[640]{0:T(1024)S(1)} %get-tuple-element.14) | copy-start | bytes 7684
  17.1 25.4 %copy-start.16 = (f32[640]{0:T(1024)}, f32[640]{0:T(1024)S(1)}, u32[]{:S(2)}) copy-start(f32[640]{0:T(1024)S(1)} %get-tuple-element.15) | copy-start | bytes 7684
  17.2 30.3 %copy-start.19 = (f32[16,512]{1,0:T(8,128)}, f32[16,512]{1,0:T(8,128)S(1)}, u32[]{:S(2)}) copy-start(f32[16,512]{1,0:T(8,128)S(1)} %fusion.129) | copy-start | bytes 98308
  18.0 13.7 %copy-start.22 = (f32[2048]{0:T(1024)}, f32[2048]{0:T(1024)S(1)}, u32[]{:S(2)}) copy-start(f32[2048]{0:T(1024)S(1)} %fusion.137) | copy-start | bytes 24580
  18.0 29.4 %copy-start.30 = (pred[16,16]{1,0:T(8,128)(4,1)}, pred[16,16]{1,0:T(8,128)(4,1)S(1)}, u32[]{:S(2)}) copy-start(pred[16,16]{1,0:T(8,128)(4,1)S(1)} %iota_compare_fusion.4) | copy-start | bytes 772
  18.9 44.2 %copy-start.28 = (f32[512]{0:T(512)}, f32[512]{0:T(512)S(1)}, u32[]{:S(2)}) copy-start(f32[512]{0:T(512)S(1)} %mul.345) | copy-start | bytes 6148
  21.7 9.6 %copy-start.3 = (bf16[256,512]{1,0:T(8,128)(2,1)S(1)}, bf16[256,512]{1,0:T(8,128)(2,1)}, u32[]{:S(2)}) copy-start(bf16[256,512]{1,0:T(8,128)(2,1)} %param.15) | copy-start | bytes 786436
  21.7 31.5 %all-to-all-start.1 = ((bf16[16,16,2048]{2,1,0:T(8,128)(2,1)}), bf16[16,16,2048]{2,1,0:T(8,128)(2,1)}, u32[]{:S(2)}, u32[]{:S(2)}) async-start(bf16[16,16,2048]{2,1,0:T(8,128)(2,1)} %gather_fusion.2), calls=%async_computation.1 | async-start | bytes 2097152 | tf_op jit(solution)/shard_map/all_to_all | solution.py:185
  31.7 6.0 %copy-start.24 = (f32[1,16]{1,0:T(1,128)S(1)}, f32[1,16]{1,0:T(1,128)}, u32[]{:S(2)}) copy-start(f32[1,16]{1,0:T(1,128)} %param.21) | copy-start | bytes 196
  31.7 6.0 %copy-start.26 = (f32[1,16]{1,0:T(1,128)S(1)}, f32[1,16]{1,0:T(1,128)}, u32[]{:S(2)}) copy-start(f32[1,16]{1,0:T(1,128)} %param.20) | copy-start | bytes 196
  36.4 1.3 copy-start.8
  36.4 6.1 %copy-start.5 = (f32[16,3,640]{2,1,0:T(4,128)S(1)}, f32[16,3,640]{2,1,0:T(4,128)}, u32[]{:S(2)}) copy-start(f32[16,3,640]{2,1,0:T(4,128)} %convert_multiply_fusion.4) | copy-start | bytes 368644
  42.6 4.9 %copy-start.12 = (f32[16,16,16]{1,2,0:T(8,128)S(1)}, f32[16,16,16]{1,2,0:T(8,128)}, u32[]{:S(2)}) copy-start(f32[16,16,16]{1,2,0:T(8,128)} %copy.56) | copy-start | bytes 49156
  42.6 4.9 %copy-start.13 = (f32[16,16,16]{1,2,0:T(8,128)S(1)}, f32[16,16,16]{1,2,0:T(8,128)}, u32[]{:S(2)}) copy-start(f32[16,16,16]{1,2,0:T(8,128)} %copy.53) | copy-start | bytes 49156
  45.2 0.8 copy-start.2
  63.1 2.5 %copy-start.20 = (f32[1,512]{1,0:T(1,128)S(1)}, f32[1,512]{1,0:T(1,128)}, u32[]{:S(2)}) copy-start(f32[1,512]{1,0:T(1,128)} %param.23) | copy-start | bytes 6148
  68.8 10.4 %collective-permute-start.3 = (bf16[256,512]{1,0:T(8,128)(2,1)}, bf16[256,512]{1,0:T(8,128)(2,1)}, u32[]{:S(2)}, u32[]{:S(2)}) collective-permute-start(bf16[256,512]{1,0:T(8,128)(2,1)} %convolution_convert_fusion.6), channel_id=1, source_target_pairs={{0,1},{1,2},{2,3},{3,0},{4,5},{5,6},{6,7},{7,4},{8,9},{9,10},{10,1... | collective-permute-start | bytes 786440 | tf_op jit(solution)/shard_map/ppermute | solution.py:89
  69.5 12.0 %collective-permute-start.4 = (bf16[256,512]{1,0:T(8,128)(2,1)}, bf16[256,512]{1,0:T(8,128)(2,1)}, u32[]{:S(2)}, u32[]{:S(2)}) collective-permute-start(bf16[256,512]{1,0:T(8,128)(2,1)} %convolution_convert_fusion.5), channel_id=1, source_target_pairs={{0,2},{1,3},{2,0},{3,1},{4,6},{5,7},{6,4},{7,5},{8,10},{9,11},{10,... | collective-permute-start | bytes 786440 | tf_op jit(solution)/shard_map/ppermute | solution.py:89
  69.9 11.6 %collective-permute-start.5 = (bf16[256,512]{1,0:T(8,128)(2,1)}, bf16[256,512]{1,0:T(8,128)(2,1)}, u32[]{:S(2)}, u32[]{:S(2)}) collective-permute-start(bf16[256,512]{1,0:T(8,128)(2,1)} %convolution_convert_fusion.4), channel_id=1, source_target_pairs={{0,3},{1,0},{2,1},{3,2},{4,7},{5,4},{6,5},{7,6},{8,11},{9,8},{10,9... | collective-permute-start | bytes 786440 | tf_op jit(solution)/shard_map/ppermute | solution.py:89
  83.8 7.3 %collective-permute-start.9 = (bf16[256,512]{1,0:T(8,128)(2,1)}, bf16[256,512]{1,0:T(8,128)(2,1)}, u32[]{:S(2)}, u32[]{:S(2)}) collective-permute-start(bf16[256,512]{1,0:T(8,128)(2,1)} %add_convert_fusion.2), channel_id=1, source_target_pairs={{0,17},{1,18},{2,19},{3,16},{4,21},{5,22},{6,23},{7,20},{8,25},{9,... | collective-permute-start | bytes 786440 | tf_op jit(solution)/shard_map/ppermute | solution.py:117
  85.8 7.2 %collective-permute-start.8 = (bf16[256,512]{1,0:T(8,128)(2,1)}, bf16[256,512]{1,0:T(8,128)(2,1)}, u32[]{:S(2)}, u32[]{:S(2)}) collective-permute-start(bf16[256,512]{1,0:T(8,128)(2,1)} %add_convert_fusion.2), channel_id=1, source_target_pairs={{0,18},{1,19},{2,16},{3,17},{4,22},{5,23},{6,20},{7,21},{8,26},{9,... | collective-permute-start | bytes 786440 | tf_op jit(solution)/shard_map/ppermute | solution.py:117
  87.7 5.5 %collective-permute-start.7 = (bf16[256,512]{1,0:T(8,128)(2,1)}, bf16[256,512]{1,0:T(8,128)(2,1)}, u32[]{:S(2)}, u32[]{:S(2)}) collective-permute-start(bf16[256,512]{1,0:T(8,128)(2,1)} %add_convert_fusion.2), channel_id=1, source_target_pairs={{0,19},{1,16},{2,17},{3,18},{4,23},{5,20},{6,21},{7,22},{8,27},{9,... | collective-permute-start | bytes 786440 | tf_op jit(solution)/shard_map/ppermute | solution.py:117
  89.7 3.5 %collective-permute-start.6 = (bf16[256,512]{1,0:T(8,128)(2,1)}, bf16[256,512]{1,0:T(8,128)(2,1)S(1)}, u32[]{:S(2)}, u32[]{:S(2)}) collective-permute-start(bf16[256,512]{1,0:T(8,128)(2,1)} %add_convert_fusion.2), channel_id=1, source_target_pairs={{0,16},{1,17},{2,18},{3,19},{4,20},{5,21},{6,22},{7,23},{8,24},{9,... | collective-permute-start | bytes 786440 | tf_op jit(solution)/shard_map/ppermute | solution.py:117
  94.8 5.9 %copy-start.25 = (f32[1,16]{1,0:T(1,128)S(1)}, f32[1,16]{1,0:T(1,128)}, u32[]{:S(2)}) copy-start(f32[1,16]{1,0:T(1,128)} %param.21) | copy-start | bytes 196
  94.8 5.8 %copy-start.27 = (f32[1,16]{1,0:T(1,128)S(1)}, f32[1,16]{1,0:T(1,128)}, u32[]{:S(2)}) copy-start(f32[1,16]{1,0:T(1,128)} %param.20) | copy-start | bytes 196
  99.9 1.1 copy-start.7
  100.0 5.1 %copy-start.6 = (f32[16,3,640]{2,1,0:T(4,128)S(1)}, f32[16,3,640]{2,1,0:T(4,128)}, u32[]{:S(2)}) copy-start(f32[16,3,640]{2,1,0:T(4,128)} %convert_multiply_fusion.4) | copy-start | bytes 368644
  100.0 5.1 %copy-start.15 = (f32[640]{0:T(1024)S(1)}, f32[640]{0:T(1024)}, u32[]{:S(2)}) copy-start(f32[640]{0:T(1024)} %copy-done.14) | copy-start | bytes 7684
  100.0 5.1 %copy-start.17 = (f32[640]{0:T(1024)S(1)}, f32[640]{0:T(1024)}, u32[]{:S(2)}) copy-start(f32[640]{0:T(1024)} %copy-done.16) | copy-start | bytes 7684
  105.5 3.2 %copy-start.11 = (f32[16,16,16]{1,2,0:T(8,128)S(1)}, f32[16,16,16]{1,2,0:T(8,128)}, u32[]{:S(2)}) copy-start(f32[16,16,16]{1,2,0:T(8,128)} %copy.61) | copy-start | bytes 49156
  105.5 3.2 %copy-start.31 = (pred[16,16]{1,0:T(8,128)(4,1)S(1)}, pred[16,16]{1,0:T(8,128)(4,1)}, u32[]{:S(2)}) copy-start(pred[16,16]{1,0:T(8,128)(4,1)} %copy-done.30) | copy-start | bytes 772
  108.7 6.1 %copy-start.1 = (bf16[16,512,64]{1,2,0:T(8,128)(2,1)S(1)}, bf16[16,512,64]{1,2,0:T(8,128)(2,1)}, u32[]{:S(2)}) copy-start(bf16[16,512,64]{1,2,0:T(8,128)(2,1)} %copy.58) | copy-start | bytes 3145732
  108.7 6.1 %copy-start.29 = (f32[512]{0:T(512)S(1)}, f32[512]{0:T(512)}, u32[]{:S(2)}) copy-start(f32[512]{0:T(512)} %copy-done.28) | copy-start | bytes 6148
  108.8 6.1 %copy-start.33 = (bf16[16]{0:T(256)(128)(2,1)S(1)}, bf16[16]{0:T(256)(128)(2,1)}, u32[]{:S(2)}) copy-start(bf16[16]{0:T(256)(128)(2,1)} %copy-done.32) | copy-start | bytes 100
  114.9 1.7 %copy-start.21 = (f32[1,512]{1,0:T(1,128)S(1)}, f32[1,512]{1,0:T(1,128)}, u32[]{:S(2)}) copy-start(f32[1,512]{1,0:T(1,128)} %param.23) | copy-start | bytes 6148
  116.5 3.2 %copy-start.9 = (bf16[1,16,3,640]{3,2,1,0:T(4,128)(2,1)S(1)}, bf16[1,16,3,640]{3,2,1,0:T(4,128)(2,1)}, u32[]{:S(2)}) copy-start(bf16[1,16,3,640]{3,2,1,0:T(4,128)(2,1)} %fusion.125) | copy-start | bytes 184324
  116.5 3.8 %copy-start.18 = (f32[16,16]{1,0:T(8,128)S(1)}, f32[16,16]{1,0:T(8,128)}, u32[]{:S(2)}) copy-start(f32[16,16]{1,0:T(8,128)} %slice_bitcast_fusion) | copy-start | bytes 3076
  116.7 8.4 %copy-start.10 = (f32[16,512]{1,0:T(8,128)S(1)}, f32[16,512]{1,0:T(8,128)}, u32[]{:S(2)}) copy-start(f32[16,512]{1,0:T(8,128)} %fusion.127) | copy-start | bytes 98308
  120.7 13.5 %collective-permute-start.10 = (bf16[256,512]{1,0:T(8,128)(2,1)}, bf16[256,512]{1,0:T(8,128)(2,1)S(1)}, u32[]{:S(2)}, u32[]{:S(2)}) collective-permute-start(bf16[256,512]{1,0:T(8,128)(2,1)} %convolution_convert_fusion.2), channel_id=1, source_target_pairs={{0,1},{1,2},{2,3},{3,0},{4,5},{5,6},{6,7},{7,4},{8,9},{9,10},{10,1... | collective-permute-start | bytes 786440 | tf_op jit(solution)/shard_map/ppermute | solution.py:89
  123.1 14.1 %collective-permute-start.11 = (bf16[256,512]{1,0:T(8,128)(2,1)}, bf16[256,512]{1,0:T(8,128)(2,1)}, u32[]{:S(2)}, u32[]{:S(2)}) collective-permute-start(bf16[256,512]{1,0:T(8,128)(2,1)} %convolution_convert_fusion.1), channel_id=1, source_target_pairs={{0,2},{1,3},{2,0},{3,1},{4,6},{5,7},{6,4},{7,5},{8,10},{9,11},{10,... | collective-permute-start | bytes 786440 | tf_op jit(solution)/shard_map/ppermute | solution.py:89
  124.7 12.4 %collective-permute-start.12 = (bf16[256,512]{1,0:T(8,128)(2,1)}, bf16[256,512]{1,0:T(8,128)(2,1)}, u32[]{:S(2)}, u32[]{:S(2)}) collective-permute-start(bf16[256,512]{1,0:T(8,128)(2,1)} %convolution_convert_fusion), channel_id=1, source_target_pairs={{0,3},{1,0},{2,1},{3,2},{4,7},{5,4},{6,5},{7,6},{8,11},{9,8},{10,9... | collective-permute-start | bytes 786440 | tf_op jit(solution)/shard_map/ppermute | solution.py:89
  130.0 7.2 %copy-start.4 = (bf16[256,512]{1,0:T(8,128)(2,1)S(1)}, bf16[256,512]{1,0:T(8,128)(2,1)}, u32[]{:S(2)}) copy-start(bf16[256,512]{1,0:T(8,128)(2,1)} %param.15) | copy-start | bytes 786436

commit v2 on v1

--- a/solution.py
+++ b/solution.py
@@ -179,16 +179,25 @@
     state_cols = kept_state.shape[3]
     chans = conv_weight.shape[2]
     kernel_len = conv_weight.shape[1]
-    send_state = kept_state[0][send_index]
-    send_conv = kept_conv[0][send_index]
+    slot_count = kept_state.shape[1]
+    send_pick = (send_index[:, None] == jnp.arange(slot_count)[None, :]).astype(jnp.bfloat16)
+
+    def select_rows(picker, rows):
+        picked = jnp.dot(picker, rows.reshape(rows.shape[0], -1), preferred_element_type=jnp.float32)
+        return picked.astype(jnp.bfloat16).reshape((picker.shape[0],) + rows.shape[1:])
+
+    send_state = select_rows(send_pick, kept_state[0])
+    send_conv = select_rows(send_pick, kept_conv[0])
     got_conv = lax.all_to_all(send_conv, "dp", split_axis=0, concat_axis=0, tiled=True)
     got_state = lax.all_to_all(send_state, "dp", split_axis=0, concat_axis=0, tiled=True)
     my_owners = lax.dynamic_index_in_dim(owners, dp_idx, 0, keepdims=False)
     my_rank = lax.dynamic_index_in_dim(owner_rank, dp_idx, 0, keepdims=False)
     recv_row = my_owners * capacity + my_rank
     keep_flag = (window_start > 0).astype(jnp.float32)
-    state_start = got_state[recv_row] * keep_flag.astype(jnp.bfloat16)[:, None, None]
-    conv_start = got_conv[recv_row].astype(jnp.float32) * keep_flag[:, None, None]
+    recv_pick = (recv_row[:, None] == jnp.arange(got_state.shape[0])[None, :]).astype(jnp.float32)
+    recv_pick = (recv_pick * keep_flag[:, None]).astype(jnp.bfloat16)
+    state_start = select_rows(recv_pick, got_state)
+    conv_start = select_rows(recv_pick, got_conv).astype(jnp.float32)
     gain_rotated = rotate_rows(norm_gain[0], shard_width)
     proj_rotated = rotate_rows(in_proj[0], shard_width)
     weight_blocks = column_blocks(out_proj[0])

time: 140 us -> 135 us (0.964)
  matrix products: 42.5 us -> 48.2 us
  other arithmetic: 11.1 us -> 5.73 us
  local copies, waits for them, and re-layouts: 39 us -> 34.2 us
    gather x6 -> x0, local copies, waits for them, and re-layouts: 14.6 us -> none  [the longest x3 9.91 us: per_device(): got_state[recv_row] * keep_flag.astype(jnp.bfloat16)[:, None, None]]
    another operation x0 -> x2, local copies, waits for them, and re-layouts: none -> 6.74 us  [mix_channels(): state_prev.reshape(doc_count, inner, state_width).astype(jnp.float32)]
    unnamed x73 -> x74, local copies, waits for them, and re-layouts: 6 us -> 10.6 us
    dot_general x0 -> x4, matrix products: none -> 2.34 us  [select_rows(): jnp.dot(picker, rows.reshape(rows.shape[0], -1), preferred_element_type=j...]
    another operation x2, other arithmetic: 2.35 us -> 0.11 us  [mix_channels(): cum_decay = jnp.cumsum(-step_size * decay_speed, axis=1)]
    mul x2, other arithmetic: 3.09 us -> 1.01 us  [mix_channels(): activated = jax.nn.silu(conv_out)]
    slice x2, local copies, waits for them, and re-layouts: 2.03 us -> 0.09 us  [mix_channels(): mixed_in = projected[:, :, inner:2 * inner + 2 * state_width]]
    all_to_all x1, waiting for transfers between devices: 0.01 us -> 1.94 us  [per_device(): lax.all_to_all(send_state, 'dp', split_axis=0, concat_axis=0, tiled=True)]
  transfers between devices with their start and end apart: 15 -> 15, of which waited for: 5 -> 5; matrix products, arithmetic and copies ran while one was open for 32% -> 36% of each run, Pallas kernels for 0% -> 0%
where the time goes in v2:
time: 135 us; the launch traced here: 134 us
  matrix products  48.2 us (36%)
  local copies, waits for them, and re-layouts  34.2 us (25%)
  starting transfers between devices  30.2 us (22%)
  waiting for transfers between devices  14.6 us (11%)
  other arithmetic  5.73 us (4%)
    dot_general x2, matrix products, mix_channels(): jnp.einsum('dtsh,dshm->dtm', weights, spread, precision=three_pass)  13.2 us
    ppermute x9, starting transfers between devices, shifted(): lax.ppermute(value, axis, [(source, (source + steps) % count) for source...  12.3 us
    ppermute x9, waiting for transfers between devices, shifted(): lax.ppermute(value, axis, [(source, (source + steps) % count) for source...  11.8 us
    unnamed x74, local copies, waits for them, and re-layouts  10.6 us
    dot_general x8, matrix products, scatter_sum(): jnp.dot(gnormed, weight_block, preferred_element_type=jnp.float32)  10.5 us
    dot_general x2, matrix products, per_device(): jnp.dot(normed, proj_rotated, preferred_element_type=jnp.float32)  9.88 us
    ppermute x4, starting transfers between devices, gather_from_behind(): parts.append(lax.ppermute(value, ('section', 'mp'), pairs))  7.77 us
    convert_element_type x2, local copies, waits for them, and re-layouts, mix_channels(): end_state.reshape(doc_count, head_count, head_dim * state_width)  7.02 us
  transfers between devices with their start and end apart: 15, of which 5 were waited for; matrix products, arithmetic and copies ran while one was open for 36% of the time, Pallas kernels for 0%

profile of v2, /device:TPU:0, one launch (start us, length us, event | category | flops | bytes accessed | tf_op | source)
XLA Modules:
  0.0 134.1 jit_solution(9684820473524434071)
XLA Ops:
  0.6 3.9 %collective-permute-start = (bf16[256,512]{1,0:T(8,128)(2,1)}, bf16[256,512]{1,0:T(8,128)(2,1)}, u32[]{:S(2)}, u32[]{:S(2)}) collective-permute-start(bf16[256,512]{1,0:T(8,128)(2,1)} %param.15), channel_id=1, source_target_pairs={{0,3},{1,0},{2,1},{3,2},{4,7},{5,4},{6,5},{7,6},{8,11},{9,8},{10,9... | collective-permute-start | bytes 786440 | tf_op jit(solution)/shard_map/ppermute | solution.py:89
  5.7 0.9 copy.60
  6.6 0.7 broadcast_in_dim.40
  7.3 0.7 reshape.217
  8.7 0.7 reshape.218
  9.4 4.9 %all-to-all-start = ((bf16[16,3,640]{2,1,0:T(4,128)(2,1)}), bf16[16,3,640]{2,1,0:T(4,128)(2,1)S(1)}, u32[]{:S(2)}, u32[]{:S(2)}) async-start(bf16[16,3,640]{2,1,0:T(4,128)(2,1)} %reshape.218), calls=%async_computation | async-start | bytes 163840 | tf_op jit(solution)/shard_map/all_to_all | solution.py:191
  14.9 0.7 compare_convert_fusion
  15.5 0.9 slice_reduce_fusion.3
  16.4 0.6 fusion.126
  17.1 1.8 %copy.83 = bf16[2,8,16,2048]{3,1,2,0:T(8,128)(2,1)S(1)} copy(bf16[2,8,16,2048]{3,2,1,0:T(8,128)(2,1)} %bitcast.95) | data formatting | bytes 2097152
  19.6 0.7 mul.331
  20.3 1.5 %copy.84 = bf16[2,8,16,2048]{3,2,1,0:T(8,128)(2,1)} copy(bf16[2,8,16,2048]{3,1,2,0:T(8,128)(2,1)S(1)} %bitcast.91) | data formatting | bytes 2097152
  21.9 5.2 %all-to-all-start.1 = ((bf16[16,16,2048]{2,1,0:T(8,128)(2,1)}), bf16[16,16,2048]{2,1,0:T(8,128)(2,1)}, u32[]{:S(2)}, u32[]{:S(2)}) async-start(bf16[16,16,2048]{2,1,0:T(8,128)(2,1)} %bitcast.93), calls=%async_computation.1 | async-start | bytes 2097152 | tf_op jit(solution)/shard_map/all_to_all | solution.py:192
  27.4 0.7 reshape.225
  28.1 1.0 constant_dynamic-update-slice_fusion.3
  29.1 1.0 constant_dynamic-update-slice_fusion.2
  30.1 1.0 constant_dynamic-update-slice_fusion.1
  31.4 4.7 %fusion.47 = f32[256,1168]{1,0:T(8,128)S(1)} fusion(bf16[256,2048]{1,0:T(8,128)(2,1)S(1)} %constant_dynamic-update-slice_fusion, f32[2048]{0:T(1024)S(1)} %fusion.134, f32[256]{0:T(256)S(1)} %add_rsqrt_fusion.3, s32[]{:T(128)S(6)} %select_n.101, bf16[2048,1168]{0,1:T(8,128)(2,1)} %bitcast.115), kind=kOutput, calls=%fused_computation.66 | convolution fusion | flops 1236402176 | bytes 7037956 | tf_op jit(solution)/shard_map/dot_general | solution.py:217
  36.8 0.8 copy-done.3
  37.6 0.9 slice.115
  38.6 0.8 copy.61
  39.4 0.8 copy.58
  40.2 1.3 fusion.102
  41.5 1.2 fusion.111
  42.6 7.0 %fusion.32 = f32[16,16,512]{2,1,0:T(8,128)} fusion(f32[16,512]{1,0:T(8,128)} %fusion.126, f32[16,16,512]{2,1,0:T(8,128)} %slice.115, f32[16,16,16]{1,2,0:T(8,128)} %copy.61, f32[16,16,16]{2,1,0:T(8,128)S(1)} %fusion.102, f32[16,16,16]{1,2,0:T(8,128)} %copy.58, pred[16,16]{1,0:T(8,128)(4,1)} %iota_compare_fusion.8), kind=kOutput, calls=%fused_computation.48 | convolution fusion | flops 203685888 | bytes 1130752 | tf_op jit(solution)/shard_map/dtsh,dshm->dtm/dot_general | solution.py:68
  49.6 1.9 %all-to-all-done.1 = bf16[16,16,2048]{2,1,0:T(8,128)(2,1)} async-done(((bf16[16,16,2048]{2,1,0:T(8,128)(2,1)}), bf16[16,16,2048]{2,1,0:T(8,128)(2,1)}, u32[]{:S(2)}, u32[]{:S(2)}) %all-to-all-start.1) | async-done | bytes 1048608 | tf_op jit(solution)/shard_map/all_to_all | solution.py:192
  51.6 1.8 %copy.85 = bf16[2,8,16,2048]{3,1,2,0:T(8,128)(2,1)S(1)} copy(bf16[2,8,16,2048]{3,2,1,0:T(8,128)(2,1)} %bitcast.33) | data formatting | bytes 2097152
  53.4 1.4 %convolution_convert_fusion = bf16[16,32768]{1,0:T(8,128)(2,1)} fusion(bf16[16,32768]{1,0:T(8,128)(2,1)S(1)} %bitcast.94, bf16[16]{0:T(256)(128)(2,1)S(1)} %copy-done.30, s32[16]{0:T(128)S(1)} %copy-done.20), kind=kOutput, calls=%fused_computation | convolution fusion | flops 17302016 | bytes 2097248 | tf_op jit(solution)/shard_map/dot_general | solution.py:186
  54.8 4.1 %reshape_reshape.4 = bf16[16,512,64]{2,1,0:T(8,128)(2,1)} reshape(bf16[16,32768]{1,0:T(8,128)(2,1)} %convolution_convert_fusion) | data formatting | bytes 2097152 | tf_op jit(solution)/shard_map/reshape;reshape | solution.py:69
  58.9 3.5 %multiply_reduce_fusion.1 = (f32[16,16]{1,0:T(8,128)S(1)}, f32[16,16,512]{2,1,0:T(8,128)S(1)}) fusion(f32[16,16,1168]{2,1,0:T(8,128)} %bitcast.102, f32[16,16,640]{2,1,0:T(8,128)} %copy-done.3, f32[512]{0:T(512)S(1)} %copy-done.26, f32[16,16,512]{2,1,0:T(8,128)} %fusion.32, f32[16,16,512]{2,1,0:T(8,128)} %fusion.111, bf16[16,512,64]{2,1,0:T(8,128)(2,1)} %reshape_reshape.4), kind=kOutput, calls=%fused_computation.119 | convolution fusion | flops 51773184 | bytes 3804160 | tf_op jit(solution)/shard_map/dtn,dmn->dtm/dot_general | solution.py:70
  62.6 1.0 convolution_convert_fusion.8
  63.6 2.3 %collective-permute-start.5 = (bf16[256,512]{1,0:T(8,128)(2,1)}, bf16[256,512]{1,0:T(8,128)(2,1)}, u32[]{:S(2)}, u32[]{:S(2)}) collective-permute-start(bf16[256,512]{1,0:T(8,128)(2,1)} %convolution_convert_fusion.8), channel_id=1, source_target_pairs={{0,3},{1,0},{2,1},{3,2},{4,7},{5,4},{6,5},{7,6},{8,11},{9,8},{10,9... | collective-permute-start | bytes 786440 | tf_op jit(solution)/shard_map/ppermute | solution.py:89
  65.9 1.0 convolution_convert_fusion.9
  66.9 1.5 %collective-permute-start.4 = (bf16[256,512]{1,0:T(8,128)(2,1)}, bf16[256,512]{1,0:T(8,128)(2,1)}, u32[]{:S(2)}, u32[]{:S(2)}) collective-permute-start(bf16[256,512]{1,0:T(8,128)(2,1)} %convolution_convert_fusion.9), channel_id=1, source_target_pairs={{0,2},{1,3},{2,0},{3,1},{4,6},{5,7},{6,4},{7,5},{8,10},{9,11},{10,... | collective-permute-start | bytes 786440 | tf_op jit(solution)/shard_map/ppermute | solution.py:89
  68.5 1.0 convolution_convert_fusion.10
  69.5 3.6 %collective-permute-done.5 = bf16[256,512]{1,0:T(8,128)(2,1)} collective-permute-done((bf16[256,512]{1,0:T(8,128)(2,1)}, bf16[256,512]{1,0:T(8,128)(2,1)}, u32[]{:S(2)}, u32[]{:S(2)}) %collective-permute-start.5) | collective-permute-done | bytes 262176 | tf_op jit(solution)/shard_map/ppermute | solution.py:89
  73.0 6.8 %collective-permute-done.4 = bf16[256,512]{1,0:T(8,128)(2,1)} collective-permute-done((bf16[256,512]{1,0:T(8,128)(2,1)}, bf16[256,512]{1,0:T(8,128)(2,1)}, u32[]{:S(2)}, u32[]{:S(2)}) %collective-permute-start.4) | collective-permute-done | bytes 262176 | tf_op jit(solution)/shard_map/ppermute | solution.py:89
  79.8 2.3 %add_convert_fusion.2 = bf16[256,512]{1,0:T(8,128)(2,1)} fusion(bf16[256,512]{1,0:T(8,128)(2,1)} %collective-permute-done.5, bf16[256,512]{1,0:T(8,128)(2,1)} %collective-permute-done.4, bf16[256,512]{1,0:T(8,128)(2,1)} %collective-permute-done.3, bf16[256,512]{1,0:T(8,128)(2,1)S(1)} %bitcast.86, bf16[256,512]{1,0:T(8,128)(2,1)} %param.15, ...), kind=kOutput, calls=%fused_computation.117 | convolution fusion | flops 135659520 | bytes 2097156 | tf_op jit(solution)/shard_map/dot_general | solution.py:135
  82.1 1.3 collective-permute-start.6
  83.4 2.5 %collective-permute-start.9 = (bf16[256,512]{1,0:T(8,128)(2,1)}, bf16[256,512]{1,0:T(8,128)(2,1)}, u32[]{:S(2)}, u32[]{:S(2)}) collective-permute-start(bf16[256,512]{1,0:T(8,128)(2,1)} %add_convert_fusion.2), channel_id=1, source_target_pairs={{0,17},{1,18},{2,19},{3,16},{4,21},{5,22},{6,23},{7,20},{8,25},{9,... | collective-permute-start | bytes 786440 | tf_op jit(solution)/shard_map/ppermute | solution.py:117
  85.9 2.0 %collective-permute-start.8 = (bf16[256,512]{1,0:T(8,128)(2,1)}, bf16[256,512]{1,0:T(8,128)(2,1)}, u32[]{:S(2)}, u32[]{:S(2)}) collective-permute-start(bf16[256,512]{1,0:T(8,128)(2,1)} %add_convert_fusion.2), channel_id=1, source_target_pairs={{0,18},{1,19},{2,16},{3,17},{4,22},{5,23},{6,20},{7,21},{8,26},{9,... | collective-permute-start | bytes 786440 | tf_op jit(solution)/shard_map/ppermute | solution.py:117
  87.9 2.0 %collective-permute-start.7 = (bf16[256,512]{1,0:T(8,128)(2,1)}, bf16[256,512]{1,0:T(8,128)(2,1)}, u32[]{:S(2)}, u32[]{:S(2)}) collective-permute-start(bf16[256,512]{1,0:T(8,128)(2,1)} %add_convert_fusion.2), channel_id=1, source_target_pairs={{0,19},{1,16},{2,17},{3,18},{4,23},{5,20},{6,21},{7,22},{8,27},{9,... | collective-permute-start | bytes 786440 | tf_op jit(solution)/shard_map/ppermute | solution.py:117
  89.9 2.7 %copy.71 = bf16[16,512,64]{1,2,0:T(8,128)(2,1)} copy(bf16[16,512,64]{2,1,0:T(8,128)(2,1)} %reshape_reshape.4) | data formatting | bytes 2097152 | tf_op jit(solution)/shard_map/reshape;reshape | solution.py:69
  92.6 0.8 collective-permute-done.7
  93.4 1.5 %fusion.13 = f32[256]{0:T(256)S(1)} fusion(bf16[256,2048]{1,0:T(8,128)(2,1)S(1)} %constant_dynamic-update-slice_fusion, bf16[256,512]{1,0:T(8,128)(2,1)S(1)} %collective-permute-done.6, bf16[256,512]{1,0:T(8,128)(2,1)} %collective-permute-done.9, bf16[256,512]{1,0:T(8,128)(2,1)} %collective-permute-done.8, bf16[256,512]{1,0:T(8,128)(2,1)} %collective-permute-done.7, ...), kind=kLoop, calls=%fused_computation.23 | loop fusion | flops 6291200 | bytes 2098177 | tf_op jit(solution)/shard_map/reduce_sum | solution.py:18
  95.0 5.1 %fusion.45 = f32[256,1168]{1,0:T(8,128)S(1)} fusion(f32[256]{0:T(256)S(1)} %add_rsqrt_fusion.2, f32[2048]{0:T(1024)S(1)} %copy-done.18, bf16[256,2048]{1,0:T(8,128)(2,1)S(1)} %constant_dynamic-update-slice_fusion, bf16[256,512]{1,0:T(8,128)(2,1)S(1)} %collective-permute-done.6, bf16[256,512]{1,0:T(8,128)(2,1)} %collective-permute-done.9, ...), kind=kOutput, calls=%fused_computation.65 | convolution fusion | flops 1241120768 | bytes 8086533 | tf_op jit(solution)/shard_map/dot_general | solution.py:217
  100.8 0.9 slice.125
  101.7 0.9 fusion.116
  102.6 0.8 copy.68
  104.0 6.2 %fusion.37 = f32[16,16,512]{2,1,0:T(8,128)S(1)} fusion(f32[16,16,512]{2,1,0:T(8,128)} %slice.125, f32[16,512]{1,0:T(8,128)} %fusion.126, f32[16,16,16]{1,2,0:T(8,128)} %copy.68, f32[16,16,16]{2,1,0:T(8,128)} %fusion.116, f32[16,16,16]{1,2,0:T(8,128)S(1)} %copy.66, pred[16,16]{1,0:T(8,128)(4,1)S(1)} %copy-done.28), kind=kOutput, calls=%fused_computation.49 | convolution fusion | flops 203685888 | bytes 1130752 | tf_op jit(solution)/shard_map/dtsh,dshm->dtm/dot_general | solution.py:68
  110.2 2.4 %multiply_reduce_fusion = (f32[16,16]{1,0:T(8,128)S(1)}, f32[16,16,512]{2,1,0:T(8,128)S(1)}) fusion(f32[16,16,1168]{2,1,0:T(8,128)} %bitcast.98, f32[16,16,640]{2,1,0:T(8,128)S(1)} %divide_multiply_fusion, f32[512]{0:T(512)S(1)} %copy-done.27, f32[16,16,512]{2,1,0:T(8,128)S(1)} %fusion.37, f32[16,16,512]{2,1,0:T(8,128)S(1)} %fusion.107, ...), kind=kOutput, calls=%fused_computation.116 | convolution fusion | flops 51773184 | bytes 3804160 | tf_op jit(solution)/shard_map/dtn,dmn->dtm/dot_general | solution.py:70
  112.8 1.0 convolution_convert_fusion.4
  113.8 1.0 convolution_convert_fusion.5
  114.8 1.0 convolution_convert_fusion.6
  115.9 1.1 collective-permute-start.12
  117.0 1.3 collective-permute-start.11
  118.3 1.0 collective-permute-start.10
  119.7 2.1 %add_convert_fusion = bf16[16,512,64]{1,2,0:T(8,128)(2,1)} fusion(bf16[16,512,64]{1,2,0:T(8,128)(2,1)S(1)} %copy-done.2, f32[16,16,512]{2,1,0:T(8,128)S(1)} %convolution_multiply_fusion, f32[16,512]{1,0:T(8,128)S(1)} %fusion.124, f32[16,16,640]{2,1,0:T(8,128)S(1)} %divide_multiply_fusion), kind=kOutput, calls=%fused_computation.26 | convolution fusion | flops 52428800 | bytes 2785280 | tf_op jit(solution)/shard_map/dsm,dsn->dmn/dot_general | solution.py:76
  121.8 2.7 %copy.73 = bf16[16,512,64]{2,1,0:T(8,128)(2,1)} copy(bf16[16,512,64]{1,2,0:T(8,128)(2,1)} %add_convert_fusion) | data formatting | bytes 2097152 | tf_op jit(solution)/shard_map/convert_element_type | solution.py:81
  124.6 4.3 %convert_element_type.173 = bf16[1,16,16,2048]{3,2,1,0:T(8,128)(2,1)} reshape(bf16[16,512,64]{2,1,0:T(8,128)(2,1)} %copy.73) | data formatting | bytes 2097152 | tf_op jit(solution)/shard_map/convert_element_type | solution.py:81
  128.8 1.0 fusion.122
  129.8 0.6 copy.74
  130.5 1.4 %collective-permute-done.10 = bf16[256,512]{1,0:T(8,128)(2,1)} collective-permute-done((bf16[256,512]{1,0:T(8,128)(2,1)}, bf16[256,512]{1,0:T(8,128)(2,1)}, u32[]{:S(2)}, u32[]{:S(2)}) %collective-permute-start.10) | collective-permute-done | bytes 262176 | tf_op jit(solution)/shard_map/ppermute | solution.py:89
  131.9 2.2 %fusion.101 = bf16[1,256,512]{2,1,0:T(8,128)(2,1)} fusion(bf16[256,512]{1,0:T(8,128)(2,1)} %collective-permute-done.12, bf16[256,512]{1,0:T(8,128)(2,1)} %collective-permute-done.11, bf16[256,512]{1,0:T(8,128)(2,1)} %collective-permute-done.10, bf16[256,512]{1,0:T(8,128)(2,1)S(1)} %copy-done.5, bf16[256,512]{1,0:T(8,128)(2,1)S(1)} %collective-permute-done.6, ...), kind=kOutput, calls=%fused_computation.130 | convolution fusion | flops 135790592 | bytes 2359301 | tf_op jit(solution)/shard_map/dot_general | solution.py:135
  (113 shorter events, 6.4 us)
Async XLA Ops:
  0.6 61.9 %copy-start = (bf16[1,512,2048]{2,1,0:T(8,128)(2,1)S(1)}, bf16[1,512,2048]{2,1,0:T(8,128)(2,1)}, u32[]{:S(2)}) copy-start(bf16[1,512,2048]{2,1,0:T(8,128)(2,1)} %param.24) | copy-start | bytes 6291460
  0.6 27.4 %collective-permute-start = (bf16[256,512]{1,0:T(8,128)(2,1)}, bf16[256,512]{1,0:T(8,128)(2,1)}, u32[]{:S(2)}, u32[]{:S(2)}) collective-permute-start(bf16[256,512]{1,0:T(8,128)(2,1)} %param.15), channel_id=1, source_target_pairs={{0,3},{1,0},{2,1},{3,2},{4,7},{5,4},{6,5},{7,6},{8,11},{9,8},{10,9... | collective-permute-start | bytes 786440 | tf_op jit(solution)/shard_map/ppermute | solution.py:89
  4.6 24.5 %collective-permute-start.1 = (bf16[256,512]{1,0:T(8,128)(2,1)}, bf16[256,512]{1,0:T(8,128)(2,1)}, u32[]{:S(2)}, u32[]{:S(2)}) collective-permute-start(bf16[256,512]{1,0:T(8,128)(2,1)} %param.15), channel_id=1, source_target_pairs={{0,2},{1,3},{2,0},{3,1},{4,6},{5,7},{6,4},{7,5},{8,10},{9,11},{10,... | collective-permute-start | bytes 786440 | tf_op jit(solution)/shard_map/ppermute | solution.py:89
  5.1 25.0 %collective-permute-start.2 = (bf16[256,512]{1,0:T(8,128)(2,1)}, bf16[256,512]{1,0:T(8,128)(2,1)}, u32[]{:S(2)}, u32[]{:S(2)}) collective-permute-start(bf16[256,512]{1,0:T(8,128)(2,1)} %param.15), channel_id=1, source_target_pairs={{0,1},{1,2},{2,3},{3,0},{4,5},{5,6},{6,7},{7,4},{8,9},{9,10},{10,1... | collective-permute-start | bytes 786440 | tf_op jit(solution)/shard_map/ppermute | solution.py:89
  9.4 12.5 %all-to-all-start = ((bf16[16,3,640]{2,1,0:T(4,128)(2,1)}), bf16[16,3,640]{2,1,0:T(4,128)(2,1)S(1)}, u32[]{:S(2)}, u32[]{:S(2)}) async-start(bf16[16,3,640]{2,1,0:T(4,128)(2,1)} %reshape.218), calls=%async_computation | async-start | bytes 163840 | tf_op jit(solution)/shard_map/all_to_all | solution.py:191
  15.5 11.6 %copy-start.29 = (bf16[16]{0:T(256)(128)(2,1)}, bf16[16]{0:T(256)(128)(2,1)S(1)}, u32[]{:S(2)}) copy-start(bf16[16]{0:T(256)(128)(2,1)S(1)} %compare_convert_fusion) | copy-start | bytes 100
  16.4 19.8 %copy-start.10 = (f32[640]{0:T(1024)}, f32[640]{0:T(1024)S(1)}, u32[]{:S(2)}) copy-start(f32[640]{0:T(1024)S(1)} %get-tuple-element.14) | copy-start | bytes 7684
  16.4 19.8 %copy-start.12 = (f32[640]{0:T(1024)}, f32[640]{0:T(1024)S(1)}, u32[]{:S(2)}) copy-start(f32[640]{0:T(1024)S(1)} %get-tuple-element.15) | copy-start | bytes 7684
  17.1 2.3 %copy-start.16 = (f32[1,2048]{1,0:T(1,128)S(1)}, f32[1,2048]{1,0:T(1,128)}, u32[]{:S(2)}) copy-start(f32[1,2048]{1,0:T(1,128)} %param.16) | copy-start | bytes 24580
  17.1 2.5 %copy-start.31 = (f32[1,16]{1,0:T(1,128)S(1)}, f32[1,16]{1,0:T(1,128)}, u32[]{:S(2)}) copy-start(f32[1,16]{1,0:T(1,128)} %param.22) | copy-start | bytes 196
  18.9 3.0 %copy-start.21 = (f32[1,640]{1,0:T(1,128)S(1)}, f32[1,640]{1,0:T(1,128)}, u32[]{:S(2)}) copy-start(f32[1,640]{1,0:T(1,128)} %param.19) | copy-start | bytes 7684
  19.5 11.9 %copy-start.17 = (f32[2048]{0:T(1024)}, f32[2048]{0:T(1024)S(1)}, u32[]{:S(2)}) copy-start(f32[2048]{0:T(1024)S(1)} %fusion.134) | copy-start | bytes 24580
  19.5 7.7 %copy-start.19 = (s32[16]{0:T(128)}, s32[16]{0:T(128)S(1)}, u32[]{:S(2)}) copy-start(s32[16]{0:T(128)S(1)} %fusion.160) | copy-start | bytes 196
  21.9 9.2 %copy-start.4 = (bf16[256,512]{1,0:T(8,128)(2,1)S(1)}, bf16[256,512]{1,0:T(8,128)(2,1)}, u32[]{:S(2)}) copy-start(bf16[256,512]{1,0:T(8,128)(2,1)} %param.15) | copy-start | bytes 786436
  21.9 29.7 %all-to-all-start.1 = ((bf16[16,16,2048]{2,1,0:T(8,128)(2,1)}), bf16[16,16,2048]{2,1,0:T(8,128)(2,1)}, u32[]{:S(2)}, u32[]{:S(2)}) async-start(bf16[16,16,2048]{2,1,0:T(8,128)(2,1)} %bitcast.93), calls=%async_computation.1 | async-start | bytes 2097152 | tf_op jit(solution)/shard_map/all_to_all | solution.py:192
  31.4 4.9 %copy-start.6 = (f32[16,3,640]{2,1,0:T(4,128)S(1)}, f32[16,3,640]{2,1,0:T(4,128)}, u32[]{:S(2)}) copy-start(f32[16,3,640]{2,1,0:T(4,128)} %reshape.225) | copy-start | bytes 368644
  36.2 2.4 %copy-start.9 = (f32[256,1168]{1,0:T(8,128)}, f32[256,1168]{1,0:T(8,128)S(1)}, u32[]{:S(2)}) copy-start(f32[256,1168]{1,0:T(8,128)S(1)} %fusion.47) | copy-start | bytes 3588100
  36.2 2.3 %copy-start.22 = (f32[1,16]{1,0:T(1,128)S(1)}, f32[1,16]{1,0:T(1,128)}, u32[]{:S(2)}) copy-start(f32[1,16]{1,0:T(1,128)} %param.21) | copy-start | bytes 196
  36.2 2.3 %copy-start.24 = (f32[1,16]{1,0:T(1,128)S(1)}, f32[1,16]{1,0:T(1,128)}, u32[]{:S(2)}) copy-start(f32[1,16]{1,0:T(1,128)} %param.20) | copy-start | bytes 196
  36.8 0.8 copy-start.3
  49.6 3.8 %copy-start.20 = (s32[16]{0:T(128)S(1)}, s32[16]{0:T(128)}, u32[]{:S(2)}) copy-start(s32[16]{0:T(128)} %copy-done.19) | copy-start | bytes 196
  49.6 3.8 %copy-start.30 = (bf16[16]{0:T(256)(128)(2,1)S(1)}, bf16[16]{0:T(256)(128)(2,1)}, u32[]{:S(2)}) copy-start(bf16[16]{0:T(256)(128)(2,1)} %copy-done.29) | copy-start | bytes 100
  54.8 4.1 %copy-start.26 = (f32[512]{0:T(512)S(1)}, f32[512]{0:T(512)}, u32[]{:S(2)}) copy-start(f32[512]{0:T(512)} %mul.331) | copy-start | bytes 6148
  58.9 3.6 %copy-start.14 = (f32[1,512]{1,0:T(1,128)S(1)}, f32[1,512]{1,0:T(1,128)}, u32[]{:S(2)}) copy-start(f32[1,512]{1,0:T(1,128)} %param.23) | copy-start | bytes 6148
  63.6 9.4 %collective-permute-start.5 = (bf16[256,512]{1,0:T(8,128)(2,1)}, bf16[256,512]{1,0:T(8,128)(2,1)}, u32[]{:S(2)}, u32[]{:S(2)}) collective-permute-start(bf16[256,512]{1,0:T(8,128)(2,1)} %convolution_convert_fusion.8), channel_id=1, source_target_pairs={{0,3},{1,0},{2,1},{3,2},{4,7},{5,4},{6,5},{7,6},{8,11},{9,8},{10,9... | collective-permute-start | bytes 786440 | tf_op jit(solution)/shard_map/ppermute | solution.py:89
  66.9 12.9 %collective-permute-start.4 = (bf16[256,512]{1,0:T(8,128)(2,1)}, bf16[256,512]{1,0:T(8,128)(2,1)}, u32[]{:S(2)}, u32[]{:S(2)}) collective-permute-start(bf16[256,512]{1,0:T(8,128)(2,1)} %convolution_convert_fusion.9), channel_id=1, source_target_pairs={{0,2},{1,3},{2,0},{3,1},{4,6},{5,7},{6,4},{7,5},{8,10},{9,11},{10,... | collective-permute-start | bytes 786440 | tf_op jit(solution)/shard_map/ppermute | solution.py:89
  69.5 10.4 %collective-permute-start.3 = (bf16[256,512]{1,0:T(8,128)(2,1)}, bf16[256,512]{1,0:T(8,128)(2,1)}, u32[]{:S(2)}, u32[]{:S(2)}) collective-permute-start(bf16[256,512]{1,0:T(8,128)(2,1)} %convolution_convert_fusion.10), channel_id=1, source_target_pairs={{0,1},{1,2},{2,3},{3,0},{4,5},{5,6},{6,7},{7,4},{8,9},{9,10},{10,1... | collective-permute-start | bytes 786440 | tf_op jit(solution)/shard_map/ppermute | solution.py:89
  82.1 10.5 %collective-permute-start.6 = (bf16[256,512]{1,0:T(8,128)(2,1)}, bf16[256,512]{1,0:T(8,128)(2,1)S(1)}, u32[]{:S(2)}, u32[]{:S(2)}) collective-permute-start(bf16[256,512]{1,0:T(8,128)(2,1)} %add_convert_fusion.2), channel_id=1, source_target_pairs={{0,16},{1,17},{2,18},{3,19},{4,20},{5,21},{6,22},{7,23},{8,24},{9,... | collective-permute-start | bytes 786440 | tf_op jit(solution)/shard_map/ppermute | solution.py:117
  83.4 9.2 %collective-permute-start.9 = (bf16[256,512]{1,0:T(8,128)(2,1)}, bf16[256,512]{1,0:T(8,128)(2,1)}, u32[]{:S(2)}, u32[]{:S(2)}) collective-permute-start(bf16[256,512]{1,0:T(8,128)(2,1)} %add_convert_fusion.2), channel_id=1, source_target_pairs={{0,17},{1,18},{2,19},{3,16},{4,21},{5,22},{6,23},{7,20},{8,25},{9,... | collective-permute-start | bytes 786440 | tf_op jit(solution)/shard_map/ppermute | solution.py:117
  85.9 6.7 %collective-permute-start.8 = (bf16[256,512]{1,0:T(8,128)(2,1)}, bf16[256,512]{1,0:T(8,128)(2,1)}, u32[]{:S(2)}, u32[]{:S(2)}) collective-permute-start(bf16[256,512]{1,0:T(8,128)(2,1)} %add_convert_fusion.2), channel_id=1, source_target_pairs={{0,18},{1,19},{2,16},{3,17},{4,22},{5,23},{6,20},{7,21},{8,26},{9,... | collective-permute-start | bytes 786440 | tf_op jit(solution)/shard_map/ppermute | solution.py:117
  87.9 5.5 %collective-permute-start.7 = (bf16[256,512]{1,0:T(8,128)(2,1)}, bf16[256,512]{1,0:T(8,128)(2,1)}, u32[]{:S(2)}, u32[]{:S(2)}) collective-permute-start(bf16[256,512]{1,0:T(8,128)(2,1)} %add_convert_fusion.2), channel_id=1, source_target_pairs={{0,19},{1,16},{2,17},{3,18},{4,23},{5,20},{6,21},{7,22},{8,27},{9,... | collective-permute-start | bytes 786440 | tf_op jit(solution)/shard_map/ppermute | solution.py:117
  89.9 5.0 %copy-start.18 = (f32[2048]{0:T(1024)S(1)}, f32[2048]{0:T(1024)}, u32[]{:S(2)}) copy-start(f32[2048]{0:T(1024)} %copy-done.17) | copy-start | bytes 24580
  94.9 5.3 %copy-start.23 = (f32[1,16]{1,0:T(1,128)S(1)}, f32[1,16]{1,0:T(1,128)}, u32[]{:S(2)}) copy-start(f32[1,16]{1,0:T(1,128)} %param.21) | copy-start | bytes 196
  94.9 5.3 %copy-start.25 = (f32[1,16]{1,0:T(1,128)S(1)}, f32[1,16]{1,0:T(1,128)}, u32[]{:S(2)}) copy-start(f32[1,16]{1,0:T(1,128)} %param.20) | copy-start | bytes 196
  94.9 5.4 %copy-start.7 = (f32[16,3,640]{2,1,0:T(4,128)S(1)}, f32[16,3,640]{2,1,0:T(4,128)}, u32[]{:S(2)}) copy-start(f32[16,3,640]{2,1,0:T(4,128)} %reshape.225) | copy-start | bytes 368644
  95.0 5.4 %copy-start.11 = (f32[640]{0:T(1024)S(1)}, f32[640]{0:T(1024)}, u32[]{:S(2)}) copy-start(f32[640]{0:T(1024)} %copy-done.10) | copy-start | bytes 7684
  95.0 5.4 %copy-start.13 = (f32[640]{0:T(1024)S(1)}, f32[640]{0:T(1024)}, u32[]{:S(2)}) copy-start(f32[640]{0:T(1024)} %copy-done.12) | copy-start | bytes 7684
  100.1 1.6 %copy-start.8 = (f32[256,1168]{1,0:T(8,128)}, f32[256,1168]{1,0:T(8,128)S(1)}, u32[]{:S(2)}) copy-start(f32[256,1168]{1,0:T(8,128)S(1)} %fusion.45) | copy-start | bytes 3588100
  100.8 3.1 %copy-start.28 = (pred[16,16]{1,0:T(8,128)(4,1)S(1)}, pred[16,16]{1,0:T(8,128)(4,1)}, u32[]{:S(2)}) copy-start(pred[16,16]{1,0:T(8,128)(4,1)} %iota_compare_fusion.8) | copy-start | bytes 772
  103.9 6.3 %copy-start.1 = (bf16[16,512,64]{2,1,0:T(8,128)(2,1)S(1)}, bf16[16,512,64]{2,1,0:T(8,128)(2,1)}, u32[]{:S(2)}) copy-start(bf16[16,512,64]{2,1,0:T(8,128)(2,1)} %reshape_reshape.4) | copy-start | bytes 3145732
  104.0 6.2 %copy-start.27 = (f32[512]{0:T(512)S(1)}, f32[512]{0:T(512)}, u32[]{:S(2)}) copy-start(f32[512]{0:T(512)} %mul.331) | copy-start | bytes 6148
  110.2 2.4 %copy-start.15 = (f32[1,512]{1,0:T(1,128)S(1)}, f32[1,512]{1,0:T(1,128)}, u32[]{:S(2)}) copy-start(f32[1,512]{1,0:T(1,128)} %param.23) | copy-start | bytes 6148
  112.7 7.0 %copy-start.2 = (bf16[16,512,64]{1,2,0:T(8,128)(2,1)S(1)}, bf16[16,512,64]{1,2,0:T(8,128)(2,1)}, u32[]{:S(2)}) copy-start(bf16[16,512,64]{1,2,0:T(8,128)(2,1)} %copy.71) | copy-start | bytes 3145732
  115.9 14.6 %collective-permute-start.12 = (bf16[256,512]{1,0:T(8,128)(2,1)}, bf16[256,512]{1,0:T(8,128)(2,1)}, u32[]{:S(2)}, u32[]{:S(2)}) collective-permute-start(bf16[256,512]{1,0:T(8,128)(2,1)} %convolution_convert_fusion.4), channel_id=1, source_target_pairs={{0,3},{1,0},{2,1},{3,2},{4,7},{5,4},{6,5},{7,6},{8,11},{9,8},{10,9... | collective-permute-start | bytes 786440 | tf_op jit(solution)/shard_map/ppermute | solution.py:89
  117.0 13.5 %collective-permute-start.11 = (bf16[256,512]{1,0:T(8,128)(2,1)}, bf16[256,512]{1,0:T(8,128)(2,1)}, u32[]{:S(2)}, u32[]{:S(2)}) collective-permute-start(bf16[256,512]{1,0:T(8,128)(2,1)} %convolution_convert_fusion.5), channel_id=1, source_target_pairs={{0,2},{1,3},{2,0},{3,1},{4,6},{5,7},{6,4},{7,5},{8,10},{9,11},{10,... | collective-permute-start | bytes 786440 | tf_op jit(solution)/shard_map/ppermute | solution.py:89
  118.3 13.6 %collective-permute-start.10 = (bf16[256,512]{1,0:T(8,128)(2,1)}, bf16[256,512]{1,0:T(8,128)(2,1)}, u32[]{:S(2)}, u32[]{:S(2)}) collective-permute-start(bf16[256,512]{1,0:T(8,128)(2,1)} %convolution_convert_fusion.6), channel_id=1, source_target_pairs={{0,1},{1,2},{2,3},{3,0},{4,5},{5,6},{6,7},{7,4},{8,9},{9,10},{10,1... | collective-permute-start | bytes 786440 | tf_op jit(solution)/shard_map/ppermute | solution.py:89
  124.6 7.4 %copy-start.5 = (bf16[256,512]{1,0:T(8,128)(2,1)S(1)}, bf16[256,512]{1,0:T(8,128)(2,1)}, u32[]{:S(2)}) copy-start(bf16[256,512]{1,0:T(8,128)(2,1)} %param.15) | copy-start | bytes 786436

commit v3 on v2

--- a/solution.py
+++ b/solution.py
@@ -6,6 +6,7 @@
 epsilon = 1e-05
 highest = lax.Precision.HIGHEST
 three_pass = lax.Precision.HIGH
+one_pass = lax.Precision.DEFAULT
 
 
 def from_behind(value, axis, steps):
@@ -65,9 +66,9 @@
     scores = jnp.einsum("dtn,dsn->dts", query_proj, key_proj, precision=three_pass)
     weights = decay * scores[:, :, :, None] * step_size[:, None, :, :]
     spread = chan_vals[:, :, None, :] * expander[None, None, :, :]
-    mixed_out = jnp.einsum("dtsh,dshm->dtm", weights, spread, precision=three_pass)
+    mixed_out = jnp.einsum("dtsh,dshm->dtm", weights, spread, precision=one_pass)
     start_state = state_prev.reshape(doc_count, inner, state_width).astype(jnp.float32)
-    carried = jnp.einsum("dtn,dmn->dtm", query_proj, start_state, precision=three_pass)
+    carried = jnp.einsum("dtn,dmn->dtm", query_proj, start_state, precision=one_pass)
     mixed_out = mixed_out + expand(jnp.exp(cum_decay)) * carried
     mixed_out = mixed_out + jnp.repeat(skip_weight, head_dim)[None, None, :] * chan_vals
     tail_weight = jnp.exp(cum_decay[:, -1:, :] - cum_decay) * step_size

time: 135 us -> 131 us (0.970)
  matrix products: 48.2 us -> 40.6 us
  waiting for transfers between devices: 14.6 us -> 17.8 us
    dot_general x4, matrix products: 19.1 us -> 11.6 us  [the longest x2 6.78 us: mix_channels(): jnp.einsum('dtsh,dshm->dtm', weights, spread, precision=one_pass)]
    all_to_all x1, waiting for transfers between devices: 1.94 us -> 5.2 us  [per_device(): lax.all_to_all(send_state, 'dp', split_axis=0, concat_axis=0, tiled=True)]
  transfers between devices with their start and end apart: 15 -> 15, of which waited for: 5 -> 5; matrix products, arithmetic and copies ran while one was open for 36% -> 35% of each run, Pallas kernels for 0% -> 0%
where the time goes in v3:
time: 131 us; the launch traced here: 130 us
  matrix products  40.6 us (31%)
  local copies, waits for them, and re-layouts  34.2 us (26%)
  starting transfers between devices  29.9 us (23%)
  waiting for transfers between devices  17.8 us (14%)
  other arithmetic  5.73 us (4%)
  between operations  1.31 us (1%)
    ppermute x9, starting transfers between devices, shifted(): lax.ppermute(value, axis, [(source, (source + steps) % count) for source...  12.1 us
    ppermute x9, waiting for transfers between devices, shifted(): lax.ppermute(value, axis, [(source, (source + steps) % count) for source...  11.9 us
    unnamed x74, local copies, waits for them, and re-layouts  10.6 us
    dot_general x8, matrix products, scatter_sum(): jnp.dot(gnormed, weight_block, preferred_element_type=jnp.float32)  10.5 us
    dot_general x2, matrix products, per_device(): jnp.dot(normed, proj_rotated, preferred_element_type=jnp.float32)  9.88 us
    ppermute x4, starting transfers between devices, gather_from_behind(): parts.append(lax.ppermute(value, ('section', 'mp'), pairs))  7.77 us
    convert_element_type x2, local copies, waits for them, and re-layouts, mix_channels(): end_state.reshape(doc_count, head_count, head_dim * state_width)  7.02 us
    dot_general x2, matrix products, mix_channels(): jnp.einsum('dtsh,dshm->dtm', weights, spread, precision=one_pass)  6.78 us
  transfers between devices with their start and end apart: 15, of which 5 were waited for; matrix products, arithmetic and copies ran while one was open for 35% of the time, Pallas kernels for 0%

profile of v3, /device:TPU:0, one launch (start us, length us, event | category | flops | bytes accessed | tf_op | source)
XLA Modules:
  0.0 129.6 jit_solution(2650539817720999385)
XLA Ops:
  0.6 3.9 %collective-permute-start = (bf16[256,512]{1,0:T(8,128)(2,1)}, bf16[256,512]{1,0:T(8,128)(2,1)}, u32[]{:S(2)}, u32[]{:S(2)}) collective-permute-start(bf16[256,512]{1,0:T(8,128)(2,1)} %param.15), channel_id=1, source_target_pairs={{0,3},{1,0},{2,1},{3,2},{4,7},{5,4},{6,5},{7,6},{8,11},{9,8},{10,9... | collective-permute-start | bytes 786440 | tf_op jit(solution)/shard_map/ppermute | solution.py:90
  5.7 0.9 copy.60
  6.6 0.7 broadcast_in_dim.40
  7.3 0.7 reshape.217
  8.7 0.7 reshape.218
  9.4 4.9 %all-to-all-start = ((bf16[16,3,640]{2,1,0:T(4,128)(2,1)}), bf16[16,3,640]{2,1,0:T(4,128)(2,1)S(1)}, u32[]{:S(2)}, u32[]{:S(2)}) async-start(bf16[16,3,640]{2,1,0:T(4,128)(2,1)} %reshape.218), calls=%async_computation | async-start | bytes 163840 | tf_op jit(solution)/shard_map/all_to_all | solution.py:192
  14.9 0.7 compare_convert_fusion
  15.5 0.9 slice_reduce_fusion.3
  16.4 0.6 fusion.126
  17.1 1.8 %copy.83 = bf16[2,8,16,2048]{3,1,2,0:T(8,128)(2,1)S(1)} copy(bf16[2,8,16,2048]{3,2,1,0:T(8,128)(2,1)} %bitcast.95) | data formatting | bytes 2097152
  19.6 0.7 mul.331
  20.3 1.5 %copy.84 = bf16[2,8,16,2048]{3,2,1,0:T(8,128)(2,1)} copy(bf16[2,8,16,2048]{3,1,2,0:T(8,128)(2,1)S(1)} %bitcast.91) | data formatting | bytes 2097152
  21.9 5.2 %all-to-all-start.1 = ((bf16[16,16,2048]{2,1,0:T(8,128)(2,1)}), bf16[16,16,2048]{2,1,0:T(8,128)(2,1)}, u32[]{:S(2)}, u32[]{:S(2)}) async-start(bf16[16,16,2048]{2,1,0:T(8,128)(2,1)} %bitcast.93), calls=%async_computation.1 | async-start | bytes 2097152 | tf_op jit(solution)/shard_map/all_to_all | solution.py:193
  27.4 0.7 reshape.225
  28.1 1.0 constant_dynamic-update-slice_fusion.3
  29.1 1.0 constant_dynamic-update-slice_fusion.2
  30.1 1.0 constant_dynamic-update-slice_fusion.1
  31.4 4.7 %fusion.47 = f32[256,1168]{1,0:T(8,128)S(1)} fusion(bf16[256,2048]{1,0:T(8,128)(2,1)S(1)} %constant_dynamic-update-slice_fusion, f32[2048]{0:T(1024)S(1)} %fusion.134, f32[256]{0:T(256)S(1)} %add_rsqrt_fusion.3, s32[]{:T(128)S(6)} %select_n.101, bf16[2048,1168]{0,1:T(8,128)(2,1)} %bitcast.115), kind=kOutput, calls=%fused_computation.66 | convolution fusion | flops 1236402176 | bytes 7037956 | tf_op jit(solution)/shard_map/dot_general | solution.py:218
  36.8 0.8 copy-done.3
  37.6 0.9 slice.115
  38.6 0.8 copy.61
  39.4 0.8 copy.58
  40.2 1.3 fusion.102
  41.5 1.2 fusion.111
  42.6 3.7 %fusion.32 = f32[16,16,512]{2,1,0:T(8,128)} fusion(f32[16,512]{1,0:T(8,128)} %fusion.126, f32[16,16,512]{2,1,0:T(8,128)} %slice.115, f32[16,16,16]{1,2,0:T(8,128)} %copy.61, f32[16,16,16]{2,1,0:T(8,128)S(1)} %fusion.102, f32[16,16,16]{1,2,0:T(8,128)} %copy.58, pred[16,16]{1,0:T(8,128)(4,1)} %iota_compare_fusion.8), kind=kOutput, calls=%fused_computation.48 | convolution fusion | flops 69468160 | bytes 1130752 | tf_op jit(solution)/shard_map/dtsh,dshm->dtm/dot_general | solution.py:69
  46.4 5.2 %all-to-all-done.1 = bf16[16,16,2048]{2,1,0:T(8,128)(2,1)} async-done(((bf16[16,16,2048]{2,1,0:T(8,128)(2,1)}), bf16[16,16,2048]{2,1,0:T(8,128)(2,1)}, u32[]{:S(2)}, u32[]{:S(2)}) %all-to-all-start.1) | async-done | bytes 1048608 | tf_op jit(solution)/shard_map/all_to_all | solution.py:193
  51.6 1.8 %copy.85 = bf16[2,8,16,2048]{3,1,2,0:T(8,128)(2,1)S(1)} copy(bf16[2,8,16,2048]{3,2,1,0:T(8,128)(2,1)} %bitcast.33) | data formatting | bytes 2097152
  53.4 1.4 %convolution_convert_fusion = bf16[16,32768]{1,0:T(8,128)(2,1)} fusion(bf16[16,32768]{1,0:T(8,128)(2,1)S(1)} %bitcast.94, bf16[16]{0:T(256)(128)(2,1)S(1)} %copy-done.30, s32[16]{0:T(128)S(1)} %copy-done.20), kind=kOutput, calls=%fused_computation | convolution fusion | flops 17302016 | bytes 2097248 | tf_op jit(solution)/shard_map/dot_general | solution.py:187
  54.8 4.1 %reshape_reshape.4 = bf16[16,512,64]{2,1,0:T(8,128)(2,1)} reshape(bf16[16,32768]{1,0:T(8,128)(2,1)} %convolution_convert_fusion) | data formatting | bytes 2097152 | tf_op jit(solution)/shard_map/reshape;reshape | solution.py:70
  58.9 3.0 %multiply_reduce_fusion.1 = (f32[16,16]{1,0:T(8,128)S(1)}, f32[16,16,512]{2,1,0:T(8,128)S(1)}) fusion(f32[16,16,1168]{2,1,0:T(8,128)} %bitcast.102, f32[16,16,640]{2,1,0:T(8,128)} %copy-done.3, f32[512]{0:T(512)S(1)} %copy-done.26, f32[16,16,512]{2,1,0:T(8,128)} %fusion.32, f32[16,16,512]{2,1,0:T(8,128)} %fusion.111, bf16[16,512,64]{2,1,0:T(8,128)(2,1)} %reshape_reshape.4), kind=kOutput, calls=%fused_computation.119 | convolution fusion | flops 18218752 | bytes 3804160 | tf_op jit(solution)/shard_map/dtn,dmn->dtm/dot_general | solution.py:71
  62.0 1.0 convolution_convert_fusion.8
  63.0 2.4 %collective-permute-start.5 = (bf16[256,512]{1,0:T(8,128)(2,1)}, bf16[256,512]{1,0:T(8,128)(2,1)}, u32[]{:S(2)}, u32[]{:S(2)}) collective-permute-start(bf16[256,512]{1,0:T(8,128)(2,1)} %convolution_convert_fusion.8), channel_id=1, source_target_pairs={{0,3},{1,0},{2,1},{3,2},{4,7},{5,4},{6,5},{7,6},{8,11},{9,8},{10,9... | collective-permute-start | bytes 786440 | tf_op jit(solution)/shard_map/ppermute | solution.py:90
  65.4 1.0 convolution_convert_fusion.9
  66.4 1.5 %collective-permute-start.4 = (bf16[256,512]{1,0:T(8,128)(2,1)}, bf16[256,512]{1,0:T(8,128)(2,1)}, u32[]{:S(2)}, u32[]{:S(2)}) collective-permute-start(bf16[256,512]{1,0:T(8,128)(2,1)} %convolution_convert_fusion.9), channel_id=1, source_target_pairs={{0,2},{1,3},{2,0},{3,1},{4,6},{5,7},{6,4},{7,5},{8,10},{9,11},{10,... | collective-permute-start | bytes 786440 | tf_op jit(solution)/shard_map/ppermute | solution.py:90
  67.9 1.0 convolution_convert_fusion.10
  68.9 3.6 %collective-permute-done.5 = bf16[256,512]{1,0:T(8,128)(2,1)} collective-permute-done((bf16[256,512]{1,0:T(8,128)(2,1)}, bf16[256,512]{1,0:T(8,128)(2,1)}, u32[]{:S(2)}, u32[]{:S(2)}) %collective-permute-start.5) | collective-permute-done | bytes 262176 | tf_op jit(solution)/shard_map/ppermute | solution.py:90
  72.5 6.8 %collective-permute-done.4 = bf16[256,512]{1,0:T(8,128)(2,1)} collective-permute-done((bf16[256,512]{1,0:T(8,128)(2,1)}, bf16[256,512]{1,0:T(8,128)(2,1)}, u32[]{:S(2)}, u32[]{:S(2)}) %collective-permute-start.4) | collective-permute-done | bytes 262176 | tf_op jit(solution)/shard_map/ppermute | solution.py:90
  79.3 2.3 %add_convert_fusion.2 = bf16[256,512]{1,0:T(8,128)(2,1)} fusion(bf16[256,512]{1,0:T(8,128)(2,1)} %collective-permute-done.5, bf16[256,512]{1,0:T(8,128)(2,1)} %collective-permute-done.4, bf16[256,512]{1,0:T(8,128)(2,1)} %collective-permute-done.3, bf16[256,512]{1,0:T(8,128)(2,1)S(1)} %bitcast.86, bf16[256,512]{1,0:T(8,128)(2,1)} %param.15, ...), kind=kOutput, calls=%fused_computation.117 | convolution fusion | flops 135659520 | bytes 2097156 | tf_op jit(solution)/shard_map/dot_general | solution.py:136
  81.6 1.3 collective-permute-start.6
  82.9 2.5 %collective-permute-start.9 = (bf16[256,512]{1,0:T(8,128)(2,1)}, bf16[256,512]{1,0:T(8,128)(2,1)}, u32[]{:S(2)}, u32[]{:S(2)}) collective-permute-start(bf16[256,512]{1,0:T(8,128)(2,1)} %add_convert_fusion.2), channel_id=1, source_target_pairs={{0,17},{1,18},{2,19},{3,16},{4,21},{5,22},{6,23},{7,20},{8,25},{9,... | collective-permute-start | bytes 786440 | tf_op jit(solution)/shard_map/ppermute | solution.py:118
  85.3 2.0 %collective-permute-start.8 = (bf16[256,512]{1,0:T(8,128)(2,1)}, bf16[256,512]{1,0:T(8,128)(2,1)}, u32[]{:S(2)}, u32[]{:S(2)}) collective-permute-start(bf16[256,512]{1,0:T(8,128)(2,1)} %add_convert_fusion.2), channel_id=1, source_target_pairs={{0,18},{1,19},{2,16},{3,17},{4,22},{5,23},{6,20},{7,21},{8,26},{9,... | collective-permute-start | bytes 786440 | tf_op jit(solution)/shard_map/ppermute | solution.py:118
  87.3 2.0 %collective-permute-start.7 = (bf16[256,512]{1,0:T(8,128)(2,1)}, bf16[256,512]{1,0:T(8,128)(2,1)}, u32[]{:S(2)}, u32[]{:S(2)}) collective-permute-start(bf16[256,512]{1,0:T(8,128)(2,1)} %add_convert_fusion.2), channel_id=1, source_target_pairs={{0,19},{1,16},{2,17},{3,18},{4,23},{5,20},{6,21},{7,22},{8,27},{9,... | collective-permute-start | bytes 786440 | tf_op jit(solution)/shard_map/ppermute | solution.py:118
  89.4 2.7 %copy.71 = bf16[16,512,64]{1,2,0:T(8,128)(2,1)} copy(bf16[16,512,64]{2,1,0:T(8,128)(2,1)} %reshape_reshape.4) | data formatting | bytes 2097152 | tf_op jit(solution)/shard_map/reshape;reshape | solution.py:70
  92.1 0.8 collective-permute-done.7
  92.8 1.5 %fusion.13 = f32[256]{0:T(256)S(1)} fusion(bf16[256,2048]{1,0:T(8,128)(2,1)S(1)} %constant_dynamic-update-slice_fusion, bf16[256,512]{1,0:T(8,128)(2,1)S(1)} %collective-permute-done.6, bf16[256,512]{1,0:T(8,128)(2,1)} %collective-permute-done.9, bf16[256,512]{1,0:T(8,128)(2,1)} %collective-permute-done.8, bf16[256,512]{1,0:T(8,128)(2,1)} %collective-permute-done.7, ...), kind=kLoop, calls=%fused_computation.23 | loop fusion | flops 6291200 | bytes 2098177 | tf_op jit(solution)/shard_map/reduce_sum | solution.py:19
  94.4 5.1 %fusion.45 = f32[256,1168]{1,0:T(8,128)S(1)} fusion(f32[256]{0:T(256)S(1)} %add_rsqrt_fusion.2, f32[2048]{0:T(1024)S(1)} %copy-done.18, bf16[256,2048]{1,0:T(8,128)(2,1)S(1)} %constant_dynamic-update-slice_fusion, bf16[256,512]{1,0:T(8,128)(2,1)S(1)} %collective-permute-done.6, bf16[256,512]{1,0:T(8,128)(2,1)} %collective-permute-done.9, ...), kind=kOutput, calls=%fused_computation.65 | convolution fusion | flops 1241120768 | bytes 8086533 | tf_op jit(solution)/shard_map/dot_general | solution.py:218
  100.3 0.9 slice.125
  101.2 0.9 fusion.116
  102.1 0.8 copy.68
  103.4 3.0 %fusion.37 = f32[16,16,512]{2,1,0:T(8,128)S(1)} fusion(f32[16,16,512]{2,1,0:T(8,128)} %slice.125, f32[16,512]{1,0:T(8,128)} %fusion.126, f32[16,16,16]{1,2,0:T(8,128)} %copy.68, f32[16,16,16]{2,1,0:T(8,128)} %fusion.116, f32[16,16,16]{1,2,0:T(8,128)S(1)} %copy.66, pred[16,16]{1,0:T(8,128)(4,1)S(1)} %copy-done.28), kind=kOutput, calls=%fused_computation.49 | convolution fusion | flops 69468160 | bytes 1130752 | tf_op jit(solution)/shard_map/dtsh,dshm->dtm/dot_general | solution.py:69
  106.5 1.8 %multiply_reduce_fusion = (f32[16,16]{1,0:T(8,128)S(1)}, f32[16,16,512]{2,1,0:T(8,128)S(1)}) fusion(f32[16,16,1168]{2,1,0:T(8,128)} %bitcast.98, f32[16,16,640]{2,1,0:T(8,128)S(1)} %divide_multiply_fusion, f32[512]{0:T(512)S(1)} %copy-done.27, f32[16,16,512]{2,1,0:T(8,128)S(1)} %fusion.37, f32[16,16,512]{2,1,0:T(8,128)S(1)} %fusion.107, ...), kind=kOutput, calls=%fused_computation.116 | convolution fusion | flops 18218752 | bytes 3804160 | tf_op jit(solution)/shard_map/dtn,dmn->dtm/dot_general | solution.py:71
  108.5 1.0 convolution_convert_fusion.4
  109.5 1.0 convolution_convert_fusion.5
  110.5 1.0 convolution_convert_fusion.6
  111.7 0.8 collective-permute-start.12
  112.4 1.3 %collective-permute-start.11 = (bf16[256,512]{1,0:T(8,128)(2,1)}, bf16[256,512]{1,0:T(8,128)(2,1)}, u32[]{:S(2)}, u32[]{:S(2)}) collective-permute-start(bf16[256,512]{1,0:T(8,128)(2,1)} %convolution_convert_fusion.5), channel_id=1, source_target_pairs={{0,2},{1,3},{2,0},{3,1},{4,6},{5,7},{6,4},{7,5},{8,10},{9,11},{10,... | collective-permute-start | bytes 786440 | tf_op jit(solution)/shard_map/ppermute | solution.py:90
  113.8 1.0 collective-permute-start.10
  115.2 2.1 %add_convert_fusion = bf16[16,512,64]{1,2,0:T(8,128)(2,1)} fusion(bf16[16,512,64]{1,2,0:T(8,128)(2,1)S(1)} %copy-done.2, f32[16,16,512]{2,1,0:T(8,128)S(1)} %convolution_multiply_fusion, f32[16,512]{1,0:T(8,128)S(1)} %fusion.124, f32[16,16,640]{2,1,0:T(8,128)S(1)} %divide_multiply_fusion), kind=kOutput, calls=%fused_computation.26 | convolution fusion | flops 52428800 | bytes 2785280 | tf_op jit(solution)/shard_map/dsm,dsn->dmn/dot_general | solution.py:77
  117.3 2.7 %copy.73 = bf16[16,512,64]{2,1,0:T(8,128)(2,1)} copy(bf16[16,512,64]{1,2,0:T(8,128)(2,1)} %add_convert_fusion) | data formatting | bytes 2097152 | tf_op jit(solution)/shard_map/convert_element_type | solution.py:82
  120.0 4.3 %convert_element_type.173 = bf16[1,16,16,2048]{3,2,1,0:T(8,128)(2,1)} reshape(bf16[16,512,64]{2,1,0:T(8,128)(2,1)} %copy.73) | data formatting | bytes 2097152 | tf_op jit(solution)/shard_map/convert_element_type | solution.py:82
  124.3 1.0 fusion.122
  125.3 0.6 copy.74
  125.9 1.5 %collective-permute-done.10 = bf16[256,512]{1,0:T(8,128)(2,1)} collective-permute-done((bf16[256,512]{1,0:T(8,128)(2,1)}, bf16[256,512]{1,0:T(8,128)(2,1)}, u32[]{:S(2)}, u32[]{:S(2)}) %collective-permute-start.10) | collective-permute-done | bytes 262176 | tf_op jit(solution)/shard_map/ppermute | solution.py:90
  127.4 2.2 %fusion.101 = bf16[1,256,512]{2,1,0:T(8,128)(2,1)} fusion(bf16[256,512]{1,0:T(8,128)(2,1)} %collective-permute-done.12, bf16[256,512]{1,0:T(8,128)(2,1)} %collective-permute-done.11, bf16[256,512]{1,0:T(8,128)(2,1)} %collective-permute-done.10, bf16[256,512]{1,0:T(8,128)(2,1)S(1)} %copy-done.5, bf16[256,512]{1,0:T(8,128)(2,1)S(1)} %collective-permute-done.6, ...), kind=kOutput, calls=%fused_computation.130 | convolution fusion | flops 135790592 | bytes 2359301 | tf_op jit(solution)/shard_map/dot_general | solution.py:136
  (113 shorter events, 6.3 us)
Async XLA Ops:
  0.6 61.4 %copy-start = (bf16[1,512,2048]{2,1,0:T(8,128)(2,1)S(1)}, bf16[1,512,2048]{2,1,0:T(8,128)(2,1)}, u32[]{:S(2)}) copy-start(bf16[1,512,2048]{2,1,0:T(8,128)(2,1)} %param.24) | copy-start | bytes 6291460
  0.6 27.4 %collective-permute-start = (bf16[256,512]{1,0:T(8,128)(2,1)}, bf16[256,512]{1,0:T(8,128)(2,1)}, u32[]{:S(2)}, u32[]{:S(2)}) collective-permute-start(bf16[256,512]{1,0:T(8,128)(2,1)} %param.15), channel_id=1, source_target_pairs={{0,3},{1,0},{2,1},{3,2},{4,7},{5,4},{6,5},{7,6},{8,11},{9,8},{10,9... | collective-permute-start | bytes 786440 | tf_op jit(solution)/shard_map/ppermute | solution.py:90
  4.6 24.5 %collective-permute-start.1 = (bf16[256,512]{1,0:T(8,128)(2,1)}, bf16[256,512]{1,0:T(8,128)(2,1)}, u32[]{:S(2)}, u32[]{:S(2)}) collective-permute-start(bf16[256,512]{1,0:T(8,128)(2,1)} %param.15), channel_id=1, source_target_pairs={{0,2},{1,3},{2,0},{3,1},{4,6},{5,7},{6,4},{7,5},{8,10},{9,11},{10,... | collective-permute-start | bytes 786440 | tf_op jit(solution)/shard_map/ppermute | solution.py:90
  5.1 25.0 %collective-permute-start.2 = (bf16[256,512]{1,0:T(8,128)(2,1)}, bf16[256,512]{1,0:T(8,128)(2,1)}, u32[]{:S(2)}, u32[]{:S(2)}) collective-permute-start(bf16[256,512]{1,0:T(8,128)(2,1)} %param.15), channel_id=1, source_target_pairs={{0,1},{1,2},{2,3},{3,0},{4,5},{5,6},{6,7},{7,4},{8,9},{9,10},{10,1... | collective-permute-start | bytes 786440 | tf_op jit(solution)/shard_map/ppermute | solution.py:90
  9.4 12.5 %all-to-all-start = ((bf16[16,3,640]{2,1,0:T(4,128)(2,1)}), bf16[16,3,640]{2,1,0:T(4,128)(2,1)S(1)}, u32[]{:S(2)}, u32[]{:S(2)}) async-start(bf16[16,3,640]{2,1,0:T(4,128)(2,1)} %reshape.218), calls=%async_computation | async-start | bytes 163840 | tf_op jit(solution)/shard_map/all_to_all | solution.py:192
  15.5 11.6 %copy-start.29 = (bf16[16]{0:T(256)(128)(2,1)}, bf16[16]{0:T(256)(128)(2,1)S(1)}, u32[]{:S(2)}) copy-start(bf16[16]{0:T(256)(128)(2,1)S(1)} %compare_convert_fusion) | copy-start | bytes 100
  16.4 19.8 %copy-start.10 = (f32[640]{0:T(1024)}, f32[640]{0:T(1024)S(1)}, u32[]{:S(2)}) copy-start(f32[640]{0:T(1024)S(1)} %get-tuple-element.14) | copy-start | bytes 7684
  16.4 19.8 %copy-start.12 = (f32[640]{0:T(1024)}, f32[640]{0:T(1024)S(1)}, u32[]{:S(2)}) copy-start(f32[640]{0:T(1024)S(1)} %get-tuple-element.15) | copy-start | bytes 7684
  17.1 2.3 %copy-start.16 = (f32[1,2048]{1,0:T(1,128)S(1)}, f32[1,2048]{1,0:T(1,128)}, u32[]{:S(2)}) copy-start(f32[1,2048]{1,0:T(1,128)} %param.16) | copy-start | bytes 24580
  17.1 2.5 %copy-start.31 = (f32[1,16]{1,0:T(1,128)S(1)}, f32[1,16]{1,0:T(1,128)}, u32[]{:S(2)}) copy-start(f32[1,16]{1,0:T(1,128)} %param.22) | copy-start | bytes 196
  18.9 3.0 %copy-start.21 = (f32[1,640]{1,0:T(1,128)S(1)}, f32[1,640]{1,0:T(1,128)}, u32[]{:S(2)}) copy-start(f32[1,640]{1,0:T(1,128)} %param.19) | copy-start | bytes 7684
  19.5 11.9 %copy-start.17 = (f32[2048]{0:T(1024)}, f32[2048]{0:T(1024)S(1)}, u32[]{:S(2)}) copy-start(f32[2048]{0:T(1024)S(1)} %fusion.134) | copy-start | bytes 24580
  19.5 7.6 %copy-start.19 = (s32[16]{0:T(128)}, s32[16]{0:T(128)S(1)}, u32[]{:S(2)}) copy-start(s32[16]{0:T(128)S(1)} %fusion.160) | copy-start | bytes 196
  21.9 9.2 %copy-start.4 = (bf16[256,512]{1,0:T(8,128)(2,1)S(1)}, bf16[256,512]{1,0:T(8,128)(2,1)}, u32[]{:S(2)}) copy-start(bf16[256,512]{1,0:T(8,128)(2,1)} %param.15) | copy-start | bytes 786436
  21.9 29.7 %all-to-all-start.1 = ((bf16[16,16,2048]{2,1,0:T(8,128)(2,1)}), bf16[16,16,2048]{2,1,0:T(8,128)(2,1)}, u32[]{:S(2)}, u32[]{:S(2)}) async-start(bf16[16,16,2048]{2,1,0:T(8,128)(2,1)} %bitcast.93), calls=%async_computation.1 | async-start | bytes 2097152 | tf_op jit(solution)/shard_map/all_to_all | solution.py:193
  31.4 4.9 %copy-start.6 = (f32[16,3,640]{2,1,0:T(4,128)S(1)}, f32[16,3,640]{2,1,0:T(4,128)}, u32[]{:S(2)}) copy-start(f32[16,3,640]{2,1,0:T(4,128)} %reshape.225) | copy-start | bytes 368644
  36.2 2.4 %copy-start.9 = (f32[256,1168]{1,0:T(8,128)}, f32[256,1168]{1,0:T(8,128)S(1)}, u32[]{:S(2)}) copy-start(f32[256,1168]{1,0:T(8,128)S(1)} %fusion.47) | copy-start | bytes 3588100
  36.2 2.3 %copy-start.22 = (f32[1,16]{1,0:T(1,128)S(1)}, f32[1,16]{1,0:T(1,128)}, u32[]{:S(2)}) copy-start(f32[1,16]{1,0:T(1,128)} %param.21) | copy-start | bytes 196
  36.2 2.3 %copy-start.24 = (f32[1,16]{1,0:T(1,128)S(1)}, f32[1,16]{1,0:T(1,128)}, u32[]{:S(2)}) copy-start(f32[1,16]{1,0:T(1,128)} %param.20) | copy-start | bytes 196
  36.8 0.8 copy-start.3
  46.3 7.0 %copy-start.20 = (s32[16]{0:T(128)S(1)}, s32[16]{0:T(128)}, u32[]{:S(2)}) copy-start(s32[16]{0:T(128)} %copy-done.19) | copy-start | bytes 196
  46.4 7.0 %copy-start.30 = (bf16[16]{0:T(256)(128)(2,1)S(1)}, bf16[16]{0:T(256)(128)(2,1)}, u32[]{:S(2)}) copy-start(bf16[16]{0:T(256)(128)(2,1)} %copy-done.29) | copy-start | bytes 100
  54.8 4.1 %copy-start.26 = (f32[512]{0:T(512)S(1)}, f32[512]{0:T(512)}, u32[]{:S(2)}) copy-start(f32[512]{0:T(512)} %mul.331) | copy-start | bytes 6148
  58.9 3.0 %copy-start.14 = (f32[1,512]{1,0:T(1,128)S(1)}, f32[1,512]{1,0:T(1,128)}, u32[]{:S(2)}) copy-start(f32[1,512]{1,0:T(1,128)} %param.23) | copy-start | bytes 6148
  63.0 9.5 %collective-permute-start.5 = (bf16[256,512]{1,0:T(8,128)(2,1)}, bf16[256,512]{1,0:T(8,128)(2,1)}, u32[]{:S(2)}, u32[]{:S(2)}) collective-permute-start(bf16[256,512]{1,0:T(8,128)(2,1)} %convolution_convert_fusion.8), channel_id=1, source_target_pairs={{0,3},{1,0},{2,1},{3,2},{4,7},{5,4},{6,5},{7,6},{8,11},{9,8},{10,9... | collective-permute-start | bytes 786440 | tf_op jit(solution)/shard_map/ppermute | solution.py:90
  66.4 12.9 %collective-permute-start.4 = (bf16[256,512]{1,0:T(8,128)(2,1)}, bf16[256,512]{1,0:T(8,128)(2,1)}, u32[]{:S(2)}, u32[]{:S(2)}) collective-permute-start(bf16[256,512]{1,0:T(8,128)(2,1)} %convolution_convert_fusion.9), channel_id=1, source_target_pairs={{0,2},{1,3},{2,0},{3,1},{4,6},{5,7},{6,4},{7,5},{8,10},{9,11},{10,... | collective-permute-start | bytes 786440 | tf_op jit(solution)/shard_map/ppermute | solution.py:90
  68.9 10.4 %collective-permute-start.3 = (bf16[256,512]{1,0:T(8,128)(2,1)}, bf16[256,512]{1,0:T(8,128)(2,1)}, u32[]{:S(2)}, u32[]{:S(2)}) collective-permute-start(bf16[256,512]{1,0:T(8,128)(2,1)} %convolution_convert_fusion.10), channel_id=1, source_target_pairs={{0,1},{1,2},{2,3},{3,0},{4,5},{5,6},{6,7},{7,4},{8,9},{9,10},{10,1... | collective-permute-start | bytes 786440 | tf_op jit(solution)/shard_map/ppermute | solution.py:90
  81.6 10.5 %collective-permute-start.6 = (bf16[256,512]{1,0:T(8,128)(2,1)}, bf16[256,512]{1,0:T(8,128)(2,1)S(1)}, u32[]{:S(2)}, u32[]{:S(2)}) collective-permute-start(bf16[256,512]{1,0:T(8,128)(2,1)} %add_convert_fusion.2), channel_id=1, source_target_pairs={{0,16},{1,17},{2,18},{3,19},{4,20},{5,21},{6,22},{7,23},{8,24},{9,... | collective-permute-start | bytes 786440 | tf_op jit(solution)/shard_map/ppermute | solution.py:118
  82.9 9.2 %collective-permute-start.9 = (bf16[256,512]{1,0:T(8,128)(2,1)}, bf16[256,512]{1,0:T(8,128)(2,1)}, u32[]{:S(2)}, u32[]{:S(2)}) collective-permute-start(bf16[256,512]{1,0:T(8,128)(2,1)} %add_convert_fusion.2), channel_id=1, source_target_pairs={{0,17},{1,18},{2,19},{3,16},{4,21},{5,22},{6,23},{7,20},{8,25},{9,... | collective-permute-start | bytes 786440 | tf_op jit(solution)/shard_map/ppermute | solution.py:118
  85.3 6.7 %collective-permute-start.8 = (bf16[256,512]{1,0:T(8,128)(2,1)}, bf16[256,512]{1,0:T(8,128)(2,1)}, u32[]{:S(2)}, u32[]{:S(2)}) collective-permute-start(bf16[256,512]{1,0:T(8,128)(2,1)} %add_convert_fusion.2), channel_id=1, source_target_pairs={{0,18},{1,19},{2,16},{3,17},{4,22},{5,23},{6,20},{7,21},{8,26},{9,... | collective-permute-start | bytes 786440 | tf_op jit(solution)/shard_map/ppermute | solution.py:118
  87.3 5.5 %collective-permute-start.7 = (bf16[256,512]{1,0:T(8,128)(2,1)}, bf16[256,512]{1,0:T(8,128)(2,1)}, u32[]{:S(2)}, u32[]{:S(2)}) collective-permute-start(bf16[256,512]{1,0:T(8,128)(2,1)} %add_convert_fusion.2), channel_id=1, source_target_pairs={{0,19},{1,16},{2,17},{3,18},{4,23},{5,20},{6,21},{7,22},{8,27},{9,... | collective-permute-start | bytes 786440 | tf_op jit(solution)/shard_map/ppermute | solution.py:118
  89.4 5.0 %copy-start.18 = (f32[2048]{0:T(1024)S(1)}, f32[2048]{0:T(1024)}, u32[]{:S(2)}) copy-start(f32[2048]{0:T(1024)} %copy-done.17) | copy-start | bytes 24580
  94.4 5.3 %copy-start.23 = (f32[1,16]{1,0:T(1,128)S(1)}, f32[1,16]{1,0:T(1,128)}, u32[]{:S(2)}) copy-start(f32[1,16]{1,0:T(1,128)} %param.21) | copy-start | bytes 196
  94.4 5.3 %copy-start.25 = (f32[1,16]{1,0:T(1,128)S(1)}, f32[1,16]{1,0:T(1,128)}, u32[]{:S(2)}) copy-start(f32[1,16]{1,0:T(1,128)} %param.20) | copy-start | bytes 196
  94.4 5.4 %copy-start.7 = (f32[16,3,640]{2,1,0:T(4,128)S(1)}, f32[16,3,640]{2,1,0:T(4,128)}, u32[]{:S(2)}) copy-start(f32[16,3,640]{2,1,0:T(4,128)} %reshape.225) | copy-start | bytes 368644
  94.4 5.4 %copy-start.11 = (f32[640]{0:T(1024)S(1)}, f32[640]{0:T(1024)}, u32[]{:S(2)}) copy-start(f32[640]{0:T(1024)} %copy-done.10) | copy-start | bytes 7684
  94.4 5.4 %copy-start.13 = (f32[640]{0:T(1024)S(1)}, f32[640]{0:T(1024)}, u32[]{:S(2)}) copy-start(f32[640]{0:T(1024)} %copy-done.12) | copy-start | bytes 7684
  99.6 1.6 %copy-start.8 = (f32[256,1168]{1,0:T(8,128)}, f32[256,1168]{1,0:T(8,128)S(1)}, u32[]{:S(2)}) copy-start(f32[256,1168]{1,0:T(8,128)S(1)} %fusion.45) | copy-start | bytes 3588100
  100.3 3.1 %copy-start.28 = (pred[16,16]{1,0:T(8,128)(4,1)S(1)}, pred[16,16]{1,0:T(8,128)(4,1)}, u32[]{:S(2)}) copy-start(pred[16,16]{1,0:T(8,128)(4,1)} %iota_compare_fusion.8) | copy-start | bytes 772
  103.4 3.1 %copy-start.1 = (bf16[16,512,64]{2,1,0:T(8,128)(2,1)S(1)}, bf16[16,512,64]{2,1,0:T(8,128)(2,1)}, u32[]{:S(2)}) copy-start(bf16[16,512,64]{2,1,0:T(8,128)(2,1)} %reshape_reshape.4) | copy-start | bytes 3145732
  103.4 3.1 %copy-start.27 = (f32[512]{0:T(512)S(1)}, f32[512]{0:T(512)}, u32[]{:S(2)}) copy-start(f32[512]{0:T(512)} %mul.331) | copy-start | bytes 6148
  106.5 1.9 %copy-start.15 = (f32[1,512]{1,0:T(1,128)S(1)}, f32[1,512]{1,0:T(1,128)}, u32[]{:S(2)}) copy-start(f32[1,512]{1,0:T(1,128)} %param.23) | copy-start | bytes 6148
  108.5 6.7 %copy-start.2 = (bf16[16,512,64]{1,2,0:T(8,128)(2,1)S(1)}, bf16[16,512,64]{1,2,0:T(8,128)(2,1)}, u32[]{:S(2)}) copy-start(bf16[16,512,64]{1,2,0:T(8,128)(2,1)} %copy.71) | copy-start | bytes 3145732
  111.7 14.3 %collective-permute-start.12 = (bf16[256,512]{1,0:T(8,128)(2,1)}, bf16[256,512]{1,0:T(8,128)(2,1)}, u32[]{:S(2)}, u32[]{:S(2)}) collective-permute-start(bf16[256,512]{1,0:T(8,128)(2,1)} %convolution_convert_fusion.4), channel_id=1, source_target_pairs={{0,3},{1,0},{2,1},{3,2},{4,7},{5,4},{6,5},{7,6},{8,11},{9,8},{10,9... | collective-permute-start | bytes 786440 | tf_op jit(solution)/shard_map/ppermute | solution.py:90
  112.4 13.5 %collective-permute-start.11 = (bf16[256,512]{1,0:T(8,128)(2,1)}, bf16[256,512]{1,0:T(8,128)(2,1)}, u32[]{:S(2)}, u32[]{:S(2)}) collective-permute-start(bf16[256,512]{1,0:T(8,128)(2,1)} %convolution_convert_fusion.5), channel_id=1, source_target_pairs={{0,2},{1,3},{2,0},{3,1},{4,6},{5,7},{6,4},{7,5},{8,10},{9,11},{10,... | collective-permute-start | bytes 786440 | tf_op jit(solution)/shard_map/ppermute | solution.py:90
  113.8 13.6 %collective-permute-start.10 = (bf16[256,512]{1,0:T(8,128)(2,1)}, bf16[256,512]{1,0:T(8,128)(2,1)}, u32[]{:S(2)}, u32[]{:S(2)}) collective-permute-start(bf16[256,512]{1,0:T(8,128)(2,1)} %convolution_convert_fusion.6), channel_id=1, source_target_pairs={{0,1},{1,2},{2,3},{3,0},{4,5},{5,6},{6,7},{7,4},{8,9},{9,10},{10,1... | collective-permute-start | bytes 786440 | tf_op jit(solution)/shard_map/ppermute | solution.py:90
  120.0 7.4 %copy-start.5 = (bf16[256,512]{1,0:T(8,128)(2,1)S(1)}, bf16[256,512]{1,0:T(8,128)(2,1)}, u32[]{:S(2)}) copy-start(bf16[256,512]{1,0:T(8,128)(2,1)} %param.15) | copy-start | bytes 786436

commit v4 on v3

--- a/solution.py
+++ b/solution.py
@@ -188,17 +188,26 @@
         return picked.astype(jnp.bfloat16).reshape((picker.shape[0],) + rows.shape[1:])
 
     send_state = select_rows(send_pick, kept_state[0])
-    send_conv = select_rows(send_pick, kept_conv[0])
-    got_conv = lax.all_to_all(send_conv, "dp", split_axis=0, concat_axis=0, tiled=True)
     got_state = lax.all_to_all(send_state, "dp", split_axis=0, concat_axis=0, tiled=True)
+    by_shift = (jnp.arange(dp_count) + dp_idx) % dp_count
+    shift_order = jnp.take(send_index.reshape(dp_count, capacity), by_shift, axis=0).reshape(-1)
+    shift_pick = (shift_order[:, None] == jnp.arange(slot_count)[None, :]).astype(jnp.bfloat16)
+    send_conv = select_rows(shift_pick, kept_conv[0])
+    conv_chunks = [send_conv[:capacity]]
+    for steps in range(1, dp_count):
+        conv_chunks.append(shifted(send_conv[steps * capacity : (steps + 1) * capacity], "dp", steps))
+    got_conv = jnp.concatenate(conv_chunks, axis=0)
     my_owners = lax.dynamic_index_in_dim(owners, dp_idx, 0, keepdims=False)
     my_rank = lax.dynamic_index_in_dim(owner_rank, dp_idx, 0, keepdims=False)
-    recv_row = my_owners * capacity + my_rank
     keep_flag = (window_start > 0).astype(jnp.float32)
-    recv_pick = (recv_row[:, None] == jnp.arange(got_state.shape[0])[None, :]).astype(jnp.float32)
-    recv_pick = (recv_pick * keep_flag[:, None]).astype(jnp.bfloat16)
-    state_start = select_rows(recv_pick, got_state)
-    conv_start = select_rows(recv_pick, got_conv).astype(jnp.float32)
+
+    def receive_pick(rows_at):
+        picker = (rows_at[:, None] == jnp.arange(got_state.shape[0])[None, :]).astype(jnp.float32)
+        return (picker * keep_flag[:, None]).astype(jnp.bfloat16)
+
+    state_start = select_rows(receive_pick(my_owners * capacity + my_rank), got_state)
+    shift_rows = ((dp_idx - my_owners) % dp_count) * capacity + my_rank
+    conv_start = select_rows(receive_pick(shift_rows), got_conv).astype(jnp.float32)
     gain_rotated = rotate_rows(norm_gain[0], shard_width)
     proj_rotated = rotate_rows(in_proj[0], shard_width)
     weight_blocks = column_blocks(out_proj[0])

time: 131 us -> 124 us (0.947)
  waiting for transfers between devices: 17.8 us -> 13.9 us
  starting transfers between devices: 29.9 us -> 28.3 us
    all_to_all x1, waiting for transfers between devices: 5.2 us -> 0.01 us  [per_device(): lax.all_to_all(send_state, 'dp', split_axis=0, concat_axis=0, tiled=True)]
    all_to_all x1 -> x0, starting transfers between devices: 4.87 us -> none  [per_device(): lax.all_to_all(send_conv, 'dp', split_axis=0, concat_axis=0, tiled=True)]
    ppermute x9 -> x12, starting transfers between devices: 12.1 us -> 16.6 us  [shifted(): lax.ppermute(value, axis, [(source, (source + steps) % count) for source...]
    ppermute x9 -> x12, waiting for transfers between devices: 11.9 us -> 13.1 us  [shifted(): lax.ppermute(value, axis, [(source, (source + steps) % count) for source...]
    unnamed x74 -> x75, local copies, waits for them, and re-layouts: 10.6 us -> 10.6 us
  transfers between devices with their start and end apart: 15 -> 17, of which waited for: 5 -> 5; matrix products, arithmetic and copies ran while one was open for 35% -> 36% of each run, Pallas kernels for 0% -> 0%
where the time goes in v4:
time: 124 us; the launch traced here: 123 us
  matrix products  40.6 us (33%)
  local copies, waits for them, and re-layouts  33.3 us (27%)
  starting transfers between devices  28.3 us (23%)
  waiting for transfers between devices  13.9 us (11%)
  other arithmetic  5.77 us (5%)
  between operations  1.32 us (1%)
    ppermute x12, starting transfers between devices, shifted(): lax.ppermute(value, axis, [(source, (source + steps) % count) for source...  16.6 us
    ppermute x12, waiting for transfers between devices, shifted(): lax.ppermute(value, axis, [(source, (source + steps) % count) for source...  13.1 us
    unnamed x75, local copies, waits for them, and re-layouts  10.6 us
    dot_general x8, matrix products, scatter_sum(): jnp.dot(gnormed, weight_block, preferred_element_type=jnp.float32)  10.5 us
    dot_general x2, matrix products, per_device(): jnp.dot(normed, proj_rotated, preferred_element_type=jnp.float32)  9.88 us
    ppermute x4, starting transfers between devices, gather_from_behind(): parts.append(lax.ppermute(value, ('section', 'mp'), pairs))  7.46 us
    convert_element_type x2, local copies, waits for them, and re-layouts, mix_channels(): end_state.reshape(doc_count, head_count, head_dim * state_width)  6.99 us
    dot_general x2, matrix products, mix_channels(): jnp.einsum('dtsh,dshm->dtm', weights, spread, precision=one_pass)  6.76 us
  transfers between devices with their start and end apart: 17, of which 5 were waited for; matrix products, arithmetic and copies ran while one was open for 36% of the time, Pallas kernels for 0%

profile of v4, /device:TPU:0, one launch (start us, length us, event | category | flops | bytes accessed | tf_op | source)
XLA Modules:
  0.0 123.1 jit_solution(11380714854351498911)
XLA Ops:
  0.6 3.9 %collective-permute-start = (bf16[256,512]{1,0:T(8,128)(2,1)}, bf16[256,512]{1,0:T(8,128)(2,1)}, u32[]{:S(2)}, u32[]{:S(2)}) collective-permute-start(bf16[256,512]{1,0:T(8,128)(2,1)} %param.15), channel_id=1, source_target_pairs={{0,3},{1,0},{2,1},{3,2},{4,7},{5,4},{6,5},{7,6},{8,11},{9,8},{10,9... | collective-permute-start | bytes 786440 | tf_op jit(solution)/shard_map/ppermute | solution.py:90
  5.1 0.9 copy.60
  6.0 0.7 broadcast_in_dim.47
  6.8 0.7 reshape.312
  8.8 3.7 %collective-permute-start.5 = (bf16[4,3,640]{2,0,1:T(4,128)(2,1)S(1)}, bf16[4,3,640]{2,0,1:T(4,128)(2,1)S(1)}, u32[]{:S(2)}, u32[]{:S(2)}) collective-permute-start(bf16[4,3,640]{2,0,1:T(4,128)(2,1)S(1)} %bitcast.119), channel_id=1, source_target_pairs={{0,12},{4,0},{8,4},{12,8},{1,13},{5,1},{9,5},{13,9},{2,14},{6,2},{... | collective-permute-start | bytes 46088 | tf_op jit(solution)/shard_map/ppermute | solution.py:90
  12.5 1.0 collective-permute-start.3
  13.6 1.8 %copy.82 = bf16[2,8,16,2048]{3,1,2,0:T(8,128)(2,1)S(1)} copy(bf16[2,8,16,2048]{3,2,1,0:T(8,128)(2,1)} %bitcast.107) | data formatting | bytes 2097152
  16.0 1.5 %copy.83 = bf16[2,8,16,2048]{3,2,1,0:T(8,128)(2,1)} copy(bf16[2,8,16,2048]{3,1,2,0:T(8,128)(2,1)S(1)} %bitcast.104) | data formatting | bytes 2097152
  17.5 4.2 %all-to-all-start = ((bf16[16,16,2048]{2,1,0:T(8,128)(2,1)}), bf16[16,16,2048]{2,1,0:T(8,128)(2,1)}, u32[]{:S(2)}, u32[]{:S(2)}) async-start(bf16[16,16,2048]{2,1,0:T(8,128)(2,1)} %bitcast.39), calls=%async_computation | async-start | bytes 2097152 | tf_op jit(solution)/shard_map/all_to_all | solution.py:191
  21.8 0.6 iota_compare_fusion.8
  22.5 0.6 fusion.133
  23.2 0.6 bitcast_add_fusion
  23.8 0.7 mul.349
  24.5 0.6 collective-permute-start.2
  25.4 0.7 reshape.318
  26.1 1.0 constant_dynamic-update-slice_fusion.3
  27.1 1.0 constant_dynamic-update-slice_fusion.2
  28.1 4.1 %collective-permute-done.2 = bf16[256,512]{1,0:T(8,128)(2,1)} collective-permute-done((bf16[256,512]{1,0:T(8,128)(2,1)S(1)}, bf16[256,512]{1,0:T(8,128)(2,1)}, u32[]{:S(2)}, u32[]{:S(2)}) %collective-permute-start.2) | collective-permute-done | bytes 262176 | tf_op jit(solution)/shard_map/ppermute | solution.py:90
  32.3 1.0 constant_dynamic-update-slice_fusion.1
  33.6 4.7 %fusion.47 = f32[256,1168]{1,0:T(8,128)S(1)} fusion(bf16[256,2048]{1,0:T(8,128)(2,1)S(1)} %constant_dynamic-update-slice_fusion, f32[2048]{0:T(1024)S(1)} %fusion.141, f32[256]{0:T(256)S(1)} %add_rsqrt_fusion.3, s32[]{:T(128)S(6)} %select_n.155, bf16[2048,1168]{0,1:T(8,128)(2,1)} %bitcast.128), kind=kOutput, calls=%fused_computation.67 | convolution fusion | flops 1236402176 | bytes 7037956 | tf_op jit(solution)/shard_map/dot_general | solution.py:227
  39.0 0.8 copy-done.3
  39.8 0.9 slice.150
  40.8 0.8 copy.61
  41.6 0.8 copy.58
  42.4 1.3 %fusion.102 = f32[16,16,16]{2,1,0:T(8,128)S(1)} fusion(f32[16,16,640]{2,1,0:T(8,128)} %copy-done.3), kind=kOutput, calls=%fused_computation.134 | convolution fusion | flops 1572864 | bytes 278528 | tf_op jit(solution)/shard_map/dtn,dsn->dts/dot_general | solution.py:66
  43.6 1.2 fusion.111
  44.8 3.7 %fusion.32 = f32[16,16,512]{2,1,0:T(8,128)} fusion(f32[16,512]{1,0:T(8,128)} %fusion.133, f32[16,16,512]{2,1,0:T(8,128)} %slice.150, f32[16,16,16]{1,2,0:T(8,128)} %copy.61, f32[16,16,16]{2,1,0:T(8,128)S(1)} %fusion.102, f32[16,16,16]{1,2,0:T(8,128)} %copy.58, pred[16,16]{1,0:T(8,128)(4,1)} %iota_compare_fusion.8), kind=kOutput, calls=%fused_computation.49 | convolution fusion | flops 69468160 | bytes 1130752 | tf_op jit(solution)/shard_map/dtsh,dshm->dtm/dot_general | solution.py:69
  48.5 1.8 %copy.84 = bf16[2,8,16,2048]{3,1,2,0:T(8,128)(2,1)S(1)} copy(bf16[2,8,16,2048]{3,2,1,0:T(8,128)(2,1)} %bitcast.40) | data formatting | bytes 2097152
  50.4 1.4 %convolution_convert_fusion = bf16[16,32768]{1,0:T(8,128)(2,1)} fusion(bf16[16,32768]{1,0:T(8,128)(2,1)S(1)} %bitcast.106, s32[16]{0:T(128)S(1)} %copy-done.28, bf16[16]{0:T(256)(128)(2,1)S(1)} %copy-done.31), kind=kOutput, calls=%fused_computation.1 | convolution fusion | flops 17302016 | bytes 2097248 | tf_op jit(solution)/shard_map/dot_general | solution.py:187
  51.8 4.0 %reshape_reshape.4 = bf16[16,512,64]{2,1,0:T(8,128)(2,1)} reshape(bf16[16,32768]{1,0:T(8,128)(2,1)} %convolution_convert_fusion) | data formatting | bytes 2097152 | tf_op jit(solution)/shard_map/reshape;reshape | solution.py:70
  55.8 3.0 %multiply_reduce_fusion.1 = (f32[16,16]{1,0:T(8,128)S(1)}, f32[16,16,512]{2,1,0:T(8,128)S(1)}) fusion(f32[16,16,1168]{2,1,0:T(8,128)} %bitcast.114, f32[16,16,640]{2,1,0:T(8,128)} %copy-done.3, f32[512]{0:T(512)S(1)} %copy-done.25, f32[16,16,512]{2,1,0:T(8,128)} %fusion.32, f32[16,16,512]{2,1,0:T(8,128)} %fusion.111, bf16[16,512,64]{2,1,0:T(8,128)(2,1)} %reshape_reshape.4), kind=kOutput, calls=%fused_computation.120 | convolution fusion | flops 18218752 | bytes 3804160 | tf_op jit(solution)/shard_map/dtn,dmn->dtm/dot_general | solution.py:71
  59.0 1.0 convolution_convert_fusion.8
  60.3 1.0 convolution_convert_fusion.9
  61.3 1.2 collective-permute-start.7
  62.5 1.0 convolution_convert_fusion.10
  63.5 2.0 %collective-permute-start.6 = (bf16[256,512]{1,0:T(8,128)(2,1)}, bf16[256,512]{1,0:T(8,128)(2,1)}, u32[]{:S(2)}, u32[]{:S(2)}) collective-permute-start(bf16[256,512]{1,0:T(8,128)(2,1)} %convolution_convert_fusion.10), channel_id=1, source_target_pairs={{0,1},{1,2},{2,3},{3,0},{4,5},{5,6},{6,7},{7,4},{8,9},{9,10},{10,1... | collective-permute-start | bytes 786440 | tf_op jit(solution)/shard_map/ppermute | solution.py:90
  65.6 3.8 %collective-permute-done.8 = bf16[256,512]{1,0:T(8,128)(2,1)} collective-permute-done((bf16[256,512]{1,0:T(8,128)(2,1)}, bf16[256,512]{1,0:T(8,128)(2,1)}, u32[]{:S(2)}, u32[]{:S(2)}) %collective-permute-start.8) | collective-permute-done | bytes 262176 | tf_op jit(solution)/shard_map/ppermute | solution.py:90
  69.4 3.8 %collective-permute-done.7 = bf16[256,512]{1,0:T(8,128)(2,1)} collective-permute-done((bf16[256,512]{1,0:T(8,128)(2,1)}, bf16[256,512]{1,0:T(8,128)(2,1)}, u32[]{:S(2)}, u32[]{:S(2)}) %collective-permute-start.7) | collective-permute-done | bytes 262176 | tf_op jit(solution)/shard_map/ppermute | solution.py:90
  73.2 2.3 %add_convert_fusion.2 = bf16[256,512]{1,0:T(8,128)(2,1)} fusion(bf16[256,512]{1,0:T(8,128)(2,1)} %collective-permute-done.8, bf16[256,512]{1,0:T(8,128)(2,1)} %collective-permute-done.7, bf16[256,512]{1,0:T(8,128)(2,1)} %collective-permute-done.6, bf16[256,512]{1,0:T(8,128)(2,1)S(1)} %bitcast.99, bf16[256,512]{1,0:T(8,128)(2,1)} %param.15, ...), kind=kOutput, calls=%fused_computation.118 | convolution fusion | flops 135659520 | bytes 2097156 | tf_op jit(solution)/shard_map/dot_general | solution.py:136
  75.5 1.3 %collective-permute-start.9 = (bf16[256,512]{1,0:T(8,128)(2,1)}, bf16[256,512]{1,0:T(8,128)(2,1)S(1)}, u32[]{:S(2)}, u32[]{:S(2)}) collective-permute-start(bf16[256,512]{1,0:T(8,128)(2,1)} %add_convert_fusion.2), channel_id=1, source_target_pairs={{0,16},{1,17},{2,18},{3,19},{4,20},{5,21},{6,22},{7,23},{8,24},{9,... | collective-permute-start | bytes 786440 | tf_op jit(solution)/shard_map/ppermute | solution.py:118
  76.8 2.0 %collective-permute-start.12 = (bf16[256,512]{1,0:T(8,128)(2,1)}, bf16[256,512]{1,0:T(8,128)(2,1)}, u32[]{:S(2)}, u32[]{:S(2)}) collective-permute-start(bf16[256,512]{1,0:T(8,128)(2,1)} %add_convert_fusion.2), channel_id=1, source_target_pairs={{0,17},{1,18},{2,19},{3,16},{4,21},{5,22},{6,23},{7,20},{8,25},{9,... | collective-permute-start | bytes 786440 | tf_op jit(solution)/shard_map/ppermute | solution.py:118
  78.8 2.2 %collective-permute-start.11 = (bf16[256,512]{1,0:T(8,128)(2,1)}, bf16[256,512]{1,0:T(8,128)(2,1)}, u32[]{:S(2)}, u32[]{:S(2)}) collective-permute-start(bf16[256,512]{1,0:T(8,128)(2,1)} %add_convert_fusion.2), channel_id=1, source_target_pairs={{0,18},{1,19},{2,16},{3,17},{4,22},{5,23},{6,20},{7,21},{8,26},{9,... | collective-permute-start | bytes 786440 | tf_op jit(solution)/shard_map/ppermute | solution.py:118
  81.0 2.0 %collective-permute-start.10 = (bf16[256,512]{1,0:T(8,128)(2,1)}, bf16[256,512]{1,0:T(8,128)(2,1)}, u32[]{:S(2)}, u32[]{:S(2)}) collective-permute-start(bf16[256,512]{1,0:T(8,128)(2,1)} %add_convert_fusion.2), channel_id=1, source_target_pairs={{0,19},{1,16},{2,17},{3,18},{4,23},{5,20},{6,21},{7,22},{8,27},{9,... | collective-permute-start | bytes 786440 | tf_op jit(solution)/shard_map/ppermute | solution.py:118
  83.0 2.7 %copy.71 = bf16[16,512,64]{1,2,0:T(8,128)(2,1)} copy(bf16[16,512,64]{2,1,0:T(8,128)(2,1)} %reshape_reshape.4) | data formatting | bytes 2097152 | tf_op jit(solution)/shard_map/reshape;reshape | solution.py:70
  85.7 0.8 collective-permute-done.10
  86.4 1.5 %fusion.13 = f32[256]{0:T(256)S(1)} fusion(bf16[256,2048]{1,0:T(8,128)(2,1)S(1)} %constant_dynamic-update-slice_fusion, bf16[256,512]{1,0:T(8,128)(2,1)S(1)} %collective-permute-done.9, bf16[256,512]{1,0:T(8,128)(2,1)} %collective-permute-done.12, bf16[256,512]{1,0:T(8,128)(2,1)} %collective-permute-done.11, bf16[256,512]{1,0:T(8,128)(2,1)} %collective-permute-done.10, ...), kind=kLoop, calls=%fused_computation.24 | loop fusion | flops 6291200 | bytes 2098177 | tf_op jit(solution)/shard_map/reduce_sum | solution.py:19
  88.0 5.1 %fusion.45 = f32[256,1168]{1,0:T(8,128)S(1)} fusion(f32[256]{0:T(256)S(1)} %add_rsqrt_fusion.2, f32[2048]{0:T(1024)S(1)} %copy-done.19, bf16[256,2048]{1,0:T(8,128)(2,1)S(1)} %constant_dynamic-update-slice_fusion, bf16[256,512]{1,0:T(8,128)(2,1)S(1)} %collective-permute-done.9, bf16[256,512]{1,0:T(8,128)(2,1)} %collective-permute-done.12, ...), kind=kOutput, calls=%fused_computation.66 | convolution fusion | flops 1241120768 | bytes 8086533 | tf_op jit(solution)/shard_map/dot_general | solution.py:227
  93.9 0.9 slice.160
  94.8 0.9 fusion.116
  95.7 0.8 copy.68
  97.0 3.0 %fusion.37 = f32[16,16,512]{2,1,0:T(8,128)S(1)} fusion(f32[16,16,512]{2,1,0:T(8,128)} %slice.160, f32[16,512]{1,0:T(8,128)} %fusion.133, f32[16,16,16]{1,2,0:T(8,128)} %copy.68, f32[16,16,16]{2,1,0:T(8,128)} %fusion.116, f32[16,16,16]{1,2,0:T(8,128)S(1)} %copy.66, pred[16,16]{1,0:T(8,128)(4,1)S(1)} %copy-done.27), kind=kOutput, calls=%fused_computation.50 | convolution fusion | flops 69468160 | bytes 1130752 | tf_op jit(solution)/shard_map/dtsh,dshm->dtm/dot_general | solution.py:69
  100.1 1.8 %multiply_reduce_fusion = (f32[16,16]{1,0:T(8,128)S(1)}, f32[16,16,512]{2,1,0:T(8,128)S(1)}) fusion(f32[16,16,1168]{2,1,0:T(8,128)} %bitcast.110, f32[16,16,640]{2,1,0:T(8,128)S(1)} %divide_multiply_fusion, f32[512]{0:T(512)S(1)} %copy-done.26, f32[16,16,512]{2,1,0:T(8,128)S(1)} %fusion.37, f32[16,16,512]{2,1,0:T(8,128)S(1)} %fusion.107, ...), kind=kOutput, calls=%fused_computation.117 | convolution fusion | flops 18218752 | bytes 3804160 | tf_op jit(solution)/shard_map/dtn,dmn->dtm/dot_general | solution.py:71
  102.1 1.0 convolution_convert_fusion.4
  103.1 1.0 convolution_convert_fusion.5
  104.1 1.0 convolution_convert_fusion.6
  105.4 1.2 collective-permute-start.14
  106.6 2.0 %collective-permute-start.13 = (bf16[256,512]{1,0:T(8,128)(2,1)}, bf16[256,512]{1,0:T(8,128)(2,1)}, u32[]{:S(2)}, u32[]{:S(2)}) collective-permute-start(bf16[256,512]{1,0:T(8,128)(2,1)} %convolution_convert_fusion.6), channel_id=1, source_target_pairs={{0,1},{1,2},{2,3},{3,0},{4,5},{5,6},{6,7},{7,4},{8,9},{9,10},{10,1... | collective-permute-start | bytes 786440 | tf_op jit(solution)/shard_map/ppermute | solution.py:90
  108.9 2.1 %add_convert_fusion = bf16[16,512,64]{1,2,0:T(8,128)(2,1)} fusion(bf16[16,512,64]{1,2,0:T(8,128)(2,1)S(1)} %copy-done.2, f32[16,16,512]{2,1,0:T(8,128)S(1)} %convolution_multiply_fusion, f32[16,512]{1,0:T(8,128)S(1)} %fusion.131, f32[16,16,640]{2,1,0:T(8,128)S(1)} %divide_multiply_fusion), kind=kOutput, calls=%fused_computation.27 | convolution fusion | flops 52428800 | bytes 2785280 | tf_op jit(solution)/shard_map/dsm,dsn->dmn/dot_general | solution.py:77
  111.0 2.7 %copy.73 = bf16[16,512,64]{2,1,0:T(8,128)(2,1)} copy(bf16[16,512,64]{1,2,0:T(8,128)(2,1)} %add_convert_fusion) | data formatting | bytes 2097152 | tf_op jit(solution)/shard_map/convert_element_type | solution.py:82
  113.7 4.3 %convert_element_type.179 = bf16[1,16,16,2048]{3,2,1,0:T(8,128)(2,1)} reshape(bf16[16,512,64]{2,1,0:T(8,128)(2,1)} %copy.73) | data formatting | bytes 2097152 | tf_op jit(solution)/shard_map/convert_element_type | solution.py:82
  118.0 1.0 fusion.122
  119.0 0.6 copy.74
  119.6 1.3 %collective-permute-done.13 = bf16[256,512]{1,0:T(8,128)(2,1)} collective-permute-done((bf16[256,512]{1,0:T(8,128)(2,1)}, bf16[256,512]{1,0:T(8,128)(2,1)}, u32[]{:S(2)}, u32[]{:S(2)}) %collective-permute-start.13) | collective-permute-done | bytes 262176 | tf_op jit(solution)/shard_map/ppermute | solution.py:90
  120.9 2.2 %fusion.101 = bf16[1,256,512]{2,1,0:T(8,128)(2,1)} fusion(bf16[256,512]{1,0:T(8,128)(2,1)} %collective-permute-done.15, bf16[256,512]{1,0:T(8,128)(2,1)} %collective-permute-done.14, bf16[256,512]{1,0:T(8,128)(2,1)} %collective-permute-done.13, bf16[256,512]{1,0:T(8,128)(2,1)S(1)} %copy-done.5, bf16[256,512]{1,0:T(8,128)(2,1)S(1)} %collective-permute-done.9, ...), kind=kOutput, calls=%fused_computation.131 | convolution fusion | flops 135790592 | bytes 2359301 | tf_op jit(solution)/shard_map/dot_general | solution.py:136
  (124 shorter events, 6.4 us)
Async XLA Ops:
  0.6 58.3 %copy-start = (bf16[1,512,2048]{2,1,0:T(8,128)(2,1)S(1)}, bf16[1,512,2048]{2,1,0:T(8,128)(2,1)}, u32[]{:S(2)}) copy-start(bf16[1,512,2048]{2,1,0:T(8,128)(2,1)} %param.24) | copy-start | bytes 6291460
  0.6 25.5 %collective-permute-start = (bf16[256,512]{1,0:T(8,128)(2,1)}, bf16[256,512]{1,0:T(8,128)(2,1)}, u32[]{:S(2)}, u32[]{:S(2)}) collective-permute-start(bf16[256,512]{1,0:T(8,128)(2,1)} %param.15), channel_id=1, source_target_pairs={{0,3},{1,0},{2,1},{3,2},{4,7},{5,4},{6,5},{7,6},{8,11},{9,8},{10,9... | collective-permute-start | bytes 786440 | tf_op jit(solution)/shard_map/ppermute | solution.py:90
  4.6 22.5 %collective-permute-start.1 = (bf16[256,512]{1,0:T(8,128)(2,1)}, bf16[256,512]{1,0:T(8,128)(2,1)}, u32[]{:S(2)}, u32[]{:S(2)}) collective-permute-start(bf16[256,512]{1,0:T(8,128)(2,1)} %param.15), channel_id=1, source_target_pairs={{0,2},{1,3},{2,0},{3,1},{4,6},{5,7},{6,4},{7,5},{8,10},{9,11},{10,... | collective-permute-start | bytes 786440 | tf_op jit(solution)/shard_map/ppermute | solution.py:90
  8.8 15.7 %collective-permute-start.5 = (bf16[4,3,640]{2,0,1:T(4,128)(2,1)S(1)}, bf16[4,3,640]{2,0,1:T(4,128)(2,1)S(1)}, u32[]{:S(2)}, u32[]{:S(2)}) collective-permute-start(bf16[4,3,640]{2,0,1:T(4,128)(2,1)S(1)} %bitcast.119), channel_id=1, source_target_pairs={{0,12},{4,0},{8,4},{12,8},{1,13},{5,1},{9,5},{13,9},{2,14},{6,2},{... | collective-permute-start | bytes 46088 | tf_op jit(solution)/shard_map/ppermute | solution.py:90
  12.5 12.7 %collective-permute-start.4 = (bf16[4,3,640]{2,0,1:T(4,128)(2,1)S(1)}, bf16[4,3,640]{2,0,1:T(4,128)(2,1)S(1)}, u32[]{:S(2)}, u32[]{:S(2)}) collective-permute-start(bf16[4,3,640]{2,0,1:T(4,128)(2,1)S(1)} %bitcast.118), channel_id=1, source_target_pairs={{0,8},{4,12},{8,0},{12,4},{1,9},{5,13},{9,1},{13,5},{2,10},{6,14},... | collective-permute-start | bytes 46088 | tf_op jit(solution)/shard_map/ppermute | solution.py:90
  12.5 12.7 %collective-permute-start.3 = (bf16[4,3,640]{2,0,1:T(4,128)(2,1)S(1)}, bf16[4,3,640]{2,0,1:T(4,128)(2,1)S(1)}, u32[]{:S(2)}, u32[]{:S(2)}) collective-permute-start(bf16[4,3,640]{2,0,1:T(4,128)(2,1)S(1)} %bitcast.117), channel_id=1, source_target_pairs={{0,4},{4,8},{8,12},{12,0},{1,5},{5,9},{9,13},{13,1},{2,6},{6,10},{... | collective-permute-start | bytes 46088 | tf_op jit(solution)/shard_map/ppermute | solution.py:90
  15.9 6.5 %copy-start.32 = (s32[16]{0:T(128)S(1)}, s32[16]{0:T(128)}, u32[]{:S(2)}) copy-start(s32[16]{0:T(128)} %param.29) | copy-start | bytes 196
  15.9 6.5 %copy-start.14 = (f32[1,4,640]{2,1,0:T(4,128)S(1)}, f32[1,4,640]{2,1,0:T(4,128)}, u32[]{:S(2)}) copy-start(f32[1,4,640]{2,1,0:T(4,128)} %param.18) | copy-start | bytes 30724
  15.9 7.2 %copy-start.17 = (f32[1,2048]{1,0:T(1,128)S(1)}, f32[1,2048]{1,0:T(1,128)}, u32[]{:S(2)}) copy-start(f32[1,2048]{1,0:T(1,128)} %param.16) | copy-start | bytes 24580
  15.9 7.8 %copy-start.29 = (f32[1,16]{1,0:T(1,128)S(1)}, f32[1,16]{1,0:T(1,128)}, u32[]{:S(2)}) copy-start(f32[1,16]{1,0:T(1,128)} %param.22) | copy-start | bytes 196
  15.9 8.6 %copy-start.20 = (f32[1,640]{1,0:T(1,128)S(1)}, f32[1,640]{1,0:T(1,128)}, u32[]{:S(2)}) copy-start(f32[1,640]{1,0:T(1,128)} %param.19) | copy-start | bytes 7684
  15.9 8.6 %copy-start.4 = (bf16[256,512]{1,0:T(8,128)(2,1)S(1)}, bf16[256,512]{1,0:T(8,128)(2,1)}, u32[]{:S(2)}) copy-start(bf16[256,512]{1,0:T(8,128)(2,1)} %param.15) | copy-start | bytes 786436
  17.5 31.0 %all-to-all-start = ((bf16[16,16,2048]{2,1,0:T(8,128)(2,1)}), bf16[16,16,2048]{2,1,0:T(8,128)(2,1)}, u32[]{:S(2)}, u32[]{:S(2)}) async-start(bf16[16,16,2048]{2,1,0:T(8,128)(2,1)} %bitcast.39), calls=%async_computation | async-start | bytes 2097152 | tf_op jit(solution)/shard_map/all_to_all | solution.py:191
  22.4 15.9 %copy-start.30 = (bf16[16]{0:T(256)(128)(2,1)}, bf16[16]{0:T(256)(128)(2,1)S(1)}, u32[]{:S(2)}) copy-start(bf16[16]{0:T(256)(128)(2,1)S(1)} %compare_convert_fusion) | copy-start | bytes 100
  22.4 16.0 %copy-start.10 = (f32[640]{0:T(1024)}, f32[640]{0:T(1024)S(1)}, u32[]{:S(2)}) copy-start(f32[640]{0:T(1024)S(1)} %get-tuple-element.14) | copy-start | bytes 7684
  22.4 16.0 %copy-start.12 = (f32[640]{0:T(1024)}, f32[640]{0:T(1024)S(1)}, u32[]{:S(2)}) copy-start(f32[640]{0:T(1024)S(1)} %get-tuple-element.15) | copy-start | bytes 7684
  23.2 15.2 %copy-start.18 = (f32[2048]{0:T(1024)}, f32[2048]{0:T(1024)S(1)}, u32[]{:S(2)}) copy-start(f32[2048]{0:T(1024)S(1)} %fusion.141) | copy-start | bytes 24580
  24.5 7.7 %collective-permute-start.2 = (bf16[256,512]{1,0:T(8,128)(2,1)S(1)}, bf16[256,512]{1,0:T(8,128)(2,1)}, u32[]{:S(2)}, u32[]{:S(2)}) collective-permute-start(bf16[256,512]{1,0:T(8,128)(2,1)S(1)} %copy-done.4), channel_id=1, source_target_pairs={{0,1},{1,2},{2,3},{3,0},{4,5},{5,6},{6,7},{7,4},{8,9},{9,10},{10,1... | collective-permute-start | bytes 786440 | tf_op jit(solution)/shard_map/ppermute | solution.py:90
  33.6 4.9 %copy-start.6 = (f32[16,3,640]{2,1,0:T(4,128)S(1)}, f32[16,3,640]{2,1,0:T(4,128)}, u32[]{:S(2)}) copy-start(f32[16,3,640]{2,1,0:T(4,128)} %reshape.318) | copy-start | bytes 368644
  38.4 2.4 %copy-start.9 = (f32[256,1168]{1,0:T(8,128)}, f32[256,1168]{1,0:T(8,128)S(1)}, u32[]{:S(2)}) copy-start(f32[256,1168]{1,0:T(8,128)S(1)} %fusion.47) | copy-start | bytes 3588100
  38.4 2.3 %copy-start.21 = (f32[1,16]{1,0:T(1,128)S(1)}, f32[1,16]{1,0:T(1,128)}, u32[]{:S(2)}) copy-start(f32[1,16]{1,0:T(1,128)} %param.21) | copy-start | bytes 196
  38.4 2.3 %copy-start.23 = (f32[1,16]{1,0:T(1,128)S(1)}, f32[1,16]{1,0:T(1,128)}, u32[]{:S(2)}) copy-start(f32[1,16]{1,0:T(1,128)} %param.20) | copy-start | bytes 196
  39.0 0.8 copy-start.3
  48.5 1.8 %copy-start.28 = (s32[16]{0:T(128)S(1)}, s32[16]{0:T(128)}, u32[]{:S(2)}) copy-start(s32[16]{0:T(128)} %get-tuple-element.24) | copy-start | bytes 196
  48.5 1.8 %copy-start.31 = (bf16[16]{0:T(256)(128)(2,1)S(1)}, bf16[16]{0:T(256)(128)(2,1)}, u32[]{:S(2)}) copy-start(bf16[16]{0:T(256)(128)(2,1)} %copy-done.30) | copy-start | bytes 100
  51.8 4.0 %copy-start.25 = (f32[512]{0:T(512)S(1)}, f32[512]{0:T(512)}, u32[]{:S(2)}) copy-start(f32[512]{0:T(512)} %mul.349) | copy-start | bytes 6148
  55.8 3.0 %copy-start.15 = (f32[1,512]{1,0:T(1,128)S(1)}, f32[1,512]{1,0:T(1,128)}, u32[]{:S(2)}) copy-start(f32[1,512]{1,0:T(1,128)} %param.23) | copy-start | bytes 6148
  60.0 9.4 %collective-permute-start.8 = (bf16[256,512]{1,0:T(8,128)(2,1)}, bf16[256,512]{1,0:T(8,128)(2,1)}, u32[]{:S(2)}, u32[]{:S(2)}) collective-permute-start(bf16[256,512]{1,0:T(8,128)(2,1)} %convolution_convert_fusion.8), channel_id=1, source_target_pairs={{0,3},{1,0},{2,1},{3,2},{4,7},{5,4},{6,5},{7,6},{8,11},{9,8},{10,9... | collective-permute-start | bytes 786440 | tf_op jit(solution)/shard_map/ppermute | solution.py:90
  61.3 11.9 %collective-permute-start.7 = (bf16[256,512]{1,0:T(8,128)(2,1)}, bf16[256,512]{1,0:T(8,128)(2,1)}, u32[]{:S(2)}, u32[]{:S(2)}) collective-permute-start(bf16[256,512]{1,0:T(8,128)(2,1)} %convolution_convert_fusion.9), channel_id=1, source_target_pairs={{0,2},{1,3},{2,0},{3,1},{4,6},{5,7},{6,4},{7,5},{8,10},{9,11},{10,... | collective-permute-start | bytes 786440 | tf_op jit(solution)/shard_map/ppermute | solution.py:90
  63.5 9.7 %collective-permute-start.6 = (bf16[256,512]{1,0:T(8,128)(2,1)}, bf16[256,512]{1,0:T(8,128)(2,1)}, u32[]{:S(2)}, u32[]{:S(2)}) collective-permute-start(bf16[256,512]{1,0:T(8,128)(2,1)} %convolution_convert_fusion.10), channel_id=1, source_target_pairs={{0,1},{1,2},{2,3},{3,0},{4,5},{5,6},{6,7},{7,4},{8,9},{9,10},{10,1... | collective-permute-start | bytes 786440 | tf_op jit(solution)/shard_map/ppermute | solution.py:90
  75.5 10.2 %collective-permute-start.9 = (bf16[256,512]{1,0:T(8,128)(2,1)}, bf16[256,512]{1,0:T(8,128)(2,1)S(1)}, u32[]{:S(2)}, u32[]{:S(2)}) collective-permute-start(bf16[256,512]{1,0:T(8,128)(2,1)} %add_convert_fusion.2), channel_id=1, source_target_pairs={{0,16},{1,17},{2,18},{3,19},{4,20},{5,21},{6,22},{7,23},{8,24},{9,... | collective-permute-start | bytes 786440 | tf_op jit(solution)/shard_map/ppermute | solution.py:118
  76.8 8.9 %collective-permute-start.12 = (bf16[256,512]{1,0:T(8,128)(2,1)}, bf16[256,512]{1,0:T(8,128)(2,1)}, u32[]{:S(2)}, u32[]{:S(2)}) collective-permute-start(bf16[256,512]{1,0:T(8,128)(2,1)} %add_convert_fusion.2), channel_id=1, source_target_pairs={{0,17},{1,18},{2,19},{3,16},{4,21},{5,22},{6,23},{7,20},{8,25},{9,... | collective-permute-start | bytes 786440 | tf_op jit(solution)/shard_map/ppermute | solution.py:118
  78.8 6.9 %collective-permute-start.11 = (bf16[256,512]{1,0:T(8,128)(2,1)}, bf16[256,512]{1,0:T(8,128)(2,1)}, u32[]{:S(2)}, u32[]{:S(2)}) collective-permute-start(bf16[256,512]{1,0:T(8,128)(2,1)} %add_convert_fusion.2), channel_id=1, source_target_pairs={{0,18},{1,19},{2,16},{3,17},{4,22},{5,23},{6,20},{7,21},{8,26},{9,... | collective-permute-start | bytes 786440 | tf_op jit(solution)/shard_map/ppermute | solution.py:118
  81.0 5.5 %collective-permute-start.10 = (bf16[256,512]{1,0:T(8,128)(2,1)}, bf16[256,512]{1,0:T(8,128)(2,1)}, u32[]{:S(2)}, u32[]{:S(2)}) collective-permute-start(bf16[256,512]{1,0:T(8,128)(2,1)} %add_convert_fusion.2), channel_id=1, source_target_pairs={{0,19},{1,16},{2,17},{3,18},{4,23},{5,20},{6,21},{7,22},{8,27},{9,... | collective-permute-start | bytes 786440 | tf_op jit(solution)/shard_map/ppermute | solution.py:118
  83.0 5.0 %copy-start.19 = (f32[2048]{0:T(1024)S(1)}, f32[2048]{0:T(1024)}, u32[]{:S(2)}) copy-start(f32[2048]{0:T(1024)} %copy-done.18) | copy-start | bytes 24580
  88.0 5.3 %copy-start.22 = (f32[1,16]{1,0:T(1,128)S(1)}, f32[1,16]{1,0:T(1,128)}, u32[]{:S(2)}) copy-start(f32[1,16]{1,0:T(1,128)} %param.21) | copy-start | bytes 196
  88.0 5.3 %copy-start.24 = (f32[1,16]{1,0:T(1,128)S(1)}, f32[1,16]{1,0:T(1,128)}, u32[]{:S(2)}) copy-start(f32[1,16]{1,0:T(1,128)} %param.20) | copy-start | bytes 196
  88.0 5.4 %copy-start.7 = (f32[16,3,640]{2,1,0:T(4,128)S(1)}, f32[16,3,640]{2,1,0:T(4,128)}, u32[]{:S(2)}) copy-start(f32[16,3,640]{2,1,0:T(4,128)} %reshape.318) | copy-start | bytes 368644
  88.0 5.4 %copy-start.11 = (f32[640]{0:T(1024)S(1)}, f32[640]{0:T(1024)}, u32[]{:S(2)}) copy-start(f32[640]{0:T(1024)} %copy-done.10) | copy-start | bytes 7684
  88.0 5.4 %copy-start.13 = (f32[640]{0:T(1024)S(1)}, f32[640]{0:T(1024)}, u32[]{:S(2)}) copy-start(f32[640]{0:T(1024)} %copy-done.12) | copy-start | bytes 7684
  93.2 1.6 %copy-start.8 = (f32[256,1168]{1,0:T(8,128)}, f32[256,1168]{1,0:T(8,128)S(1)}, u32[]{:S(2)}) copy-start(f32[256,1168]{1,0:T(8,128)S(1)} %fusion.45) | copy-start | bytes 3588100
  93.9 3.1 %copy-start.27 = (pred[16,16]{1,0:T(8,128)(4,1)S(1)}, pred[16,16]{1,0:T(8,128)(4,1)}, u32[]{:S(2)}) copy-start(pred[16,16]{1,0:T(8,128)(4,1)} %iota_compare_fusion.8) | copy-start | bytes 772
  97.0 3.1 %copy-start.1 = (bf16[16,512,64]{2,1,0:T(8,128)(2,1)S(1)}, bf16[16,512,64]{2,1,0:T(8,128)(2,1)}, u32[]{:S(2)}) copy-start(bf16[16,512,64]{2,1,0:T(8,128)(2,1)} %reshape_reshape.4) | copy-start | bytes 3145732
  97.0 3.1 %copy-start.26 = (f32[512]{0:T(512)S(1)}, f32[512]{0:T(512)}, u32[]{:S(2)}) copy-start(f32[512]{0:T(512)} %mul.349) | copy-start | bytes 6148
  100.1 1.9 %copy-start.16 = (f32[1,512]{1,0:T(1,128)S(1)}, f32[1,512]{1,0:T(1,128)}, u32[]{:S(2)}) copy-start(f32[1,512]{1,0:T(1,128)} %param.23) | copy-start | bytes 6148
  102.1 6.8 %copy-start.2 = (bf16[16,512,64]{1,2,0:T(8,128)(2,1)S(1)}, bf16[16,512,64]{1,2,0:T(8,128)(2,1)}, u32[]{:S(2)}) copy-start(bf16[16,512,64]{1,2,0:T(8,128)(2,1)} %copy.71) | copy-start | bytes 3145732
  105.3 14.3 %collective-permute-start.15 = (bf16[256,512]{1,0:T(8,128)(2,1)}, bf16[256,512]{1,0:T(8,128)(2,1)}, u32[]{:S(2)}, u32[]{:S(2)}) collective-permute-start(bf16[256,512]{1,0:T(8,128)(2,1)} %convolution_convert_fusion.4), channel_id=1, source_target_pairs={{0,3},{1,0},{2,1},{3,2},{4,7},{5,4},{6,5},{7,6},{8,11},{9,8},{10,9... | collective-permute-start | bytes 786440 | tf_op jit(solution)/shard_map/ppermute | solution.py:90
  105.4 14.3 %collective-permute-start.14 = (bf16[256,512]{1,0:T(8,128)(2,1)}, bf16[256,512]{1,0:T(8,128)(2,1)}, u32[]{:S(2)}, u32[]{:S(2)}) collective-permute-start(bf16[256,512]{1,0:T(8,128)(2,1)} %convolution_convert_fusion.5), channel_id=1, source_target_pairs={{0,2},{1,3},{2,0},{3,1},{4,6},{5,7},{6,4},{7,5},{8,10},{9,11},{10,... | collective-permute-start | bytes 786440 | tf_op jit(solution)/shard_map/ppermute | solution.py:90
  106.6 14.4 %collective-permute-start.13 = (bf16[256,512]{1,0:T(8,128)(2,1)}, bf16[256,512]{1,0:T(8,128)(2,1)}, u32[]{:S(2)}, u32[]{:S(2)}) collective-permute-start(bf16[256,512]{1,0:T(8,128)(2,1)} %convolution_convert_fusion.6), channel_id=1, source_target_pairs={{0,1},{1,2},{2,3},{3,0},{4,5},{5,6},{6,7},{7,4},{8,9},{9,10},{10,1... | collective-permute-start | bytes 786440 | tf_op jit(solution)/shard_map/ppermute | solution.py:90
  113.7 7.2 %copy-start.5 = (bf16[256,512]{1,0:T(8,128)(2,1)S(1)}, bf16[256,512]{1,0:T(8,128)(2,1)}, u32[]{:S(2)}) copy-start(bf16[256,512]{1,0:T(8,128)(2,1)} %param.15) | copy-start | bytes 786436

commit v5 on v4

--- a/solution.py
+++ b/solution.py
@@ -187,12 +187,12 @@
         picked = jnp.dot(picker, rows.reshape(rows.shape[0], -1), preferred_element_type=jnp.float32)
         return picked.astype(jnp.bfloat16).reshape((picker.shape[0],) + rows.shape[1:])
 
-    send_state = select_rows(send_pick, kept_state[0])
+    send_state = kept_state[0][send_index]
     got_state = lax.all_to_all(send_state, "dp", split_axis=0, concat_axis=0, tiled=True)
     by_shift = (jnp.arange(dp_count) + dp_idx) % dp_count
     shift_order = jnp.take(send_index.reshape(dp_count, capacity), by_shift, axis=0).reshape(-1)
     shift_pick = (shift_order[:, None] == jnp.arange(slot_count)[None, :]).astype(jnp.bfloat16)
-    send_conv = select_rows(shift_pick, kept_conv[0])
+    send_conv = kept_conv[0][shift_order]
     conv_chunks = [send_conv[:capacity]]
     for steps in range(1, dp_count):
         conv_chunks.append(shifted(send_conv[steps * capacity : (steps + 1) * capacity], "dp", steps))

time: 124 us -> 123 us (level)
    gather x0 -> x2, local copies, waits for them, and re-layouts: none -> 3.48 us  [the longest x1 2.85 us: per_device(): send_state = kept_state[0][send_index]]
    unnamed x75 -> x73, local copies, waits for them, and re-layouts: 10.6 us -> 7.21 us
where the time goes in v5:
time: 123 us; the launch traced here: 122 us
  matrix products  39.9 us (32%)
  local copies, waits for them, and re-layouts  33.4 us (27%)
  starting transfers between devices  28.1 us (23%)
  waiting for transfers between devices  13.7 us (11%)
  other arithmetic  5.86 us (5%)
  between operations  1.32 us (1%)
    ppermute x12, starting transfers between devices, shifted(): lax.ppermute(value, axis, [(source, (source + steps) % count) for source...  16.6 us
    ppermute x12, waiting for transfers between devices, shifted(): lax.ppermute(value, axis, [(source, (source + steps) % count) for source...  13 us
    dot_general x8, matrix products, scatter_sum(): jnp.dot(gnormed, weight_block, preferred_element_type=jnp.float32)  10.5 us
    dot_general x2, matrix products, per_device(): jnp.dot(normed, proj_rotated, preferred_element_type=jnp.float32)  9.87 us
    ppermute x4, starting transfers between devices, gather_from_behind(): parts.append(lax.ppermute(value, ('section', 'mp'), pairs))  7.3 us
    unnamed x73, local copies, waits for them, and re-layouts  7.21 us
    convert_element_type x2, local copies, waits for them, and re-layouts, mix_channels(): end_state.reshape(doc_count, head_count, head_dim * state_width)  6.99 us
    dot_general x2, matrix products, mix_channels(): jnp.einsum('dtsh,dshm->dtm', weights, spread, precision=one_pass)  6.78 us
  transfers between devices with their start and end apart: 17, of which 5 were waited for; matrix products, arithmetic and copies ran while one was open for 36% of the time, Pallas kernels for 0%

profile of v5, /device:TPU:0, one launch (start us, length us, event | category | flops | bytes accessed | tf_op | source)
XLA Modules:
  0.0 122.4 jit_solution(4014545508206084426)
XLA Ops:
  0.6 3.9 %collective-permute-start = (bf16[256,512]{1,0:T(8,128)(2,1)}, bf16[256,512]{1,0:T(8,128)(2,1)}, u32[]{:S(2)}, u32[]{:S(2)}) collective-permute-start(bf16[256,512]{1,0:T(8,128)(2,1)} %param.15), channel_id=1, source_target_pairs={{0,3},{1,0},{2,1},{3,2},{4,7},{5,4},{6,5},{7,6},{8,11},{9,8},{10,9... | collective-permute-start | bytes 786440 | tf_op jit(solution)/shard_map/ppermute | solution.py:90
  5.1 0.9 copy.102
  6.0 0.7 broadcast_in_dim.47
  6.7 0.7 reshape.349
  8.7 0.6 gather_fusion.1
  9.4 3.7 %collective-permute-start.5 = (bf16[4,3,640]{2,1,0:T(4,128)(2,1)S(1)}, bf16[4,3,640]{2,1,0:T(4,128)(2,1)S(1)}, u32[]{:S(2)}, u32[]{:S(2)}) collective-permute-start(bf16[4,3,640]{2,1,0:T(4,128)(2,1)S(1)} %get-tuple-element.23), channel_id=1, source_target_pairs={{0,12},{4,0},{8,4},{12,8},{1,13},{5,1},{9,5},{13,9},{2,14},{6,2},{... | collective-permute-start | bytes 46088 | tf_op jit(solution)/shard_map/ppermute | solution.py:90
  13.0 1.0 collective-permute-start.3
  14.1 2.9 %gather_fusion.2 = bf16[16,16,2048]{2,1,0:T(8,128)(2,1)} fusion(bf16[16,16,2048]{2,1,0:T(8,128)(2,1)} %bitcast.100, s32[1024]{0:T(1024)S(1)} %pad_clamp_fusion), kind=kCustom, calls=%fused_computation.2 | custom fusion | bytes 2097216 | tf_op jit(solution)/shard_map/gather | solution.py:190
  17.0 4.2 %all-to-all-start = ((bf16[16,16,2048]{2,1,0:T(8,128)(2,1)}), bf16[16,16,2048]{2,1,0:T(8,128)(2,1)}, u32[]{:S(2)}, u32[]{:S(2)}) async-start(bf16[16,16,2048]{2,1,0:T(8,128)(2,1)} %gather_fusion.2), calls=%async_computation | async-start | bytes 2097152 | tf_op jit(solution)/shard_map/all_to_all | solution.py:191
  21.2 0.6 iota_compare_fusion.6
  21.9 0.6 fusion.126
  22.6 0.6 bitcast_add_fusion
  23.3 0.7 mul.349
  24.0 0.6 collective-permute-start.2
  24.9 0.7 reshape.356
  25.7 1.0 constant_dynamic-update-slice_fusion.3
  26.7 1.0 constant_dynamic-update-slice_fusion.2
  27.7 4.0 %collective-permute-done.2 = bf16[256,512]{1,0:T(8,128)(2,1)} collective-permute-done((bf16[256,512]{1,0:T(8,128)(2,1)S(1)}, bf16[256,512]{1,0:T(8,128)(2,1)}, u32[]{:S(2)}, u32[]{:S(2)}) %collective-permute-start.2) | collective-permute-done | bytes 262176 | tf_op jit(solution)/shard_map/ppermute | solution.py:90
  31.7 1.0 constant_dynamic-update-slice_fusion.1
  33.0 4.7 %fusion.47 = f32[256,1168]{1,0:T(8,128)S(1)} fusion(bf16[256,2048]{1,0:T(8,128)(2,1)S(1)} %constant_dynamic-update-slice_fusion, f32[2048]{0:T(1024)S(1)} %fusion.134, f32[256]{0:T(256)S(1)} %add_rsqrt_fusion.3, s32[]{:T(128)S(6)} %select_n.179, bf16[2048,1168]{0,1:T(8,128)(2,1)} %bitcast.119), kind=kOutput, calls=%fused_computation.67 | convolution fusion | flops 1236402176 | bytes 7037956 | tf_op jit(solution)/shard_map/dot_general | solution.py:227
  38.4 0.8 copy-done.3
  39.2 0.9 slice.141
  40.2 0.8 copy.61
  41.0 0.8 copy.58
  41.8 1.3 %fusion.102 = f32[16,16,16]{2,1,0:T(8,128)S(1)} fusion(f32[16,16,640]{2,1,0:T(8,128)} %copy-done.3), kind=kOutput, calls=%fused_computation.134 | convolution fusion | flops 1572864 | bytes 278528 | tf_op jit(solution)/shard_map/dtn,dsn->dts/dot_general | solution.py:66
  43.1 1.2 fusion.111
  44.2 3.7 %fusion.32 = f32[16,16,512]{2,1,0:T(8,128)} fusion(f32[16,512]{1,0:T(8,128)} %fusion.126, f32[16,16,512]{2,1,0:T(8,128)} %slice.141, f32[16,16,16]{1,2,0:T(8,128)} %copy.61, f32[16,16,16]{2,1,0:T(8,128)S(1)} %fusion.102, f32[16,16,16]{1,2,0:T(8,128)} %copy.58, pred[16,16]{1,0:T(8,128)(4,1)} %iota_compare_fusion.6), kind=kOutput, calls=%fused_computation.49 | convolution fusion | flops 69468160 | bytes 1130752 | tf_op jit(solution)/shard_map/dtsh,dshm->dtm/dot_general | solution.py:69
  48.0 1.8 %copy.82 = bf16[2,8,16,2048]{3,1,2,0:T(8,128)(2,1)S(1)} copy(bf16[2,8,16,2048]{3,2,1,0:T(8,128)(2,1)} %bitcast.32) | data formatting | bytes 2097152
  49.8 1.4 %convolution_convert_fusion = bf16[16,32768]{1,0:T(8,128)(2,1)} fusion(bf16[16,32768]{1,0:T(8,128)(2,1)S(1)} %bitcast.99, s32[16]{0:T(128)S(1)} %copy-done.30, bf16[16]{0:T(256)(128)(2,1)S(1)} %copy-done.29), kind=kOutput, calls=%fused_computation.3 | convolution fusion | flops 17302016 | bytes 2097248 | tf_op jit(solution)/shard_map/dot_general | solution.py:187
  51.3 4.0 %reshape_reshape.4 = bf16[16,512,64]{2,1,0:T(8,128)(2,1)} reshape(bf16[16,32768]{1,0:T(8,128)(2,1)} %convolution_convert_fusion) | data formatting | bytes 2097152 | tf_op jit(solution)/shard_map/reshape;reshape | solution.py:70
  55.3 3.0 %multiply_reduce_fusion.1 = (f32[16,16]{1,0:T(8,128)S(1)}, f32[16,16,512]{2,1,0:T(8,128)S(1)}) fusion(f32[16,16,1168]{2,1,0:T(8,128)} %bitcast.107, f32[16,16,640]{2,1,0:T(8,128)} %copy-done.3, f32[512]{0:T(512)S(1)} %copy-done.25, f32[16,16,512]{2,1,0:T(8,128)} %fusion.32, f32[16,16,512]{2,1,0:T(8,128)} %fusion.111, bf16[16,512,64]{2,1,0:T(8,128)(2,1)} %reshape_reshape.4), kind=kOutput, calls=%fused_computation.120 | convolution fusion | flops 18218752 | bytes 3804160 | tf_op jit(solution)/shard_map/dtn,dmn->dtm/dot_general | solution.py:71
  58.4 1.0 convolution_convert_fusion.6
  59.8 1.0 convolution_convert_fusion.7
  60.8 1.2 collective-permute-start.7
  62.0 1.0 convolution_convert_fusion.8
  63.0 2.0 %collective-permute-start.6 = (bf16[256,512]{1,0:T(8,128)(2,1)}, bf16[256,512]{1,0:T(8,128)(2,1)}, u32[]{:S(2)}, u32[]{:S(2)}) collective-permute-start(bf16[256,512]{1,0:T(8,128)(2,1)} %convolution_convert_fusion.8), channel_id=1, source_target_pairs={{0,1},{1,2},{2,3},{3,0},{4,5},{5,6},{6,7},{7,4},{8,9},{9,10},{10,1... | collective-permute-start | bytes 786440 | tf_op jit(solution)/shard_map/ppermute | solution.py:90
  65.0 3.8 %collective-permute-done.8 = bf16[256,512]{1,0:T(8,128)(2,1)} collective-permute-done((bf16[256,512]{1,0:T(8,128)(2,1)}, bf16[256,512]{1,0:T(8,128)(2,1)}, u32[]{:S(2)}, u32[]{:S(2)}) %collective-permute-start.8) | collective-permute-done | bytes 262176 | tf_op jit(solution)/shard_map/ppermute | solution.py:90
  68.8 3.8 %collective-permute-done.7 = bf16[256,512]{1,0:T(8,128)(2,1)} collective-permute-done((bf16[256,512]{1,0:T(8,128)(2,1)}, bf16[256,512]{1,0:T(8,128)(2,1)}, u32[]{:S(2)}, u32[]{:S(2)}) %collective-permute-start.7) | collective-permute-done | bytes 262176 | tf_op jit(solution)/shard_map/ppermute | solution.py:90
  72.7 2.3 %add_convert_fusion.2 = bf16[256,512]{1,0:T(8,128)(2,1)} fusion(bf16[256,512]{1,0:T(8,128)(2,1)} %collective-permute-done.8, bf16[256,512]{1,0:T(8,128)(2,1)} %collective-permute-done.7, bf16[256,512]{1,0:T(8,128)(2,1)} %collective-permute-done.6, bf16[256,512]{1,0:T(8,128)(2,1)S(1)} %bitcast.94, bf16[256,512]{1,0:T(8,128)(2,1)} %param.15, ...), kind=kOutput, calls=%fused_computation.118 | convolution fusion | flops 135659520 | bytes 2097156 | tf_op jit(solution)/shard_map/dot_general | solution.py:136
  74.9 1.3 %collective-permute-start.9 = (bf16[256,512]{1,0:T(8,128)(2,1)}, bf16[256,512]{1,0:T(8,128)(2,1)S(1)}, u32[]{:S(2)}, u32[]{:S(2)}) collective-permute-start(bf16[256,512]{1,0:T(8,128)(2,1)} %add_convert_fusion.2), channel_id=1, source_target_pairs={{0,16},{1,17},{2,18},{3,19},{4,20},{5,21},{6,22},{7,23},{8,24},{9,... | collective-permute-start | bytes 786440 | tf_op jit(solution)/shard_map/ppermute | solution.py:118
  76.2 2.0 %collective-permute-start.12 = (bf16[256,512]{1,0:T(8,128)(2,1)}, bf16[256,512]{1,0:T(8,128)(2,1)}, u32[]{:S(2)}, u32[]{:S(2)}) collective-permute-start(bf16[256,512]{1,0:T(8,128)(2,1)} %add_convert_fusion.2), channel_id=1, source_target_pairs={{0,17},{1,18},{2,19},{3,16},{4,21},{5,22},{6,23},{7,20},{8,25},{9,... | collective-permute-start | bytes 786440 | tf_op jit(solution)/shard_map/ppermute | solution.py:118
  78.2 2.0 %collective-permute-start.11 = (bf16[256,512]{1,0:T(8,128)(2,1)}, bf16[256,512]{1,0:T(8,128)(2,1)}, u32[]{:S(2)}, u32[]{:S(2)}) collective-permute-start(bf16[256,512]{1,0:T(8,128)(2,1)} %add_convert_fusion.2), channel_id=1, source_target_pairs={{0,18},{1,19},{2,16},{3,17},{4,22},{5,23},{6,20},{7,21},{8,26},{9,... | collective-permute-start | bytes 786440 | tf_op jit(solution)/shard_map/ppermute | solution.py:118
  80.2 2.0 %collective-permute-start.10 = (bf16[256,512]{1,0:T(8,128)(2,1)}, bf16[256,512]{1,0:T(8,128)(2,1)}, u32[]{:S(2)}, u32[]{:S(2)}) collective-permute-start(bf16[256,512]{1,0:T(8,128)(2,1)} %add_convert_fusion.2), channel_id=1, source_target_pairs={{0,19},{1,16},{2,17},{3,18},{4,23},{5,20},{6,21},{7,22},{8,27},{9,... | collective-permute-start | bytes 786440 | tf_op jit(solution)/shard_map/ppermute | solution.py:118
  82.2 2.7 %copy.71 = bf16[16,512,64]{1,2,0:T(8,128)(2,1)} copy(bf16[16,512,64]{2,1,0:T(8,128)(2,1)} %reshape_reshape.4) | data formatting | bytes 2097152 | tf_op jit(solution)/shard_map/reshape;reshape | solution.py:70
  85.0 0.8 collective-permute-done.10
  85.7 1.5 %fusion.13 = f32[256]{0:T(256)S(1)} fusion(bf16[256,2048]{1,0:T(8,128)(2,1)S(1)} %constant_dynamic-update-slice_fusion, bf16[256,512]{1,0:T(8,128)(2,1)S(1)} %collective-permute-done.9, bf16[256,512]{1,0:T(8,128)(2,1)} %collective-permute-done.12, bf16[256,512]{1,0:T(8,128)(2,1)} %collective-permute-done.11, bf16[256,512]{1,0:T(8,128)(2,1)} %collective-permute-done.10, ...), kind=kLoop, calls=%fused_computation.24 | loop fusion | flops 6291200 | bytes 2098177 | tf_op jit(solution)/shard_map/reduce_sum | solution.py:19
  87.3 5.1 %fusion.45 = f32[256,1168]{1,0:T(8,128)S(1)} fusion(f32[256]{0:T(256)S(1)} %add_rsqrt_fusion.2, f32[2048]{0:T(1024)S(1)} %copy-done.19, bf16[256,2048]{1,0:T(8,128)(2,1)S(1)} %constant_dynamic-update-slice_fusion, bf16[256,512]{1,0:T(8,128)(2,1)S(1)} %collective-permute-done.9, bf16[256,512]{1,0:T(8,128)(2,1)} %collective-permute-done.12, ...), kind=kOutput, calls=%fused_computation.66 | convolution fusion | flops 1241120768 | bytes 8086533 | tf_op jit(solution)/shard_map/dot_general | solution.py:227
  93.2 0.9 slice.151
  94.0 0.9 fusion.116
  95.0 0.8 copy.68
  96.3 3.0 %fusion.37 = f32[16,16,512]{2,1,0:T(8,128)S(1)} fusion(f32[16,16,512]{2,1,0:T(8,128)} %slice.151, f32[16,512]{1,0:T(8,128)} %fusion.126, f32[16,16,16]{1,2,0:T(8,128)} %copy.68, f32[16,16,16]{2,1,0:T(8,128)} %fusion.116, f32[16,16,16]{1,2,0:T(8,128)S(1)} %copy.66, pred[16,16]{1,0:T(8,128)(4,1)S(1)} %copy-done.27), kind=kOutput, calls=%fused_computation.50 | convolution fusion | flops 69468160 | bytes 1130752 | tf_op jit(solution)/shard_map/dtsh,dshm->dtm/dot_general | solution.py:69
  99.4 1.8 %multiply_reduce_fusion = (f32[16,16]{1,0:T(8,128)S(1)}, f32[16,16,512]{2,1,0:T(8,128)S(1)}) fusion(f32[16,16,1168]{2,1,0:T(8,128)} %bitcast.103, f32[16,16,640]{2,1,0:T(8,128)S(1)} %divide_multiply_fusion, f32[512]{0:T(512)S(1)} %copy-done.26, f32[16,16,512]{2,1,0:T(8,128)S(1)} %fusion.37, f32[16,16,512]{2,1,0:T(8,128)S(1)} %fusion.107, ...), kind=kOutput, calls=%fused_computation.117 | convolution fusion | flops 18218752 | bytes 3804160 | tf_op jit(solution)/shard_map/dtn,dmn->dtm/dot_general | solution.py:71
  101.4 1.0 convolution_convert_fusion.2
  102.4 1.0 convolution_convert_fusion.3
  103.4 1.0 convolution_convert_fusion.4
  104.7 1.2 collective-permute-start.14
  105.8 1.9 %collective-permute-start.13 = (bf16[256,512]{1,0:T(8,128)(2,1)}, bf16[256,512]{1,0:T(8,128)(2,1)}, u32[]{:S(2)}, u32[]{:S(2)}) collective-permute-start(bf16[256,512]{1,0:T(8,128)(2,1)} %convolution_convert_fusion.4), channel_id=1, source_target_pairs={{0,1},{1,2},{2,3},{3,0},{4,5},{5,6},{6,7},{7,4},{8,9},{9,10},{10,1... | collective-permute-start | bytes 786440 | tf_op jit(solution)/shard_map/ppermute | solution.py:90
  108.2 2.1 %add_convert_fusion = bf16[16,512,64]{1,2,0:T(8,128)(2,1)} fusion(bf16[16,512,64]{1,2,0:T(8,128)(2,1)S(1)} %copy-done.2, f32[16,16,512]{2,1,0:T(8,128)S(1)} %convolution_multiply_fusion, f32[16,512]{1,0:T(8,128)S(1)} %fusion.124, f32[16,16,640]{2,1,0:T(8,128)S(1)} %divide_multiply_fusion), kind=kOutput, calls=%fused_computation.27 | convolution fusion | flops 52428800 | bytes 2785280 | tf_op jit(solution)/shard_map/dsm,dsn->dmn/dot_general | solution.py:77
  110.3 2.7 %copy.73 = bf16[16,512,64]{2,1,0:T(8,128)(2,1)} copy(bf16[16,512,64]{1,2,0:T(8,128)(2,1)} %add_convert_fusion) | data formatting | bytes 2097152 | tf_op jit(solution)/shard_map/convert_element_type | solution.py:82
  113.0 4.3 %convert_element_type.169 = bf16[1,16,16,2048]{3,2,1,0:T(8,128)(2,1)} reshape(bf16[16,512,64]{2,1,0:T(8,128)(2,1)} %copy.73) | data formatting | bytes 2097152 | tf_op jit(solution)/shard_map/convert_element_type | solution.py:82
  117.2 1.0 fusion.122
  118.3 0.6 copy.74
  118.9 1.3 %collective-permute-done.13 = bf16[256,512]{1,0:T(8,128)(2,1)} collective-permute-done((bf16[256,512]{1,0:T(8,128)(2,1)}, bf16[256,512]{1,0:T(8,128)(2,1)}, u32[]{:S(2)}, u32[]{:S(2)}) %collective-permute-start.13) | collective-permute-done | bytes 262176 | tf_op jit(solution)/shard_map/ppermute | solution.py:90
  120.2 2.2 %fusion.101 = bf16[1,256,512]{2,1,0:T(8,128)(2,1)} fusion(bf16[256,512]{1,0:T(8,128)(2,1)} %collective-permute-done.15, bf16[256,512]{1,0:T(8,128)(2,1)} %collective-permute-done.14, bf16[256,512]{1,0:T(8,128)(2,1)} %collective-permute-done.13, bf16[256,512]{1,0:T(8,128)(2,1)S(1)} %copy-done.5, bf16[256,512]{1,0:T(8,128)(2,1)S(1)} %collective-permute-done.9, ...), kind=kOutput, calls=%fused_computation.131 | convolution fusion | flops 135790592 | bytes 2359301 | tf_op jit(solution)/shard_map/dot_general | solution.py:136
  (126 shorter events, 5.8 us)
Async XLA Ops:
  0.6 57.8 %copy-start = (bf16[1,512,2048]{2,1,0:T(8,128)(2,1)S(1)}, bf16[1,512,2048]{2,1,0:T(8,128)(2,1)}, u32[]{:S(2)}) copy-start(bf16[1,512,2048]{2,1,0:T(8,128)(2,1)} %param.24) | copy-start | bytes 6291460
  0.6 25.0 %collective-permute-start = (bf16[256,512]{1,0:T(8,128)(2,1)}, bf16[256,512]{1,0:T(8,128)(2,1)}, u32[]{:S(2)}, u32[]{:S(2)}) collective-permute-start(bf16[256,512]{1,0:T(8,128)(2,1)} %param.15), channel_id=1, source_target_pairs={{0,3},{1,0},{2,1},{3,2},{4,7},{5,4},{6,5},{7,6},{8,11},{9,8},{10,9... | collective-permute-start | bytes 786440 | tf_op jit(solution)/shard_map/ppermute | solution.py:90
  4.6 22.1 %collective-permute-start.1 = (bf16[256,512]{1,0:T(8,128)(2,1)}, bf16[256,512]{1,0:T(8,128)(2,1)}, u32[]{:S(2)}, u32[]{:S(2)}) collective-permute-start(bf16[256,512]{1,0:T(8,128)(2,1)} %param.15), channel_id=1, source_target_pairs={{0,2},{1,3},{2,0},{3,1},{4,6},{5,7},{6,4},{7,5},{8,10},{9,11},{10,... | collective-permute-start | bytes 786440 | tf_op jit(solution)/shard_map/ppermute | solution.py:90
  9.4 14.6 %collective-permute-start.5 = (bf16[4,3,640]{2,1,0:T(4,128)(2,1)S(1)}, bf16[4,3,640]{2,1,0:T(4,128)(2,1)S(1)}, u32[]{:S(2)}, u32[]{:S(2)}) collective-permute-start(bf16[4,3,640]{2,1,0:T(4,128)(2,1)S(1)} %get-tuple-element.23), channel_id=1, source_target_pairs={{0,12},{4,0},{8,4},{12,8},{1,13},{5,1},{9,5},{13,9},{2,14},{6,2},{... | collective-permute-start | bytes 46088 | tf_op jit(solution)/shard_map/ppermute | solution.py:90
  13.0 11.6 %collective-permute-start.4 = (bf16[4,3,640]{2,1,0:T(4,128)(2,1)S(1)}, bf16[4,3,640]{2,1,0:T(4,128)(2,1)S(1)}, u32[]{:S(2)}, u32[]{:S(2)}) collective-permute-start(bf16[4,3,640]{2,1,0:T(4,128)(2,1)S(1)} %get-tuple-element.21), channel_id=1, source_target_pairs={{0,8},{4,12},{8,0},{12,4},{1,9},{5,13},{9,1},{13,5},{2,10},{6,14},... | collective-permute-start | bytes 46088 | tf_op jit(solution)/shard_map/ppermute | solution.py:90
  13.0 11.6 %collective-permute-start.3 = (bf16[4,3,640]{2,1,0:T(4,128)(2,1)S(1)}, bf16[4,3,640]{2,1,0:T(4,128)(2,1)S(1)}, u32[]{:S(2)}, u32[]{:S(2)}) collective-permute-start(bf16[4,3,640]{2,1,0:T(4,128)(2,1)S(1)} %get-tuple-element.22), channel_id=1, source_target_pairs={{0,4},{4,8},{8,12},{12,0},{1,5},{5,9},{9,13},{13,1},{2,6},{6,10},{... | collective-permute-start | bytes 46088 | tf_op jit(solution)/shard_map/ppermute | solution.py:90
  14.0 7.8 %copy-start.32 = (s32[16]{0:T(128)S(1)}, s32[16]{0:T(128)}, u32[]{:S(2)}) copy-start(s32[16]{0:T(128)} %param.29) | copy-start | bytes 196
  14.0 7.8 %copy-start.14 = (f32[1,4,640]{2,1,0:T(4,128)S(1)}, f32[1,4,640]{2,1,0:T(4,128)}, u32[]{:S(2)}) copy-start(f32[1,4,640]{2,1,0:T(4,128)} %param.18) | copy-start | bytes 30724
  14.0 8.5 %copy-start.17 = (f32[1,2048]{1,0:T(1,128)S(1)}, f32[1,2048]{1,0:T(1,128)}, u32[]{:S(2)}) copy-start(f32[1,2048]{1,0:T(1,128)} %param.16) | copy-start | bytes 24580
  14.1 9.1 %copy-start.31 = (f32[1,16]{1,0:T(1,128)S(1)}, f32[1,16]{1,0:T(1,128)}, u32[]{:S(2)}) copy-start(f32[1,16]{1,0:T(1,128)} %param.22) | copy-start | bytes 196
  14.1 9.9 %copy-start.20 = (f32[1,640]{1,0:T(1,128)S(1)}, f32[1,640]{1,0:T(1,128)}, u32[]{:S(2)}) copy-start(f32[1,640]{1,0:T(1,128)} %param.19) | copy-start | bytes 7684
  14.1 9.9 %copy-start.4 = (bf16[256,512]{1,0:T(8,128)(2,1)S(1)}, bf16[256,512]{1,0:T(8,128)(2,1)}, u32[]{:S(2)}) copy-start(bf16[256,512]{1,0:T(8,128)(2,1)} %param.15) | copy-start | bytes 786436
  17.0 31.0 %all-to-all-start = ((bf16[16,16,2048]{2,1,0:T(8,128)(2,1)}), bf16[16,16,2048]{2,1,0:T(8,128)(2,1)}, u32[]{:S(2)}, u32[]{:S(2)}) async-start(bf16[16,16,2048]{2,1,0:T(8,128)(2,1)} %gather_fusion.2), calls=%async_computation | async-start | bytes 2097152 | tf_op jit(solution)/shard_map/all_to_all | solution.py:191
  21.8 15.9 %copy-start.28 = (bf16[16]{0:T(256)(128)(2,1)}, bf16[16]{0:T(256)(128)(2,1)S(1)}, u32[]{:S(2)}) copy-start(bf16[16]{0:T(256)(128)(2,1)S(1)} %compare_convert_fusion) | copy-start | bytes 100
  21.9 16.0 %copy-start.10 = (f32[640]{0:T(1024)}, f32[640]{0:T(1024)S(1)}, u32[]{:S(2)}) copy-start(f32[640]{0:T(1024)S(1)} %get-tuple-element.14) | copy-start | bytes 7684
  21.9 16.0 %copy-start.12 = (f32[640]{0:T(1024)}, f32[640]{0:T(1024)S(1)}, u32[]{:S(2)}) copy-start(f32[640]{0:T(1024)S(1)} %get-tuple-element.15) | copy-start | bytes 7684
  22.6 15.2 %copy-start.18 = (f32[2048]{0:T(1024)}, f32[2048]{0:T(1024)S(1)}, u32[]{:S(2)}) copy-start(f32[2048]{0:T(1024)S(1)} %fusion.134) | copy-start | bytes 24580
  24.0 7.7 %collective-permute-start.2 = (bf16[256,512]{1,0:T(8,128)(2,1)S(1)}, bf16[256,512]{1,0:T(8,128)(2,1)}, u32[]{:S(2)}, u32[]{:S(2)}) collective-permute-start(bf16[256,512]{1,0:T(8,128)(2,1)S(1)} %copy-done.4), channel_id=1, source_target_pairs={{0,1},{1,2},{2,3},{3,0},{4,5},{5,6},{6,7},{7,4},{8,9},{9,10},{10,1... | collective-permute-start | bytes 786440 | tf_op jit(solution)/shard_map/ppermute | solution.py:90
  33.0 4.9 %copy-start.6 = (f32[16,3,640]{2,1,0:T(4,128)S(1)}, f32[16,3,640]{2,1,0:T(4,128)}, u32[]{:S(2)}) copy-start(f32[16,3,640]{2,1,0:T(4,128)} %reshape.356) | copy-start | bytes 368644
  37.8 2.4 %copy-start.9 = (f32[256,1168]{1,0:T(8,128)}, f32[256,1168]{1,0:T(8,128)S(1)}, u32[]{:S(2)}) copy-start(f32[256,1168]{1,0:T(8,128)S(1)} %fusion.47) | copy-start | bytes 3588100
  37.8 2.3 %copy-start.21 = (f32[1,16]{1,0:T(1,128)S(1)}, f32[1,16]{1,0:T(1,128)}, u32[]{:S(2)}) copy-start(f32[1,16]{1,0:T(1,128)} %param.21) | copy-start | bytes 196
  37.8 2.3 %copy-start.23 = (f32[1,16]{1,0:T(1,128)S(1)}, f32[1,16]{1,0:T(1,128)}, u32[]{:S(2)}) copy-start(f32[1,16]{1,0:T(1,128)} %param.20) | copy-start | bytes 196
  38.4 0.8 copy-start.3
  48.0 1.8 %copy-start.29 = (bf16[16]{0:T(256)(128)(2,1)S(1)}, bf16[16]{0:T(256)(128)(2,1)}, u32[]{:S(2)}) copy-start(bf16[16]{0:T(256)(128)(2,1)} %copy-done.28) | copy-start | bytes 100
  48.0 1.8 %copy-start.30 = (s32[16]{0:T(128)S(1)}, s32[16]{0:T(128)}, u32[]{:S(2)}) copy-start(s32[16]{0:T(128)} %get-tuple-element.24) | copy-start | bytes 196
  51.3 4.0 %copy-start.25 = (f32[512]{0:T(512)S(1)}, f32[512]{0:T(512)}, u32[]{:S(2)}) copy-start(f32[512]{0:T(512)} %mul.349) | copy-start | bytes 6148
  55.3 3.0 %copy-start.15 = (f32[1,512]{1,0:T(1,128)S(1)}, f32[1,512]{1,0:T(1,128)}, u32[]{:S(2)}) copy-start(f32[1,512]{1,0:T(1,128)} %param.23) | copy-start | bytes 6148
  59.4 9.4 %collective-permute-start.8 = (bf16[256,512]{1,0:T(8,128)(2,1)}, bf16[256,512]{1,0:T(8,128)(2,1)}, u32[]{:S(2)}, u32[]{:S(2)}) collective-permute-start(bf16[256,512]{1,0:T(8,128)(2,1)} %convolution_convert_fusion.6), channel_id=1, source_target_pairs={{0,3},{1,0},{2,1},{3,2},{4,7},{5,4},{6,5},{7,6},{8,11},{9,8},{10,9... | collective-permute-start | bytes 786440 | tf_op jit(solution)/shard_map/ppermute | solution.py:90
  60.8 11.9 %collective-permute-start.7 = (bf16[256,512]{1,0:T(8,128)(2,1)}, bf16[256,512]{1,0:T(8,128)(2,1)}, u32[]{:S(2)}, u32[]{:S(2)}) collective-permute-start(bf16[256,512]{1,0:T(8,128)(2,1)} %convolution_convert_fusion.7), channel_id=1, source_target_pairs={{0,2},{1,3},{2,0},{3,1},{4,6},{5,7},{6,4},{7,5},{8,10},{9,11},{10,... | collective-permute-start | bytes 786440 | tf_op jit(solution)/shard_map/ppermute | solution.py:90
  63.0 9.7 %collective-permute-start.6 = (bf16[256,512]{1,0:T(8,128)(2,1)}, bf16[256,512]{1,0:T(8,128)(2,1)}, u32[]{:S(2)}, u32[]{:S(2)}) collective-permute-start(bf16[256,512]{1,0:T(8,128)(2,1)} %convolution_convert_fusion.8), channel_id=1, source_target_pairs={{0,1},{1,2},{2,3},{3,0},{4,5},{5,6},{6,7},{7,4},{8,9},{9,10},{10,1... | collective-permute-start | bytes 786440 | tf_op jit(solution)/shard_map/ppermute | solution.py:90
  74.9 10.0 %collective-permute-start.9 = (bf16[256,512]{1,0:T(8,128)(2,1)}, bf16[256,512]{1,0:T(8,128)(2,1)S(1)}, u32[]{:S(2)}, u32[]{:S(2)}) collective-permute-start(bf16[256,512]{1,0:T(8,128)(2,1)} %add_convert_fusion.2), channel_id=1, source_target_pairs={{0,16},{1,17},{2,18},{3,19},{4,20},{5,21},{6,22},{7,23},{8,24},{9,... | collective-permute-start | bytes 786440 | tf_op jit(solution)/shard_map/ppermute | solution.py:118
  76.2 8.7 %collective-permute-start.12 = (bf16[256,512]{1,0:T(8,128)(2,1)}, bf16[256,512]{1,0:T(8,128)(2,1)}, u32[]{:S(2)}, u32[]{:S(2)}) collective-permute-start(bf16[256,512]{1,0:T(8,128)(2,1)} %add_convert_fusion.2), channel_id=1, source_target_pairs={{0,17},{1,18},{2,19},{3,16},{4,21},{5,22},{6,23},{7,20},{8,25},{9,... | collective-permute-start | bytes 786440 | tf_op jit(solution)/shard_map/ppermute | solution.py:118
  78.2 6.7 %collective-permute-start.11 = (bf16[256,512]{1,0:T(8,128)(2,1)}, bf16[256,512]{1,0:T(8,128)(2,1)}, u32[]{:S(2)}, u32[]{:S(2)}) collective-permute-start(bf16[256,512]{1,0:T(8,128)(2,1)} %add_convert_fusion.2), channel_id=1, source_target_pairs={{0,18},{1,19},{2,16},{3,17},{4,22},{5,23},{6,20},{7,21},{8,26},{9,... | collective-permute-start | bytes 786440 | tf_op jit(solution)/shard_map/ppermute | solution.py:118
  80.2 5.5 %collective-permute-start.10 = (bf16[256,512]{1,0:T(8,128)(2,1)}, bf16[256,512]{1,0:T(8,128)(2,1)}, u32[]{:S(2)}, u32[]{:S(2)}) collective-permute-start(bf16[256,512]{1,0:T(8,128)(2,1)} %add_convert_fusion.2), channel_id=1, source_target_pairs={{0,19},{1,16},{2,17},{3,18},{4,23},{5,20},{6,21},{7,22},{8,27},{9,... | collective-permute-start | bytes 786440 | tf_op jit(solution)/shard_map/ppermute | solution.py:118
  82.2 5.0 %copy-start.19 = (f32[2048]{0:T(1024)S(1)}, f32[2048]{0:T(1024)}, u32[]{:S(2)}) copy-start(f32[2048]{0:T(1024)} %copy-done.18) | copy-start | bytes 24580
  87.3 5.3 %copy-start.22 = (f32[1,16]{1,0:T(1,128)S(1)}, f32[1,16]{1,0:T(1,128)}, u32[]{:S(2)}) copy-start(f32[1,16]{1,0:T(1,128)} %param.21) | copy-start | bytes 196
  87.3 5.3 %copy-start.24 = (f32[1,16]{1,0:T(1,128)S(1)}, f32[1,16]{1,0:T(1,128)}, u32[]{:S(2)}) copy-start(f32[1,16]{1,0:T(1,128)} %param.20) | copy-start | bytes 196
  87.3 5.4 %copy-start.7 = (f32[16,3,640]{2,1,0:T(4,128)S(1)}, f32[16,3,640]{2,1,0:T(4,128)}, u32[]{:S(2)}) copy-start(f32[16,3,640]{2,1,0:T(4,128)} %reshape.356) | copy-start | bytes 368644
  87.3 5.4 %copy-start.11 = (f32[640]{0:T(1024)S(1)}, f32[640]{0:T(1024)}, u32[]{:S(2)}) copy-start(f32[640]{0:T(1024)} %copy-done.10) | copy-start | bytes 7684
  87.3 5.4 %copy-start.13 = (f32[640]{0:T(1024)S(1)}, f32[640]{0:T(1024)}, u32[]{:S(2)}) copy-start(f32[640]{0:T(1024)} %copy-done.12) | copy-start | bytes 7684
  92.5 1.6 %copy-start.8 = (f32[256,1168]{1,0:T(8,128)}, f32[256,1168]{1,0:T(8,128)S(1)}, u32[]{:S(2)}) copy-start(f32[256,1168]{1,0:T(8,128)S(1)} %fusion.45) | copy-start | bytes 3588100
  93.2 3.1 %copy-start.27 = (pred[16,16]{1,0:T(8,128)(4,1)S(1)}, pred[16,16]{1,0:T(8,128)(4,1)}, u32[]{:S(2)}) copy-start(pred[16,16]{1,0:T(8,128)(4,1)} %iota_compare_fusion.6) | copy-start | bytes 772
  96.3 3.1 %copy-start.1 = (bf16[16,512,64]{2,1,0:T(8,128)(2,1)S(1)}, bf16[16,512,64]{2,1,0:T(8,128)(2,1)}, u32[]{:S(2)}) copy-start(bf16[16,512,64]{2,1,0:T(8,128)(2,1)} %reshape_reshape.4) | copy-start | bytes 3145732
  96.3 3.1 %copy-start.26 = (f32[512]{0:T(512)S(1)}, f32[512]{0:T(512)}, u32[]{:S(2)}) copy-start(f32[512]{0:T(512)} %mul.349) | copy-start | bytes 6148
  99.4 1.9 %copy-start.16 = (f32[1,512]{1,0:T(1,128)S(1)}, f32[1,512]{1,0:T(1,128)}, u32[]{:S(2)}) copy-start(f32[1,512]{1,0:T(1,128)} %param.23) | copy-start | bytes 6148
  101.4 6.8 %copy-start.2 = (bf16[16,512,64]{1,2,0:T(8,128)(2,1)S(1)}, bf16[16,512,64]{1,2,0:T(8,128)(2,1)}, u32[]{:S(2)}) copy-start(bf16[16,512,64]{1,2,0:T(8,128)(2,1)} %copy.71) | copy-start | bytes 3145732
  104.6 14.3 %collective-permute-start.15 = (bf16[256,512]{1,0:T(8,128)(2,1)}, bf16[256,512]{1,0:T(8,128)(2,1)}, u32[]{:S(2)}, u32[]{:S(2)}) collective-permute-start(bf16[256,512]{1,0:T(8,128)(2,1)} %convolution_convert_fusion.2), channel_id=1, source_target_pairs={{0,3},{1,0},{2,1},{3,2},{4,7},{5,4},{6,5},{7,6},{8,11},{9,8},{10,9... | collective-permute-start | bytes 786440 | tf_op jit(solution)/shard_map/ppermute | solution.py:90
  104.7 14.2 %collective-permute-start.14 = (bf16[256,512]{1,0:T(8,128)(2,1)}, bf16[256,512]{1,0:T(8,128)(2,1)}, u32[]{:S(2)}, u32[]{:S(2)}) collective-permute-start(bf16[256,512]{1,0:T(8,128)(2,1)} %convolution_convert_fusion.3), channel_id=1, source_target_pairs={{0,2},{1,3},{2,0},{3,1},{4,6},{5,7},{6,4},{7,5},{8,10},{9,11},{10,... | collective-permute-start | bytes 786440 | tf_op jit(solution)/shard_map/ppermute | solution.py:90
  105.8 14.3 %collective-permute-start.13 = (bf16[256,512]{1,0:T(8,128)(2,1)}, bf16[256,512]{1,0:T(8,128)(2,1)}, u32[]{:S(2)}, u32[]{:S(2)}) collective-permute-start(bf16[256,512]{1,0:T(8,128)(2,1)} %convolution_convert_fusion.4), channel_id=1, source_target_pairs={{0,1},{1,2},{2,3},{3,0},{4,5},{5,6},{6,7},{7,4},{8,9},{9,10},{10,1... | collective-permute-start | bytes 786440 | tf_op jit(solution)/shard_map/ppermute | solution.py:90
  113.0 7.2 %copy-start.5 = (bf16[256,512]{1,0:T(8,128)(2,1)S(1)}, bf16[256,512]{1,0:T(8,128)(2,1)}, u32[]{:S(2)}) copy-start(bf16[256,512]{1,0:T(8,128)(2,1)} %param.15) | copy-start | bytes 786436

commit v6 on v5

--- a/solution.py
+++ b/solution.py
@@ -53,7 +53,7 @@
     ).astype(jnp.float32)
 
     def expand(per_head):
-        return jnp.einsum("...h,hm->...m", per_head, expander, precision=highest)
+        return jnp.einsum("...h,hm->...m", per_head, expander, precision=three_pass)
 
     key_proj = activated[:, :, inner : inner + state_width]
     query_proj = activated[:, :, inner + state_width :]

time: 123 us -> 123 us (level)
  no operation moved by 1% of the time
where the time goes in v6:
time: 123 us; the launch traced here: 122 us
  matrix products  39.7 us (32%)
  local copies, waits for them, and re-layouts  33.4 us (27%)
  starting transfers between devices  28.1 us (23%)
  waiting for transfers between devices  13.8 us (11%)
  other arithmetic  5.86 us (5%)
  between operations  1.32 us (1%)
    ppermute x12, starting transfers between devices, shifted(): lax.ppermute(value, axis, [(source, (source + steps) % count) for source...  16.6 us
    ppermute x12, waiting for transfers between devices, shifted(): lax.ppermute(value, axis, [(source, (source + steps) % count) for source...  13 us
    dot_general x8, matrix products, scatter_sum(): jnp.dot(gnormed, weight_block, preferred_element_type=jnp.float32)  10.5 us
    dot_general x2, matrix products, per_device(): jnp.dot(normed, proj_rotated, preferred_element_type=jnp.float32)  9.86 us
    ppermute x4, starting transfers between devices, gather_from_behind(): parts.append(lax.ppermute(value, ('section', 'mp'), pairs))  7.3 us
    unnamed x73, local copies, waits for them, and re-layouts  7.21 us
    convert_element_type x2, local copies, waits for them, and re-layouts, mix_channels(): end_state.reshape(doc_count, head_count, head_dim * state_width)  6.99 us
    dot_general x2, matrix products, mix_channels(): jnp.einsum('dtsh,dshm->dtm', weights, spread, precision=one_pass)  6.78 us
  transfers between devices with their start and end apart: 17, of which 5 were waited for; matrix products, arithmetic and copies ran while one was open for 36% of the time, Pallas kernels for 0%

profile of v6, /device:TPU:0, one launch (start us, length us, event | category | flops | bytes accessed | tf_op | source)
XLA Modules:
  0.0 122.2 jit_solution(1082494493717868539)
XLA Ops:
  0.6 3.9 %collective-permute-start = (bf16[256,512]{1,0:T(8,128)(2,1)}, bf16[256,512]{1,0:T(8,128)(2,1)}, u32[]{:S(2)}, u32[]{:S(2)}) collective-permute-start(bf16[256,512]{1,0:T(8,128)(2,1)} %param.15), channel_id=1, source_target_pairs={{0,3},{1,0},{2,1},{3,2},{4,7},{5,4},{6,5},{7,6},{8,11},{9,8},{10,9... | collective-permute-start | bytes 786440 | tf_op jit(solution)/shard_map/ppermute | solution.py:90
  5.1 0.9 copy.102
  6.0 0.7 broadcast_in_dim.47
  6.7 0.7 reshape.349
  8.7 0.6 gather_fusion.1
  9.4 3.7 %collective-permute-start.5 = (bf16[4,3,640]{2,1,0:T(4,128)(2,1)S(1)}, bf16[4,3,640]{2,1,0:T(4,128)(2,1)S(1)}, u32[]{:S(2)}, u32[]{:S(2)}) collective-permute-start(bf16[4,3,640]{2,1,0:T(4,128)(2,1)S(1)} %get-tuple-element.23), channel_id=1, source_target_pairs={{0,12},{4,0},{8,4},{12,8},{1,13},{5,1},{9,5},{13,9},{2,14},{6,2},{... | collective-permute-start | bytes 46088 | tf_op jit(solution)/shard_map/ppermute | solution.py:90
  13.0 1.0 collective-permute-start.3
  14.1 2.9 %gather_fusion.2 = bf16[16,16,2048]{2,1,0:T(8,128)(2,1)} fusion(bf16[16,16,2048]{2,1,0:T(8,128)(2,1)} %bitcast.100, s32[1024]{0:T(1024)S(1)} %pad_clamp_fusion), kind=kCustom, calls=%fused_computation.2 | custom fusion | bytes 2097216 | tf_op jit(solution)/shard_map/gather | solution.py:190
  17.0 4.2 %all-to-all-start = ((bf16[16,16,2048]{2,1,0:T(8,128)(2,1)}), bf16[16,16,2048]{2,1,0:T(8,128)(2,1)}, u32[]{:S(2)}, u32[]{:S(2)}) async-start(bf16[16,16,2048]{2,1,0:T(8,128)(2,1)} %gather_fusion.2), calls=%async_computation | async-start | bytes 2097152 | tf_op jit(solution)/shard_map/all_to_all | solution.py:191
  21.2 0.6 iota_compare_fusion.6
  21.9 0.6 fusion.126
  22.6 0.6 bitcast_add_fusion
  23.3 0.7 mul.349
  24.0 0.6 collective-permute-start.2
  24.9 0.7 reshape.356
  25.7 1.0 constant_dynamic-update-slice_fusion.3
  26.7 1.0 constant_dynamic-update-slice_fusion.2
  27.7 4.0 %collective-permute-done.2 = bf16[256,512]{1,0:T(8,128)(2,1)} collective-permute-done((bf16[256,512]{1,0:T(8,128)(2,1)S(1)}, bf16[256,512]{1,0:T(8,128)(2,1)}, u32[]{:S(2)}, u32[]{:S(2)}) %collective-permute-start.2) | collective-permute-done | bytes 262176 | tf_op jit(solution)/shard_map/ppermute | solution.py:90
  31.7 1.0 constant_dynamic-update-slice_fusion.1
  33.0 4.7 %fusion.47 = f32[256,1168]{1,0:T(8,128)S(1)} fusion(bf16[256,2048]{1,0:T(8,128)(2,1)S(1)} %constant_dynamic-update-slice_fusion, f32[2048]{0:T(1024)S(1)} %fusion.134, f32[256]{0:T(256)S(1)} %add_rsqrt_fusion.3, s32[]{:T(128)S(6)} %select_n.179, bf16[2048,1168]{0,1:T(8,128)(2,1)} %bitcast.119), kind=kOutput, calls=%fused_computation.67 | convolution fusion | flops 1236402176 | bytes 7037956 | tf_op jit(solution)/shard_map/dot_general | solution.py:227
  38.4 0.8 copy-done.3
  39.2 0.9 slice.141
  40.2 0.8 copy.61
  41.0 0.8 copy.58
  41.8 1.3 %fusion.102 = f32[16,16,16]{2,1,0:T(8,128)S(1)} fusion(f32[16,16,640]{2,1,0:T(8,128)} %copy-done.3), kind=kOutput, calls=%fused_computation.134 | convolution fusion | flops 1572864 | bytes 278528 | tf_op jit(solution)/shard_map/dtn,dsn->dts/dot_general | solution.py:66
  43.1 1.1 fusion.111
  44.2 3.7 %fusion.32 = f32[16,16,512]{2,1,0:T(8,128)} fusion(f32[16,512]{1,0:T(8,128)} %fusion.126, f32[16,16,512]{2,1,0:T(8,128)} %slice.141, f32[16,16,16]{1,2,0:T(8,128)} %copy.61, f32[16,16,16]{2,1,0:T(8,128)S(1)} %fusion.102, f32[16,16,16]{1,2,0:T(8,128)} %copy.58, pred[16,16]{1,0:T(8,128)(4,1)} %iota_compare_fusion.6), kind=kOutput, calls=%fused_computation.49 | convolution fusion | flops 69468160 | bytes 1130752 | tf_op jit(solution)/shard_map/dtsh,dshm->dtm/dot_general | solution.py:69
  47.9 1.8 %copy.82 = bf16[2,8,16,2048]{3,1,2,0:T(8,128)(2,1)S(1)} copy(bf16[2,8,16,2048]{3,2,1,0:T(8,128)(2,1)} %bitcast.32) | data formatting | bytes 2097152
  49.7 1.4 %convolution_convert_fusion = bf16[16,32768]{1,0:T(8,128)(2,1)} fusion(bf16[16,32768]{1,0:T(8,128)(2,1)S(1)} %bitcast.99, s32[16]{0:T(128)S(1)} %copy-done.30, bf16[16]{0:T(256)(128)(2,1)S(1)} %copy-done.29), kind=kOutput, calls=%fused_computation.3 | convolution fusion | flops 17302016 | bytes 2097248 | tf_op jit(solution)/shard_map/dot_general | solution.py:187
  51.2 4.0 %reshape_reshape.4 = bf16[16,512,64]{2,1,0:T(8,128)(2,1)} reshape(bf16[16,32768]{1,0:T(8,128)(2,1)} %convolution_convert_fusion) | data formatting | bytes 2097152 | tf_op jit(solution)/shard_map/reshape;reshape | solution.py:70
  55.2 3.0 %multiply_reduce_fusion.1 = (f32[16,16]{1,0:T(8,128)S(1)}, f32[16,16,512]{2,1,0:T(8,128)S(1)}) fusion(f32[16,16,1168]{2,1,0:T(8,128)} %bitcast.107, f32[16,16,640]{2,1,0:T(8,128)} %copy-done.3, f32[512]{0:T(512)S(1)} %copy-done.25, f32[16,16,512]{2,1,0:T(8,128)} %fusion.32, f32[16,16,512]{2,1,0:T(8,128)} %fusion.111, bf16[16,512,64]{2,1,0:T(8,128)(2,1)} %reshape_reshape.4), kind=kOutput, calls=%fused_computation.120 | convolution fusion | flops 18218752 | bytes 3804160 | tf_op jit(solution)/shard_map/dtn,dmn->dtm/dot_general | solution.py:71
  58.3 1.0 convolution_convert_fusion.6
  59.7 1.0 convolution_convert_fusion.7
  60.7 1.2 collective-permute-start.7
  61.9 1.0 convolution_convert_fusion.8
  62.9 2.0 %collective-permute-start.6 = (bf16[256,512]{1,0:T(8,128)(2,1)}, bf16[256,512]{1,0:T(8,128)(2,1)}, u32[]{:S(2)}, u32[]{:S(2)}) collective-permute-start(bf16[256,512]{1,0:T(8,128)(2,1)} %convolution_convert_fusion.8), channel_id=1, source_target_pairs={{0,1},{1,2},{2,3},{3,0},{4,5},{5,6},{6,7},{7,4},{8,9},{9,10},{10,1... | collective-permute-start | bytes 786440 | tf_op jit(solution)/shard_map/ppermute | solution.py:90
  65.0 3.8 %collective-permute-done.8 = bf16[256,512]{1,0:T(8,128)(2,1)} collective-permute-done((bf16[256,512]{1,0:T(8,128)(2,1)}, bf16[256,512]{1,0:T(8,128)(2,1)}, u32[]{:S(2)}, u32[]{:S(2)}) %collective-permute-start.8) | collective-permute-done | bytes 262176 | tf_op jit(solution)/shard_map/ppermute | solution.py:90
  68.8 3.8 %collective-permute-done.7 = bf16[256,512]{1,0:T(8,128)(2,1)} collective-permute-done((bf16[256,512]{1,0:T(8,128)(2,1)}, bf16[256,512]{1,0:T(8,128)(2,1)}, u32[]{:S(2)}, u32[]{:S(2)}) %collective-permute-start.7) | collective-permute-done | bytes 262176 | tf_op jit(solution)/shard_map/ppermute | solution.py:90
  72.6 2.3 %add_convert_fusion.2 = bf16[256,512]{1,0:T(8,128)(2,1)} fusion(bf16[256,512]{1,0:T(8,128)(2,1)} %collective-permute-done.8, bf16[256,512]{1,0:T(8,128)(2,1)} %collective-permute-done.7, bf16[256,512]{1,0:T(8,128)(2,1)} %collective-permute-done.6, bf16[256,512]{1,0:T(8,128)(2,1)S(1)} %bitcast.94, bf16[256,512]{1,0:T(8,128)(2,1)} %param.15, ...), kind=kOutput, calls=%fused_computation.118 | convolution fusion | flops 135659520 | bytes 2097156 | tf_op jit(solution)/shard_map/dot_general | solution.py:136
  74.9 1.3 %collective-permute-start.9 = (bf16[256,512]{1,0:T(8,128)(2,1)}, bf16[256,512]{1,0:T(8,128)(2,1)S(1)}, u32[]{:S(2)}, u32[]{:S(2)}) collective-permute-start(bf16[256,512]{1,0:T(8,128)(2,1)} %add_convert_fusion.2), channel_id=1, source_target_pairs={{0,16},{1,17},{2,18},{3,19},{4,20},{5,21},{6,22},{7,23},{8,24},{9,... | collective-permute-start | bytes 786440 | tf_op jit(solution)/shard_map/ppermute | solution.py:118
  76.2 2.0 %collective-permute-start.12 = (bf16[256,512]{1,0:T(8,128)(2,1)}, bf16[256,512]{1,0:T(8,128)(2,1)}, u32[]{:S(2)}, u32[]{:S(2)}) collective-permute-start(bf16[256,512]{1,0:T(8,128)(2,1)} %add_convert_fusion.2), channel_id=1, source_target_pairs={{0,17},{1,18},{2,19},{3,16},{4,21},{5,22},{6,23},{7,20},{8,25},{9,... | collective-permute-start | bytes 786440 | tf_op jit(solution)/shard_map/ppermute | solution.py:118
  78.2 2.0 %collective-permute-start.11 = (bf16[256,512]{1,0:T(8,128)(2,1)}, bf16[256,512]{1,0:T(8,128)(2,1)}, u32[]{:S(2)}, u32[]{:S(2)}) collective-permute-start(bf16[256,512]{1,0:T(8,128)(2,1)} %add_convert_fusion.2), channel_id=1, source_target_pairs={{0,18},{1,19},{2,16},{3,17},{4,22},{5,23},{6,20},{7,21},{8,26},{9,... | collective-permute-start | bytes 786440 | tf_op jit(solution)/shard_map/ppermute | solution.py:118
  80.2 2.0 %collective-permute-start.10 = (bf16[256,512]{1,0:T(8,128)(2,1)}, bf16[256,512]{1,0:T(8,128)(2,1)}, u32[]{:S(2)}, u32[]{:S(2)}) collective-permute-start(bf16[256,512]{1,0:T(8,128)(2,1)} %add_convert_fusion.2), channel_id=1, source_target_pairs={{0,19},{1,16},{2,17},{3,18},{4,23},{5,20},{6,21},{7,22},{8,27},{9,... | collective-permute-start | bytes 786440 | tf_op jit(solution)/shard_map/ppermute | solution.py:118
  82.2 2.7 %copy.71 = bf16[16,512,64]{1,2,0:T(8,128)(2,1)} copy(bf16[16,512,64]{2,1,0:T(8,128)(2,1)} %reshape_reshape.4) | data formatting | bytes 2097152 | tf_op jit(solution)/shard_map/reshape;reshape | solution.py:70
  84.9 0.8 collective-permute-done.10
  85.6 1.5 %fusion.13 = f32[256]{0:T(256)S(1)} fusion(bf16[256,2048]{1,0:T(8,128)(2,1)S(1)} %constant_dynamic-update-slice_fusion, bf16[256,512]{1,0:T(8,128)(2,1)S(1)} %collective-permute-done.9, bf16[256,512]{1,0:T(8,128)(2,1)} %collective-permute-done.12, bf16[256,512]{1,0:T(8,128)(2,1)} %collective-permute-done.11, bf16[256,512]{1,0:T(8,128)(2,1)} %collective-permute-done.10, ...), kind=kLoop, calls=%fused_computation.24 | loop fusion | flops 6291200 | bytes 2098177 | tf_op jit(solution)/shard_map/reduce_sum | solution.py:19
  87.2 5.1 %fusion.45 = f32[256,1168]{1,0:T(8,128)S(1)} fusion(f32[256]{0:T(256)S(1)} %add_rsqrt_fusion.2, f32[2048]{0:T(1024)S(1)} %copy-done.19, bf16[256,2048]{1,0:T(8,128)(2,1)S(1)} %constant_dynamic-update-slice_fusion, bf16[256,512]{1,0:T(8,128)(2,1)S(1)} %collective-permute-done.9, bf16[256,512]{1,0:T(8,128)(2,1)} %collective-permute-done.12, ...), kind=kOutput, calls=%fused_computation.66 | convolution fusion | flops 1241120768 | bytes 8086533 | tf_op jit(solution)/shard_map/dot_general | solution.py:227
  93.1 0.9 slice.151
  94.0 0.9 fusion.116
  94.9 0.8 copy.68
  96.2 3.0 %fusion.37 = f32[16,16,512]{2,1,0:T(8,128)S(1)} fusion(f32[16,16,512]{2,1,0:T(8,128)} %slice.151, f32[16,512]{1,0:T(8,128)} %fusion.126, f32[16,16,16]{1,2,0:T(8,128)} %copy.68, f32[16,16,16]{2,1,0:T(8,128)} %fusion.116, f32[16,16,16]{1,2,0:T(8,128)S(1)} %copy.66, pred[16,16]{1,0:T(8,128)(4,1)S(1)} %copy-done.27), kind=kOutput, calls=%fused_computation.50 | convolution fusion | flops 69468160 | bytes 1130752 | tf_op jit(solution)/shard_map/dtsh,dshm->dtm/dot_general | solution.py:69
  99.2 1.8 %multiply_reduce_fusion = (f32[16,16]{1,0:T(8,128)S(1)}, f32[16,16,512]{2,1,0:T(8,128)S(1)}) fusion(f32[16,16,1168]{2,1,0:T(8,128)} %bitcast.103, f32[16,16,640]{2,1,0:T(8,128)S(1)} %divide_multiply_fusion, f32[512]{0:T(512)S(1)} %copy-done.26, f32[16,16,512]{2,1,0:T(8,128)S(1)} %fusion.37, f32[16,16,512]{2,1,0:T(8,128)S(1)} %fusion.107, ...), kind=kOutput, calls=%fused_computation.117 | convolution fusion | flops 18218752 | bytes 3804160 | tf_op jit(solution)/shard_map/dtn,dmn->dtm/dot_general | solution.py:71
  101.2 1.0 convolution_convert_fusion.2
  102.2 1.0 convolution_convert_fusion.3
  103.2 1.0 convolution_convert_fusion.4
  104.5 1.2 collective-permute-start.14
  105.7 1.9 %collective-permute-start.13 = (bf16[256,512]{1,0:T(8,128)(2,1)}, bf16[256,512]{1,0:T(8,128)(2,1)}, u32[]{:S(2)}, u32[]{:S(2)}) collective-permute-start(bf16[256,512]{1,0:T(8,128)(2,1)} %convolution_convert_fusion.4), channel_id=1, source_target_pairs={{0,1},{1,2},{2,3},{3,0},{4,5},{5,6},{6,7},{7,4},{8,9},{9,10},{10,1... | collective-permute-start | bytes 786440 | tf_op jit(solution)/shard_map/ppermute | solution.py:90
  107.9 2.1 %add_convert_fusion = bf16[16,512,64]{1,2,0:T(8,128)(2,1)} fusion(bf16[16,512,64]{1,2,0:T(8,128)(2,1)S(1)} %copy-done.2, f32[16,16,512]{2,1,0:T(8,128)S(1)} %convolution_multiply_fusion, f32[16,512]{1,0:T(8,128)S(1)} %fusion.124, f32[16,16,640]{2,1,0:T(8,128)S(1)} %divide_multiply_fusion), kind=kOutput, calls=%fused_computation.27 | convolution fusion | flops 52428800 | bytes 2785280 | tf_op jit(solution)/shard_map/dsm,dsn->dmn/dot_general | solution.py:77
  110.0 2.7 %copy.73 = bf16[16,512,64]{2,1,0:T(8,128)(2,1)} copy(bf16[16,512,64]{1,2,0:T(8,128)(2,1)} %add_convert_fusion) | data formatting | bytes 2097152 | tf_op jit(solution)/shard_map/convert_element_type | solution.py:82
  112.7 4.3 %convert_element_type.169 = bf16[1,16,16,2048]{3,2,1,0:T(8,128)(2,1)} reshape(bf16[16,512,64]{2,1,0:T(8,128)(2,1)} %copy.73) | data formatting | bytes 2097152 | tf_op jit(solution)/shard_map/convert_element_type | solution.py:82
  117.0 1.0 fusion.122
  118.0 0.6 copy.74
  118.7 1.4 %collective-permute-done.13 = bf16[256,512]{1,0:T(8,128)(2,1)} collective-permute-done((bf16[256,512]{1,0:T(8,128)(2,1)}, bf16[256,512]{1,0:T(8,128)(2,1)}, u32[]{:S(2)}, u32[]{:S(2)}) %collective-permute-start.13) | collective-permute-done | bytes 262176 | tf_op jit(solution)/shard_map/ppermute | solution.py:90
  120.0 2.2 %fusion.101 = bf16[1,256,512]{2,1,0:T(8,128)(2,1)} fusion(bf16[256,512]{1,0:T(8,128)(2,1)} %collective-permute-done.15, bf16[256,512]{1,0:T(8,128)(2,1)} %collective-permute-done.14, bf16[256,512]{1,0:T(8,128)(2,1)} %collective-permute-done.13, bf16[256,512]{1,0:T(8,128)(2,1)S(1)} %copy-done.5, bf16[256,512]{1,0:T(8,128)(2,1)S(1)} %collective-permute-done.9, ...), kind=kOutput, calls=%fused_computation.131 | convolution fusion | flops 135790592 | bytes 2359301 | tf_op jit(solution)/shard_map/dot_general | solution.py:136
  (126 shorter events, 5.7 us)
Async XLA Ops:
  0.6 57.7 %copy-start = (bf16[1,512,2048]{2,1,0:T(8,128)(2,1)S(1)}, bf16[1,512,2048]{2,1,0:T(8,128)(2,1)}, u32[]{:S(2)}) copy-start(bf16[1,512,2048]{2,1,0:T(8,128)(2,1)} %param.24) | copy-start | bytes 6291460
  0.6 25.0 %collective-permute-start = (bf16[256,512]{1,0:T(8,128)(2,1)}, bf16[256,512]{1,0:T(8,128)(2,1)}, u32[]{:S(2)}, u32[]{:S(2)}) collective-permute-start(bf16[256,512]{1,0:T(8,128)(2,1)} %param.15), channel_id=1, source_target_pairs={{0,3},{1,0},{2,1},{3,2},{4,7},{5,4},{6,5},{7,6},{8,11},{9,8},{10,9... | collective-permute-start | bytes 786440 | tf_op jit(solution)/shard_map/ppermute | solution.py:90
  4.6 22.1 %collective-permute-start.1 = (bf16[256,512]{1,0:T(8,128)(2,1)}, bf16[256,512]{1,0:T(8,128)(2,1)}, u32[]{:S(2)}, u32[]{:S(2)}) collective-permute-start(bf16[256,512]{1,0:T(8,128)(2,1)} %param.15), channel_id=1, source_target_pairs={{0,2},{1,3},{2,0},{3,1},{4,6},{5,7},{6,4},{7,5},{8,10},{9,11},{10,... | collective-permute-start | bytes 786440 | tf_op jit(solution)/shard_map/ppermute | solution.py:90
  9.4 14.6 %collective-permute-start.5 = (bf16[4,3,640]{2,1,0:T(4,128)(2,1)S(1)}, bf16[4,3,640]{2,1,0:T(4,128)(2,1)S(1)}, u32[]{:S(2)}, u32[]{:S(2)}) collective-permute-start(bf16[4,3,640]{2,1,0:T(4,128)(2,1)S(1)} %get-tuple-element.23), channel_id=1, source_target_pairs={{0,12},{4,0},{8,4},{12,8},{1,13},{5,1},{9,5},{13,9},{2,14},{6,2},{... | collective-permute-start | bytes 46088 | tf_op jit(solution)/shard_map/ppermute | solution.py:90
  13.0 11.6 %collective-permute-start.4 = (bf16[4,3,640]{2,1,0:T(4,128)(2,1)S(1)}, bf16[4,3,640]{2,1,0:T(4,128)(2,1)S(1)}, u32[]{:S(2)}, u32[]{:S(2)}) collective-permute-start(bf16[4,3,640]{2,1,0:T(4,128)(2,1)S(1)} %get-tuple-element.21), channel_id=1, source_target_pairs={{0,8},{4,12},{8,0},{12,4},{1,9},{5,13},{9,1},{13,5},{2,10},{6,14},... | collective-permute-start | bytes 46088 | tf_op jit(solution)/shard_map/ppermute | solution.py:90
  13.0 11.6 %collective-permute-start.3 = (bf16[4,3,640]{2,1,0:T(4,128)(2,1)S(1)}, bf16[4,3,640]{2,1,0:T(4,128)(2,1)S(1)}, u32[]{:S(2)}, u32[]{:S(2)}) collective-permute-start(bf16[4,3,640]{2,1,0:T(4,128)(2,1)S(1)} %get-tuple-element.22), channel_id=1, source_target_pairs={{0,4},{4,8},{8,12},{12,0},{1,5},{5,9},{9,13},{13,1},{2,6},{6,10},{... | collective-permute-start | bytes 46088 | tf_op jit(solution)/shard_map/ppermute | solution.py:90
  14.0 7.8 %copy-start.32 = (s32[16]{0:T(128)S(1)}, s32[16]{0:T(128)}, u32[]{:S(2)}) copy-start(s32[16]{0:T(128)} %param.29) | copy-start | bytes 196
  14.0 7.8 %copy-start.14 = (f32[1,4,640]{2,1,0:T(4,128)S(1)}, f32[1,4,640]{2,1,0:T(4,128)}, u32[]{:S(2)}) copy-start(f32[1,4,640]{2,1,0:T(4,128)} %param.18) | copy-start | bytes 30724
  14.1 8.5 %copy-start.17 = (f32[1,2048]{1,0:T(1,128)S(1)}, f32[1,2048]{1,0:T(1,128)}, u32[]{:S(2)}) copy-start(f32[1,2048]{1,0:T(1,128)} %param.16) | copy-start | bytes 24580
  14.1 9.1 %copy-start.31 = (f32[1,16]{1,0:T(1,128)S(1)}, f32[1,16]{1,0:T(1,128)}, u32[]{:S(2)}) copy-start(f32[1,16]{1,0:T(1,128)} %param.22) | copy-start | bytes 196
  14.1 9.9 %copy-start.20 = (f32[1,640]{1,0:T(1,128)S(1)}, f32[1,640]{1,0:T(1,128)}, u32[]{:S(2)}) copy-start(f32[1,640]{1,0:T(1,128)} %param.19) | copy-start | bytes 7684
  14.1 9.9 %copy-start.4 = (bf16[256,512]{1,0:T(8,128)(2,1)S(1)}, bf16[256,512]{1,0:T(8,128)(2,1)}, u32[]{:S(2)}) copy-start(bf16[256,512]{1,0:T(8,128)(2,1)} %param.15) | copy-start | bytes 786436
  17.0 30.9 %all-to-all-start = ((bf16[16,16,2048]{2,1,0:T(8,128)(2,1)}), bf16[16,16,2048]{2,1,0:T(8,128)(2,1)}, u32[]{:S(2)}, u32[]{:S(2)}) async-start(bf16[16,16,2048]{2,1,0:T(8,128)(2,1)} %gather_fusion.2), calls=%async_computation | async-start | bytes 2097152 | tf_op jit(solution)/shard_map/all_to_all | solution.py:191
  21.8 15.9 %copy-start.28 = (bf16[16]{0:T(256)(128)(2,1)}, bf16[16]{0:T(256)(128)(2,1)S(1)}, u32[]{:S(2)}) copy-start(bf16[16]{0:T(256)(128)(2,1)S(1)} %compare_convert_fusion) | copy-start | bytes 100
  21.9 16.0 %copy-start.10 = (f32[640]{0:T(1024)}, f32[640]{0:T(1024)S(1)}, u32[]{:S(2)}) copy-start(f32[640]{0:T(1024)S(1)} %get-tuple-element.14) | copy-start | bytes 7684
  21.9 16.0 %copy-start.12 = (f32[640]{0:T(1024)}, f32[640]{0:T(1024)S(1)}, u32[]{:S(2)}) copy-start(f32[640]{0:T(1024)S(1)} %get-tuple-element.15) | copy-start | bytes 7684
  22.6 15.2 %copy-start.18 = (f32[2048]{0:T(1024)}, f32[2048]{0:T(1024)S(1)}, u32[]{:S(2)}) copy-start(f32[2048]{0:T(1024)S(1)} %fusion.134) | copy-start | bytes 24580
  24.0 7.7 %collective-permute-start.2 = (bf16[256,512]{1,0:T(8,128)(2,1)S(1)}, bf16[256,512]{1,0:T(8,128)(2,1)}, u32[]{:S(2)}, u32[]{:S(2)}) collective-permute-start(bf16[256,512]{1,0:T(8,128)(2,1)S(1)} %copy-done.4), channel_id=1, source_target_pairs={{0,1},{1,2},{2,3},{3,0},{4,5},{5,6},{6,7},{7,4},{8,9},{9,10},{10,1... | collective-permute-start | bytes 786440 | tf_op jit(solution)/shard_map/ppermute | solution.py:90
  33.0 4.9 %copy-start.6 = (f32[16,3,640]{2,1,0:T(4,128)S(1)}, f32[16,3,640]{2,1,0:T(4,128)}, u32[]{:S(2)}) copy-start(f32[16,3,640]{2,1,0:T(4,128)} %reshape.356) | copy-start | bytes 368644
  37.8 2.4 %copy-start.9 = (f32[256,1168]{1,0:T(8,128)}, f32[256,1168]{1,0:T(8,128)S(1)}, u32[]{:S(2)}) copy-start(f32[256,1168]{1,0:T(8,128)S(1)} %fusion.47) | copy-start | bytes 3588100
  37.8 2.3 %copy-start.21 = (f32[1,16]{1,0:T(1,128)S(1)}, f32[1,16]{1,0:T(1,128)}, u32[]{:S(2)}) copy-start(f32[1,16]{1,0:T(1,128)} %param.21) | copy-start | bytes 196
  37.8 2.3 %copy-start.23 = (f32[1,16]{1,0:T(1,128)S(1)}, f32[1,16]{1,0:T(1,128)}, u32[]{:S(2)}) copy-start(f32[1,16]{1,0:T(1,128)} %param.20) | copy-start | bytes 196
  38.4 0.8 copy-start.3
  47.9 1.8 %copy-start.29 = (bf16[16]{0:T(256)(128)(2,1)S(1)}, bf16[16]{0:T(256)(128)(2,1)}, u32[]{:S(2)}) copy-start(bf16[16]{0:T(256)(128)(2,1)} %copy-done.28) | copy-start | bytes 100
  47.9 1.8 %copy-start.30 = (s32[16]{0:T(128)S(1)}, s32[16]{0:T(128)}, u32[]{:S(2)}) copy-start(s32[16]{0:T(128)} %get-tuple-element.24) | copy-start | bytes 196
  51.2 4.0 %copy-start.25 = (f32[512]{0:T(512)S(1)}, f32[512]{0:T(512)}, u32[]{:S(2)}) copy-start(f32[512]{0:T(512)} %mul.349) | copy-start | bytes 6148
  55.2 3.0 %copy-start.15 = (f32[1,512]{1,0:T(1,128)S(1)}, f32[1,512]{1,0:T(1,128)}, u32[]{:S(2)}) copy-start(f32[1,512]{1,0:T(1,128)} %param.23) | copy-start | bytes 6148
  59.3 9.4 %collective-permute-start.8 = (bf16[256,512]{1,0:T(8,128)(2,1)}, bf16[256,512]{1,0:T(8,128)(2,1)}, u32[]{:S(2)}, u32[]{:S(2)}) collective-permute-start(bf16[256,512]{1,0:T(8,128)(2,1)} %convolution_convert_fusion.6), channel_id=1, source_target_pairs={{0,3},{1,0},{2,1},{3,2},{4,7},{5,4},{6,5},{7,6},{8,11},{9,8},{10,9... | collective-permute-start | bytes 786440 | tf_op jit(solution)/shard_map/ppermute | solution.py:90
  60.7 11.9 %collective-permute-start.7 = (bf16[256,512]{1,0:T(8,128)(2,1)}, bf16[256,512]{1,0:T(8,128)(2,1)}, u32[]{:S(2)}, u32[]{:S(2)}) collective-permute-start(bf16[256,512]{1,0:T(8,128)(2,1)} %convolution_convert_fusion.7), channel_id=1, source_target_pairs={{0,2},{1,3},{2,0},{3,1},{4,6},{5,7},{6,4},{7,5},{8,10},{9,11},{10,... | collective-permute-start | bytes 786440 | tf_op jit(solution)/shard_map/ppermute | solution.py:90
  62.9 9.7 %collective-permute-start.6 = (bf16[256,512]{1,0:T(8,128)(2,1)}, bf16[256,512]{1,0:T(8,128)(2,1)}, u32[]{:S(2)}, u32[]{:S(2)}) collective-permute-start(bf16[256,512]{1,0:T(8,128)(2,1)} %convolution_convert_fusion.8), channel_id=1, source_target_pairs={{0,1},{1,2},{2,3},{3,0},{4,5},{5,6},{6,7},{7,4},{8,9},{9,10},{10,1... | collective-permute-start | bytes 786440 | tf_op jit(solution)/shard_map/ppermute | solution.py:90
  74.9 10.0 %collective-permute-start.9 = (bf16[256,512]{1,0:T(8,128)(2,1)}, bf16[256,512]{1,0:T(8,128)(2,1)S(1)}, u32[]{:S(2)}, u32[]{:S(2)}) collective-permute-start(bf16[256,512]{1,0:T(8,128)(2,1)} %add_convert_fusion.2), channel_id=1, source_target_pairs={{0,16},{1,17},{2,18},{3,19},{4,20},{5,21},{6,22},{7,23},{8,24},{9,... | collective-permute-start | bytes 786440 | tf_op jit(solution)/shard_map/ppermute | solution.py:118
  76.2 8.7 %collective-permute-start.12 = (bf16[256,512]{1,0:T(8,128)(2,1)}, bf16[256,512]{1,0:T(8,128)(2,1)}, u32[]{:S(2)}, u32[]{:S(2)}) collective-permute-start(bf16[256,512]{1,0:T(8,128)(2,1)} %add_convert_fusion.2), channel_id=1, source_target_pairs={{0,17},{1,18},{2,19},{3,16},{4,21},{5,22},{6,23},{7,20},{8,25},{9,... | collective-permute-start | bytes 786440 | tf_op jit(solution)/shard_map/ppermute | solution.py:118
  78.2 6.7 %collective-permute-start.11 = (bf16[256,512]{1,0:T(8,128)(2,1)}, bf16[256,512]{1,0:T(8,128)(2,1)}, u32[]{:S(2)}, u32[]{:S(2)}) collective-permute-start(bf16[256,512]{1,0:T(8,128)(2,1)} %add_convert_fusion.2), channel_id=1, source_target_pairs={{0,18},{1,19},{2,16},{3,17},{4,22},{5,23},{6,20},{7,21},{8,26},{9,... | collective-permute-start | bytes 786440 | tf_op jit(solution)/shard_map/ppermute | solution.py:118
  80.2 5.5 %collective-permute-start.10 = (bf16[256,512]{1,0:T(8,128)(2,1)}, bf16[256,512]{1,0:T(8,128)(2,1)}, u32[]{:S(2)}, u32[]{:S(2)}) collective-permute-start(bf16[256,512]{1,0:T(8,128)(2,1)} %add_convert_fusion.2), channel_id=1, source_target_pairs={{0,19},{1,16},{2,17},{3,18},{4,23},{5,20},{6,21},{7,22},{8,27},{9,... | collective-permute-start | bytes 786440 | tf_op jit(solution)/shard_map/ppermute | solution.py:118
  82.2 5.0 %copy-start.19 = (f32[2048]{0:T(1024)S(1)}, f32[2048]{0:T(1024)}, u32[]{:S(2)}) copy-start(f32[2048]{0:T(1024)} %copy-done.18) | copy-start | bytes 24580
  87.2 5.3 %copy-start.22 = (f32[1,16]{1,0:T(1,128)S(1)}, f32[1,16]{1,0:T(1,128)}, u32[]{:S(2)}) copy-start(f32[1,16]{1,0:T(1,128)} %param.21) | copy-start | bytes 196
  87.2 5.3 %copy-start.24 = (f32[1,16]{1,0:T(1,128)S(1)}, f32[1,16]{1,0:T(1,128)}, u32[]{:S(2)}) copy-start(f32[1,16]{1,0:T(1,128)} %param.20) | copy-start | bytes 196
  87.2 5.4 %copy-start.7 = (f32[16,3,640]{2,1,0:T(4,128)S(1)}, f32[16,3,640]{2,1,0:T(4,128)}, u32[]{:S(2)}) copy-start(f32[16,3,640]{2,1,0:T(4,128)} %reshape.356) | copy-start | bytes 368644
  87.2 5.4 %copy-start.11 = (f32[640]{0:T(1024)S(1)}, f32[640]{0:T(1024)}, u32[]{:S(2)}) copy-start(f32[640]{0:T(1024)} %copy-done.10) | copy-start | bytes 7684
  87.2 5.4 %copy-start.13 = (f32[640]{0:T(1024)S(1)}, f32[640]{0:T(1024)}, u32[]{:S(2)}) copy-start(f32[640]{0:T(1024)} %copy-done.12) | copy-start | bytes 7684
  92.4 1.6 %copy-start.8 = (f32[256,1168]{1,0:T(8,128)}, f32[256,1168]{1,0:T(8,128)S(1)}, u32[]{:S(2)}) copy-start(f32[256,1168]{1,0:T(8,128)S(1)} %fusion.45) | copy-start | bytes 3588100
  93.1 3.0 %copy-start.27 = (pred[16,16]{1,0:T(8,128)(4,1)S(1)}, pred[16,16]{1,0:T(8,128)(4,1)}, u32[]{:S(2)}) copy-start(pred[16,16]{1,0:T(8,128)(4,1)} %iota_compare_fusion.6) | copy-start | bytes 772
  96.1 3.1 %copy-start.1 = (bf16[16,512,64]{2,1,0:T(8,128)(2,1)S(1)}, bf16[16,512,64]{2,1,0:T(8,128)(2,1)}, u32[]{:S(2)}) copy-start(bf16[16,512,64]{2,1,0:T(8,128)(2,1)} %reshape_reshape.4) | copy-start | bytes 3145732
  96.1 3.1 %copy-start.26 = (f32[512]{0:T(512)S(1)}, f32[512]{0:T(512)}, u32[]{:S(2)}) copy-start(f32[512]{0:T(512)} %mul.349) | copy-start | bytes 6148
  99.2 1.9 %copy-start.16 = (f32[1,512]{1,0:T(1,128)S(1)}, f32[1,512]{1,0:T(1,128)}, u32[]{:S(2)}) copy-start(f32[1,512]{1,0:T(1,128)} %param.23) | copy-start | bytes 6148
  101.2 6.7 %copy-start.2 = (bf16[16,512,64]{1,2,0:T(8,128)(2,1)S(1)}, bf16[16,512,64]{1,2,0:T(8,128)(2,1)}, u32[]{:S(2)}) copy-start(bf16[16,512,64]{1,2,0:T(8,128)(2,1)} %copy.71) | copy-start | bytes 3145732
  104.4 14.3 %collective-permute-start.15 = (bf16[256,512]{1,0:T(8,128)(2,1)}, bf16[256,512]{1,0:T(8,128)(2,1)}, u32[]{:S(2)}, u32[]{:S(2)}) collective-permute-start(bf16[256,512]{1,0:T(8,128)(2,1)} %convolution_convert_fusion.2), channel_id=1, source_target_pairs={{0,3},{1,0},{2,1},{3,2},{4,7},{5,4},{6,5},{7,6},{8,11},{9,8},{10,9... | collective-permute-start | bytes 786440 | tf_op jit(solution)/shard_map/ppermute | solution.py:90
  104.5 14.2 %collective-permute-start.14 = (bf16[256,512]{1,0:T(8,128)(2,1)}, bf16[256,512]{1,0:T(8,128)(2,1)}, u32[]{:S(2)}, u32[]{:S(2)}) collective-permute-start(bf16[256,512]{1,0:T(8,128)(2,1)} %convolution_convert_fusion.3), channel_id=1, source_target_pairs={{0,2},{1,3},{2,0},{3,1},{4,6},{5,7},{6,4},{7,5},{8,10},{9,11},{10,... | collective-permute-start | bytes 786440 | tf_op jit(solution)/shard_map/ppermute | solution.py:90
  105.7 14.3 %collective-permute-start.13 = (bf16[256,512]{1,0:T(8,128)(2,1)}, bf16[256,512]{1,0:T(8,128)(2,1)}, u32[]{:S(2)}, u32[]{:S(2)}) collective-permute-start(bf16[256,512]{1,0:T(8,128)(2,1)} %convolution_convert_fusion.4), channel_id=1, source_target_pairs={{0,1},{1,2},{2,3},{3,0},{4,5},{5,6},{6,7},{7,4},{8,9},{9,10},{10,1... | collective-permute-start | bytes 786440 | tf_op jit(solution)/shard_map/ppermute | solution.py:90
  112.7 7.3 %copy-start.5 = (bf16[256,512]{1,0:T(8,128)(2,1)S(1)}, bf16[256,512]{1,0:T(8,128)(2,1)}, u32[]{:S(2)}) copy-start(bf16[256,512]{1,0:T(8,128)(2,1)} %param.15) | copy-start | bytes 786436
